TPU v7x, 512 devices: a whole 4x8x8 slice. The times are simulated.
512 devices in a mesh: ctx: 256 (over z, y, x_lo, core), kvh: 2 (over x_hi).
Axes of the slice: x: 4 (x_hi: 2, x_lo: 2; x = x_hi * 2 + x_lo), y: 8, z: 8, core: 2. Of those that a mesh axis runs over, the one named last changes fastest.
Arguments:
- queries: bfloat16 [65536, 64, 128], P('ctx', 'kvh'), may hold values from -110 to 110
- key_value: bfloat16 [2, 65536, 8, 128], P(None, 'ctx', 'kvh'), may hold values from -5 to 5
- span_table: int32 [512], replicated, may hold values from 0 to 511, as said below
Outputs:
- attended: bfloat16 [65536, 8192], P(('ctx', 'kvh'))
Inputs may be any that keep to these rules, and one draw needn't show every extreme that they name: `span_table`: entries 2 d and 2 d + 1 are the spans of ctx index d: the first below 256, the second 256 or above; every span of 0 to 511 appears exactly once.
All inputs are finite; a program needn't handle non-finite values.
Results may differ from a plain program's by a relative error of at most 0.0065.
Values may be sent and summed in bfloat16 or wider, within the bound.
No kernel may reach another device: no remote copies, remote signals or barrier semaphores. Data moves between devices by JAX's collectives and lax.ppermute only.
A program may use at most 64 MiB of HBM per device.

v0:
```python
import jax
import jax.numpy as jnp
from jax import lax
from jax.sharding import PartitionSpec as P

STEPS = 4


def passed_along(value, axis, steps):
    count = lax.axis_size(axis)
    pairs = [(source, (source + steps) % count) for source in range(count)]
    return lax.ppermute(value, axis, pairs)


def body(queries, key_value, span_table):
    rows = queries.shape[0]
    heads_here = queries.shape[1]
    head_size = queries.shape[2]
    kv_here = key_value.shape[2]
    group = heads_here // kv_here
    span = rows // 2
    scale = 1.0 / head_size**0.5
    cycle = lax.axis_size("ctx")
    myself = lax.axis_index("ctx")
    table = span_table.reshape(cycle, 2)
    offsets = jnp.arange(span, dtype=jnp.int32)

    def positions_of(device):
        pair = lax.dynamic_index_in_dim(table, device, 0, keepdims=False)
        return (pair[:, None] * span + offsets[None, :]).reshape(rows)

    query_pos = positions_of(myself)
    grouped = queries.reshape(rows, kv_here, group, head_size)

    def attend(carry, block, source):
        run_max, numer, denom = carry
        key_pos = positions_of(source)
        scores = (
            jnp.einsum("qghd,kgd->ghqk", grouped, block[0], preferred_element_type=jnp.float32)
            * scale
        )
        visible = (key_pos[None, :] <= query_pos[:, None])[None, None]
        masked = jnp.where(visible, scores, -jnp.inf)
        block_max = jnp.maximum(jnp.max(masked, axis=-1), jnp.float32(-1e30))
        weight = jnp.exp(masked - block_max[..., None])
        block_sum = jnp.sum(weight, axis=-1)
        block_out = jnp.einsum(
            "ghqk,kgd->ghqd",
            weight.astype(jnp.bfloat16),
            block[1],
            preferred_element_type=jnp.float32,
        )
        new_max = jnp.maximum(run_max, block_max)
        old_factor = jnp.exp(run_max - new_max)
        new_factor = jnp.exp(block_max - new_max)
        numer = numer * old_factor[..., None] + block_out * new_factor[..., None]
        denom = denom * old_factor + block_sum * new_factor
        return (new_max, numer, denom)

    start = (
        jnp.full((kv_here, group, rows), -1e30, jnp.float32),
        jnp.zeros((kv_here, group, rows, head_size), jnp.float32),
        jnp.zeros((kv_here, group, rows), jnp.float32),
    )
    carry = attend(start, key_value, myself)
    moving = key_value
    for distance in range(1, STEPS):
        moving = passed_along(moving, "ctx", 1)
        carry = attend(carry, moving, (myself - distance) % cycle)
    run_max, numer, denom = carry
    result = numer / denom[..., None]
    local_out = (
        jnp.transpose(result, (2, 0, 1, 3))
        .reshape(rows, heads_here * head_size)
        .astype(jnp.bfloat16)
    )
    return lax.all_to_all(local_out, "kvh", split_axis=0, concat_axis=1, tiled=True)


def solution(mesh):
    in_specs = (P("ctx", "kvh", None), P(None, "ctx", "kvh", None), P())
    out_specs = P(("ctx", "kvh"), None)
    return jax.shard_map(body, mesh=mesh, in_specs=in_specs, out_specs=out_specs, check_vma=False)
```

profile of v0, /device:TPU:4, one launch (start us, length us, event | category | flops | bytes accessed | tf_op | source)
XLA Modules:
  0.0 106.6 jit_solution(826526950033051445)
XLA Ops:
  0.0 1.3 %copy.27 = bf16[2,256,4,128]{3,1,2,0:T(8,128)(2,1)S(1)} copy(bf16[2,256,4,128]{3,2,1,0:T(4,128)(2,1)} %param.4) | data formatting | bytes 1048576 | tf_op args[1]
  1.3 1.9 %collective-permute-start = (bf16[2,256,4,128]{3,1,2,0:T(8,128)(2,1)S(1)}, bf16[2,256,4,128]{3,1,2,0:T(8,128)(2,1)S(1)}, u32[]{:S(2)}, u32[]{:S(2)}) collective-permute-start(bf16[2,256,4,128]{3,1,2,0:T(8,128)(2,1)S(1)} %copy.27), channel_id=1, source_target_pairs={{0,2},{2,4},{4,6},{6,8},{8,10},{10,12},{12,14},{14,16},{16,18},{18... | collective-permute-start | bytes 1572872 | tf_op jit(solution)/shard_map/ppermute | solution.py:12
  4.5 2.1 %fusion.8 = (f32[4,8,256]{2,1,0:T(8,128)S(1)}, f32[4,256,256,8]{2,1,3,0:T(8,128)S(1)}) fusion(pred[256,256]{0,1:T(8,128)(4,1)S(1)} %get-tuple-element.23, bf16[256,4,8,128]{3,2,1,0:T(8,128)(2,1)S(1)} %bitcast.239, bf16[2,256,4,128]{3,1,2,0:T(8,128)(2,1)S(1)} %copy.27), kind=kOutput, calls=%fused_computation.16 | convolution fusion | flops 543154176 | bytes 10846208 | tf_op jit(solution)/shard_map/qghd,kgd->ghqk/dot_general | solution.py:39
  6.7 2.4 %fusion.18 = f32[4,8,256,128]{3,2,1,0:T(8,128)S(1)} fusion(f32[4,256,256,8]{2,1,3,0:T(8,128)S(1)} %get-tuple-element.30, f32[4,8,256]{2,1,0:T(8,128)S(1)} %broadcast_maximum_fusion.3, pred[256,256]{0,1:T(8,128)(4,1)S(1)} %get-tuple-element.23, bf16[2,256,4,128]{3,1,2,0:T(8,128)(2,1)S(1)} %copy.27), kind=kOutput, calls=%fused_computation.23 | convolution fusion | flops 545259520 | bytes 12943360 | tf_op jit(solution)/shard_map/ghqk,kgd->ghqd/dot_general | solution.py:47
  9.0 1.8 %fusion = f32[4,8,256]{2,1,0:T(8,128)S(1)} fusion(f32[4,256,256,8]{2,1,3,0:T(8,128)S(1)} %get-tuple-element.30, f32[4,8,256]{2,1,0:T(8,128)S(1)} %broadcast_maximum_fusion.3, pred[256,256]{0,1:T(8,128)(4,1)S(1)} %get-tuple-element.23), kind=kLoop, calls=%fused_computation.8 | loop fusion | flops 8380416 | bytes 8519680 | tf_op jit(solution)/shard_map/reduce_sum | solution.py:46
  10.8 11.2 %collective-permute-done = bf16[2,256,4,128]{3,1,2,0:T(8,128)(2,1)S(1)} collective-permute-done((bf16[2,256,4,128]{3,1,2,0:T(8,128)(2,1)S(1)}, bf16[2,256,4,128]{3,1,2,0:T(8,128)(2,1)S(1)}, u32[]{:S(2)}, u32[]{:S(2)}) %collective-permute-start) | collective-permute-done | bytes 524320 | tf_op jit(solution)/shard_map/ppermute | solution.py:12
  22.1 2.1 %fusion.9 = (f32[4,8,256]{2,1,0:T(8,128)S(1)}, f32[4,256,256,8]{2,1,3,0:T(8,128)S(1)}) fusion(pred[256,256]{0,1:T(8,128)(4,1)S(1)} %get-tuple-element.24, bf16[256,4,8,128]{3,2,1,0:T(8,128)(2,1)S(1)} %bitcast.242, bf16[2,256,4,128]{3,1,2,0:T(8,128)(2,1)S(1)} %collective-permute-done), kind=kOutput, calls=%fused_computation.17 | convolution fusion | flops 543154176 | bytes 10846208 | tf_op jit(solution)/shard_map/qghd,kgd->ghqk/dot_general | solution.py:39
  24.2 2.1 %collective-permute-start.1 = (bf16[2,256,4,128]{3,1,2,0:T(8,128)(2,1)S(1)}, bf16[2,256,4,128]{3,1,2,0:T(8,128)(2,1)S(1)}, u32[]{:S(2)}, u32[]{:S(2)}) collective-permute-start(bf16[2,256,4,128]{3,1,2,0:T(8,128)(2,1)S(1)} %collective-permute-done), channel_id=1, source_target_pairs={{0,2},{2,4},{4,6},{6,8},{8,10},{10,12},{12,14},{14,16},{16,18},{18... | collective-permute-start | bytes 1572872 | tf_op jit(solution)/shard_map/ppermute | solution.py:12
  26.3 2.4 %fusion.16 = f32[4,8,256,128]{3,2,1,0:T(8,128)S(1)} fusion(f32[4,256,256,8]{2,1,3,0:T(8,128)S(1)} %get-tuple-element.28, f32[4,8,256]{2,1,0:T(8,128)S(1)} %broadcast_maximum_fusion.2, pred[256,256]{0,1:T(8,128)(4,1)S(1)} %get-tuple-element.24, bf16[2,256,4,128]{3,1,2,0:T(8,128)(2,1)S(1)} %collective-permute-done), kind=kOutput, calls=%fused_computation.22 | convolution fusion | flops 545259520 | bytes 12943360 | tf_op jit(solution)/shard_map/ghqk,kgd->ghqd/dot_general | solution.py:47
  28.7 1.8 %fusion.2 = f32[4,8,256]{2,1,0:T(8,128)S(1)} fusion(f32[4,256,256,8]{2,1,3,0:T(8,128)S(1)} %get-tuple-element.28, f32[4,8,256]{2,1,0:T(8,128)S(1)} %broadcast_maximum_fusion.2, pred[256,256]{0,1:T(8,128)(4,1)S(1)} %get-tuple-element.24), kind=kLoop, calls=%fused_computation.10 | loop fusion | flops 8380416 | bytes 8519680 | tf_op jit(solution)/shard_map/reduce_sum | solution.py:46
  30.5 8.4 %collective-permute-done.1 = bf16[2,256,4,128]{3,1,2,0:T(8,128)(2,1)S(1)} collective-permute-done((bf16[2,256,4,128]{3,1,2,0:T(8,128)(2,1)S(1)}, bf16[2,256,4,128]{3,1,2,0:T(8,128)(2,1)S(1)}, u32[]{:S(2)}, u32[]{:S(2)}) %collective-permute-start.1) | collective-permute-done | bytes 524320 | tf_op jit(solution)/shard_map/ppermute | solution.py:12
  38.9 2.1 %fusion.10 = (f32[4,8,256]{2,1,0:T(8,128)S(1)}, f32[4,256,256,8]{2,1,3,0:T(8,128)S(1)}) fusion(pred[256,256]{0,1:T(8,128)(4,1)S(1)} %get-tuple-element.22, bf16[256,4,8,128]{3,2,1,0:T(8,128)(2,1)S(1)} %bitcast.241, bf16[2,256,4,128]{3,1,2,0:T(8,128)(2,1)S(1)} %collective-permute-done.1), kind=kOutput, calls=%fused_computation.18 | convolution fusion | flops 543154176 | bytes 10846208 | tf_op jit(solution)/shard_map/qghd,kgd->ghqk/dot_general | solution.py:39
  41.1 2.1 %collective-permute-start.2 = (bf16[2,256,4,128]{3,1,2,0:T(8,128)(2,1)S(1)}, bf16[2,256,4,128]{3,1,2,0:T(8,128)(2,1)S(1)}, u32[]{:S(2)}, u32[]{:S(2)}) collective-permute-start(bf16[2,256,4,128]{3,1,2,0:T(8,128)(2,1)S(1)} %collective-permute-done.1), channel_id=1, source_target_pairs={{0,2},{2,4},{4,6},{6,8},{8,10},{10,12},{12,14},{14,16},{16,18},{18... | collective-permute-start | bytes 1572872 | tf_op jit(solution)/shard_map/ppermute | solution.py:12
  43.3 2.4 %fusion.14 = f32[4,8,256,128]{3,2,1,0:T(8,128)S(1)} fusion(f32[4,256,256,8]{2,1,3,0:T(8,128)S(1)} %get-tuple-element.26, f32[4,8,256]{2,1,0:T(8,128)S(1)} %broadcast_maximum_fusion.1, pred[256,256]{0,1:T(8,128)(4,1)S(1)} %get-tuple-element.22, bf16[2,256,4,128]{3,1,2,0:T(8,128)(2,1)S(1)} %collective-permute-done.1), kind=kOutput, calls=%fused_computation.21 | convolution fusion | flops 545259520 | bytes 12943360 | tf_op jit(solution)/shard_map/ghqk,kgd->ghqd/dot_general | solution.py:47
  45.6 1.8 %fusion.4 = f32[4,8,256]{2,1,0:T(8,128)S(1)} fusion(f32[4,256,256,8]{2,1,3,0:T(8,128)S(1)} %get-tuple-element.26, f32[4,8,256]{2,1,0:T(8,128)S(1)} %broadcast_maximum_fusion.1, pred[256,256]{0,1:T(8,128)(4,1)S(1)} %get-tuple-element.22), kind=kLoop, calls=%fused_computation.12 | loop fusion | flops 8380416 | bytes 8519680 | tf_op jit(solution)/shard_map/reduce_sum | solution.py:46
  47.4 8.4 %collective-permute-done.2 = bf16[2,256,4,128]{3,1,2,0:T(8,128)(2,1)S(1)} collective-permute-done((bf16[2,256,4,128]{3,1,2,0:T(8,128)(2,1)S(1)}, bf16[2,256,4,128]{3,1,2,0:T(8,128)(2,1)S(1)}, u32[]{:S(2)}, u32[]{:S(2)}) %collective-permute-start.2) | collective-permute-done | bytes 524320 | tf_op jit(solution)/shard_map/ppermute | solution.py:12
  55.8 2.1 %fusion.11 = (f32[4,8,256]{2,1,0:T(8,128)S(1)}, f32[4,256,256,8]{2,1,3,0:T(8,128)S(1)}) fusion(pred[256,256]{0,1:T(8,128)(4,1)S(1)} %get-tuple-element.21, bf16[256,4,8,128]{3,2,1,0:T(8,128)(2,1)S(1)} %bitcast.240, bf16[2,256,4,128]{3,1,2,0:T(8,128)(2,1)S(1)} %collective-permute-done.2), kind=kOutput, calls=%fused_computation.19 | convolution fusion | flops 543154176 | bytes 10846208 | tf_op jit(solution)/shard_map/qghd,kgd->ghqk/dot_general | solution.py:39
  58.0 1.8 %fusion.6 = f32[4,8,256]{2,1,0:T(8,128)S(1)} fusion(f32[4,256,256,8]{2,1,3,0:T(8,128)S(1)} %get-tuple-element.32, f32[4,8,256]{2,1,0:T(8,128)S(1)} %broadcast_maximum_fusion, pred[256,256]{0,1:T(8,128)(4,1)S(1)} %get-tuple-element.21), kind=kLoop, calls=%fused_computation.14 | loop fusion | flops 8380416 | bytes 8519680 | tf_op jit(solution)/shard_map/reduce_sum | solution.py:46
  59.8 12.3 %fusion.22 = bf16[256,4,8,128]{3,0,2,1:T(8,128)(2,1)S(1)} fusion(f32[4,8,256,128]{3,2,1,0:T(8,128)S(1)} %fusion.14, f32[4,8,256,128]{3,2,1,0:T(8,128)S(1)} %fusion.16, f32[4,8,256,128]{3,2,1,0:T(8,128)S(1)} %fusion.18, f32[256,4,8]{0,2,1:T(8,128)S(1)} %get-tuple-element.7, f32[256,4,8]{0,2,1:T(8,128)S(1)} %get-tuple-element.10, ...), kind=kOutput, calls=%fused_computation.27 | convolution fusion | flops 558891008 | bytes 23724032 | tf_op jit(solution)/shard_map/ghqk,kgd->ghqd/dot_general | solution.py:47
  72.1 2.7 %copy.38 = bf16[256,4,8,128]{3,2,1,0:T(8,128)(2,1)} copy(bf16[256,4,8,128]{3,0,2,1:T(8,128)(2,1)S(1)} %fusion.22) | data formatting | bytes 4194304 | tf_op jit(solution)/shard_map/convert_element_type | solution.py:75
  74.8 4.2 %convert_element_type.24 = bf16[2,128,4096]{2,1,0:T(8,128)(2,1)} reshape(bf16[256,4,8,128]{3,2,1,0:T(8,128)(2,1)} %copy.38) | data formatting | bytes 4194304 | tf_op jit(solution)/shard_map/convert_element_type | solution.py:75
  79.0 19.5 %all_to_all.16 = bf16[2,128,4096]{2,1,0:T(8,128)(2,1)} all-to-all(bf16[2,128,4096]{2,1,0:T(8,128)(2,1)} %convert_element_type.24), channel_id=1, replica_groups=mesh['ctx'=256,'kvh'=2] {'kvh'}, dimensions={0} | all-to-all | bytes 4194304 | tf_op jit(solution)/shard_map/all_to_all | solution.py:77
  98.4 4.1 %copy.39 = bf16[128,2,4096]{0,2,1:T(8,128)(2,1)} copy(bf16[128,2,4096]{2,0,1:T(8,128)(2,1)} %bitcast.243) | data formatting | bytes 4194304 | tf_op jit(solution)/shard_map/all_to_all | solution.py:77
  102.5 4.1 %copy.40 = bf16[128,8192]{1,0:T(8,128)(2,1)} copy(bf16[128,8192]{0,1:T(8,128)(2,1)} %bitcast.244) | data formatting | bytes 4194304 | tf_op jit(solution)/shard_map/all_to_all | solution.py:77
  (13 shorter events, 1.3 us)
Async XLA Ops:
  0.0 4.5 %copy-start = (bf16[256,32,128]{2,1,0:T(8,128)(2,1)S(1)}, bf16[256,32,128]{2,1,0:T(8,128)(2,1)}, u32[]{:S(2)}) copy-start(bf16[256,32,128]{2,1,0:T(8,128)(2,1)} %param.3) | copy-start | bytes 6291460
  1.3 20.8 %collective-permute-start = (bf16[2,256,4,128]{3,1,2,0:T(8,128)(2,1)S(1)}, bf16[2,256,4,128]{3,1,2,0:T(8,128)(2,1)S(1)}, u32[]{:S(2)}, u32[]{:S(2)}) collective-permute-start(bf16[2,256,4,128]{3,1,2,0:T(8,128)(2,1)S(1)} %copy.27), channel_id=1, source_target_pairs={{0,2},{2,4},{4,6},{6,8},{8,10},{10,12},{12,14},{14,16},{16,18},{18... | collective-permute-start | bytes 1572872 | tf_op jit(solution)/shard_map/ppermute | solution.py:12
  24.2 14.7 %collective-permute-start.1 = (bf16[2,256,4,128]{3,1,2,0:T(8,128)(2,1)S(1)}, bf16[2,256,4,128]{3,1,2,0:T(8,128)(2,1)S(1)}, u32[]{:S(2)}, u32[]{:S(2)}) collective-permute-start(bf16[2,256,4,128]{3,1,2,0:T(8,128)(2,1)S(1)} %collective-permute-done), channel_id=1, source_target_pairs={{0,2},{2,4},{4,6},{6,8},{8,10},{10,12},{12,14},{14,16},{16,18},{18... | collective-permute-start | bytes 1572872 | tf_op jit(solution)/shard_map/ppermute | solution.py:12
  41.1 14.7 %collective-permute-start.2 = (bf16[2,256,4,128]{3,1,2,0:T(8,128)(2,1)S(1)}, bf16[2,256,4,128]{3,1,2,0:T(8,128)(2,1)S(1)}, u32[]{:S(2)}, u32[]{:S(2)}) collective-permute-start(bf16[2,256,4,128]{3,1,2,0:T(8,128)(2,1)S(1)} %collective-permute-done.1), channel_id=1, source_target_pairs={{0,2},{2,4},{4,6},{6,8},{8,10},{10,12},{12,14},{14,16},{16,18},{18... | collective-permute-start | bytes 1572872 | tf_op jit(solution)/shard_map/ppermute | solution.py:12
where the time goes:
time: 107 us
  waiting for transfers between devices  28.1 us (26%)
  matrix products  27.9 us (26%)
  blocking collectives  19.5 us (18%)
  local copies, waits for them, and re-layouts  17.1 us (16%)
  other arithmetic  7.65 us (7%)
  starting transfers between devices  6.16 us (6%)
    ppermute x3, waiting for transfers between devices, passed_along(): return lax.ppermute(value, axis, pairs)  28.1 us
    all_to_all x1, blocking collectives, body(): lax.all_to_all(local_out, 'kvh', split_axis=0, concat_axis=1, tiled=True)  19.5 us
    dot_general x4, matrix products, attend(): jnp.einsum('ghqk,kgd->ghqd', weight.astype(jnp.bfloat16), block[1], prefe...  19.3 us
    dot_general x4, matrix products, attend(): jnp.einsum('qghd,kgd->ghqk', grouped, block[0], preferred_element_type=jn...  8.5 us
    all_to_all x2, local copies, waits for them, and re-layouts, body(): lax.all_to_all(local_out, 'kvh', split_axis=0, concat_axis=1, tiled=True)  8.14 us
    reduce_sum x4, other arithmetic, attend(): block_sum = jnp.sum(weight, axis=-1)  7.15 us
    convert_element_type x2, local copies, waits for them, and re-layouts, body(): local_out = jnp.transpose(result, (2, 0, 1, 3)).reshape(rows, heads_here...  6.85 us
    ppermute x3, starting transfers between devices, passed_along(): return lax.ppermute(value, axis, pairs)  6.16 us
  transfers between devices with their start and end apart: 3, of which 3 were waited for; matrix products, arithmetic and copies ran while one was open for 15% of the time, Pallas kernels for 0%

commit v1 on v0

v1 whole, which is shorter than its diff:
```python
import functools

import jax
import jax.numpy as jnp
from jax import lax
from jax.experimental import pallas as pl
from jax.experimental.pallas import tpu as pltpu
from jax.sharding import PartitionSpec as P

STEPS = 4


def shifted(value, axis, steps):
    count = lax.axis_size(axis)
    pairs = [(source, (source + steps) % count) for source in range(count)]
    return lax.ppermute(value, axis, pairs)


def attend_kernel(info_ref, q_ref, *refs, span, group, head_size, steps, scale):
    kv_refs = refs[:steps]
    o_ref = refs[steps]
    m_ref, l_ref, acc_ref = refs[steps + 1 :]
    query_span = info_ref[1]

    m_ref[...] = jnp.full(m_ref.shape, -jnp.inf, jnp.float32)
    l_ref[...] = jnp.zeros(l_ref.shape, jnp.float32)
    acc_ref[...] = jnp.zeros(acc_ref.shape, jnp.float32)

    row = lax.broadcasted_iota(jnp.int32, (span, span), 0)
    col = lax.broadcasted_iota(jnp.int32, (span, span), 1)

    def run(kv_ref, t, masked):
        k = kv_ref[0, t * span : (t + 1) * span, :]
        v = kv_ref[1, t * span : (t + 1) * span, :]

        def head(h, carry):
            off = pl.multiple_of(h * head_size, head_size)
            qv = q_ref[:, pl.ds(off, head_size)]
            s = lax.dot_general(
                qv, k, (((1,), (1,)), ((), ())), preferred_element_type=jnp.float32
            ) * scale
            if masked:
                s = jnp.where(col <= row, s, -jnp.inf)
            m_old = m_ref[h]
            m_new = jnp.maximum(m_old, jnp.max(s, axis=1, keepdims=True))
            p = jnp.exp(s - m_new)
            alpha = jnp.exp(m_old - m_new)
            l_ref[h] = alpha * l_ref[h] + jnp.sum(p, axis=1, keepdims=True)
            acc_ref[h] = alpha * acc_ref[h] + jnp.dot(
                p.astype(jnp.bfloat16), v, preferred_element_type=jnp.float32
            )
            m_ref[h] = m_new
            return carry

        lax.fori_loop(0, group, head, 0)

    for b in range(steps):
        for t in range(2):
            key_span = info_ref[2 + 2 * b + t]

            @pl.when(key_span < query_span)
            def _(b=b, t=t):
                run(kv_refs[b], t, False)

            @pl.when(key_span == query_span)
            def _(b=b, t=t):
                run(kv_refs[b], t, True)

    def finish(h, carry):
        off = pl.multiple_of(h * head_size, head_size)
        o_ref[:, pl.ds(off, head_size)] = (acc_ref[h] / l_ref[h]).astype(o_ref.dtype)
        return carry

    lax.fori_loop(0, group, finish, 0)


def attend_half(info, q2, blocks, *, span, group, kv_here, head_size, out_cols, out_block0):
    steps = len(blocks)
    width = group * head_size
    kernel = functools.partial(
        attend_kernel,
        span=span,
        group=group,
        head_size=head_size,
        steps=steps,
        scale=1.0 / head_size**0.5,
    )
    q_spec = pl.BlockSpec((span, width), lambda g, info: (info[0], g))
    kv_spec = pl.BlockSpec((2, 2 * span, head_size), lambda g, info: (0, 0, g))
    o_spec = pl.BlockSpec((span, width), lambda g, info: (0, out_block0(info) + g))
    flops = 4 * span * 2 * span * steps * head_size * group * kv_here
    return pl.pallas_call(
        kernel,
        out_shape=jax.ShapeDtypeStruct((span, out_cols), jnp.bfloat16),
        grid_spec=pltpu.PrefetchScalarGridSpec(
            num_scalar_prefetch=1,
            grid=(kv_here,),
            in_specs=[q_spec] + [kv_spec] * steps,
            out_specs=o_spec,
            scratch_shapes=[
                pltpu.VMEM((group, span, 1), jnp.float32),
                pltpu.VMEM((group, span, 1), jnp.float32),
                pltpu.VMEM((group, span, head_size), jnp.float32),
            ],
        ),
        compiler_params=pltpu.CompilerParams(dimension_semantics=("arbitrary",)),
        cost_estimate=pl.CostEstimate(
            flops=flops,
            transcendentals=flops // (4 * head_size),
            bytes_accessed=2 * span * width * kv_here * 2 + steps * 2 * 2 * span * kv_here * head_size * 2,
        ),
    )(info, q2, *blocks)


def body(queries, key_value, span_table):
    rows = queries.shape[0]
    heads_here = queries.shape[1]
    head_size = queries.shape[2]
    kv_here = key_value.shape[2]
    group = heads_here // kv_here
    span = rows // 2
    cycle = lax.axis_size("ctx")
    myself = lax.axis_index("ctx")
    half = lax.axis_index("kvh")
    table = span_table.reshape(cycle, 2)

    q2 = queries.reshape(rows, heads_here * head_size)
    own = key_value.reshape(2, rows, kv_here * head_size)
    blocks = [own] + [shifted(own, "ctx", d) for d in range(1, STEPS)]

    sources = (myself - jnp.arange(STEPS, dtype=jnp.int32)) % cycle
    key_spans = table[sources].reshape(2 * STEPS)

    def info_for(qh):
        return jnp.concatenate(
            [jnp.stack([qh, table[myself, qh]]).astype(jnp.int32), key_spans]
        )

    width = heads_here * head_size
    sent_info = info_for(1 - half)
    kept_info = info_for(half)
    common = dict(span=span, group=group, kv_here=kv_here, head_size=head_size)
    sent = attend_half(sent_info, q2, blocks, out_cols=width, out_block0=lambda i: 0, **common)
    arrived = shifted(sent, "kvh", 1)
    out = attend_half(
        kept_info,
        q2,
        blocks,
        out_cols=2 * width,
        out_block0=lambda i: i[0] * kv_here,
        **common,
    )
    return lax.dynamic_update_slice(out, arrived, (0, (1 - half) * width))


def solution(mesh):
    in_specs = (P("ctx", "kvh", None), P(None, "ctx", "kvh", None), P())
    out_specs = P(("ctx", "kvh"), None)
    return jax.shard_map(body, mesh=mesh, in_specs=in_specs, out_specs=out_specs, check_vma=False)
```

time: 107 us -> 282 us (2.64)
  the two profiles are of different devices: /device:TPU:4 before, /device:TPU:388 now
where the time goes in v1:
time: 282 us
  Pallas kernels  184 us (65%)
  starting transfers between devices  67.4 us (24%)
  waiting for transfers between devices  19.3 us (7%)
  local copies, waits for them, and re-layouts  9.1 us (3%)
    pallas_call x2, Pallas kernels, attend_half(): pl.pallas_call(kernel, out_shape=jax.ShapeDtypeStruct((span, out_cols), j...  184 us
    ppermute x4, starting transfers between devices, shifted(): return lax.ppermute(value, axis, pairs)  67.4 us
    ppermute x4, waiting for transfers between devices, shifted(): return lax.ppermute(value, axis, pairs)  19.3 us
  transfers between devices with their start and end apart: 4, of which 2 were waited for; matrix products, arithmetic and copies ran while one was open for 3% of the time, Pallas kernels for 43%

profile of v1, /device:TPU:388, one launch (start us, length us, event | category | flops | bytes accessed | tf_op | source)
XLA Modules:
  0.0 281.7 jit_solution(14182645726039869643)
XLA Ops:
  0.0 1.2 reshape.64.refs_0_
  1.2 0.0 copy-start
  1.3 2.5 collective-permute-start.2
  3.8 3.8 %collective-permute-start.1 = (bf16[2,256,512]{2,1,0:T(8,128)(2,1)S(1)}, bf16[2,256,512]{2,1,0:T(8,128)(2,1)S(1)}, u32[]{:S(2)}, u32[]{:S(2)}) collective-permute-start(bf16[2,256,512]{2,1,0:T(8,128)(2,1)S(1)} %reshape.64.refs_0_), channel_id=1, source_target_pairs={{0,4},{2,6},{4,8},{6,10},{8,12},{10,14},{12,16},{14,18},{16,20},{1... | collective-permute-start | bytes 1572872 | tf_op jit(solution)/shard_map/ppermute | solution.py:16
  7.6 2.1 collective-permute-start
  9.6 0.8 reshape.61
  10.5 0.6 gather_fusion
  11.1 0.1 reshape.62
  11.1 3.9 %copy.6 = bf16[32,8,32,128]{3,1,2,0:T(8,128)(2,1)} copy(bf16[32,8,32,128]{3,2,1,0:T(8,128)(2,1)} %bitcast.10) | data formatting | bytes 4194304
  15.1 0.0 copy-done
  15.1 0.7 fusion.2
  15.7 1.9 add_add_fusion.1
  17.7 0.0 collective-permute-done.2.refs_3_
  17.7 0.0 copy-start.1
  17.7 14.0 %collective-permute-done.1.refs_2_ = bf16[2,256,512]{2,1,0:T(8,128)(2,1)S(1)} collective-permute-done((bf16[2,256,512]{2,1,0:T(8,128)(2,1)S(1)}, bf16[2,256,512]{2,1,0:T(8,128)(2,1)S(1)}, u32[]{:S(2)}, u32[]{:S(2)}) %collective-permute-start.1) | collective-permute-done | bytes 524320 | tf_op jit(solution)/shard_map/ppermute | solution.py:16
  31.6 5.3 %collective-permute-done.refs_1_ = bf16[2,256,512]{2,1,0:T(8,128)(2,1)S(1)} collective-permute-done((bf16[2,256,512]{2,1,0:T(8,128)(2,1)S(1)}, bf16[2,256,512]{2,1,0:T(8,128)(2,1)S(1)}, u32[]{:S(2)}, u32[]{:S(2)}) %collective-permute-start) | collective-permute-done | bytes 524320 | tf_op jit(solution)/shard_map/ppermute | solution.py:16
  37.0 0.0 copy-done.1
  37.0 0.0 copy-done.2
  37.0 0.8 copy-done.3
  37.8 63.8 %shard_map.38 = bf16[128,4096]{1,0:T(8,128)(2,1)} custom-call(s32[10]{0:T(128)} %get-tuple-element.7.info_ref, bf16[256,4096]{1,0:T(8,128)(2,1)} %bitcast.11, bf16[2,256,512]{2,1,0:T(8,128)(2,1)} %copy-done, bf16[2,256,512]{2,1,0:T(8,128)(2,1)} %copy-done.3, bf16[2,256,512]{2,1,0:T(8,128)(2,1)} %copy-done.2, bf16[2,256,512]{2,1,0:T(8,128)(2,1)} %copy-done.1), custom_call_target="tpu_custom_call" | custom-call | flops 2147483648 | bytes 4194304 | tf_op jit(solution)/shard_map/pallas_call | solution.py:92
  101.5 59.1 %collective-permute-start.3 = (bf16[128,4096]{1,0:T(8,128)(2,1)}, bf16[128,4096]{1,0:T(8,128)(2,1)S(1)}, u32[]{:S(2)}, u32[]{:S(2)}) collective-permute-start(bf16[128,4096]{1,0:T(8,128)(2,1)} %shard_map.38), channel_id=1, source_target_pairs={{0,1},{1,0},{2,3},{3,2},{4,5},{5,4},{6,7},{7,6},{8,9},{9,8},{10,11... | collective-permute-start | bytes 3145736 | tf_op jit(solution)/shard_map/ppermute | solution.py:16
  160.6 120.1 %shard_map.37 = bf16[128,8192]{1,0:T(8,128)(2,1)} custom-call(s32[10]{0:T(128)} %get-tuple-element.8.info_ref, bf16[256,4096]{1,0:T(8,128)(2,1)} %bitcast.12, bf16[2,256,512]{2,1,0:T(8,128)(2,1)} %copy-done, bf16[2,256,512]{2,1,0:T(8,128)(2,1)} %copy-done.3, bf16[2,256,512]{2,1,0:T(8,128)(2,1)} %copy-done.2, bf16[2,256,512]{2,1,0:T(8,128)(2,1)} %copy-done.1), custom_call_target="tpu_custom_call" | custom-call | flops 2147483648 | bytes 4194304 | tf_op jit(solution)/shard_map/pallas_call | solution.py:92
  280.7 0.0 collective-permute-done.3
  280.7 1.0 constant_dynamic-update-slice_fusion
  (4 shorter events, 0.0 us)
Async XLA Ops:
  1.2 13.8 %copy-start = (bf16[2,256,512]{2,1,0:T(8,128)(2,1)}, bf16[2,256,512]{2,1,0:T(8,128)(2,1)S(1)}, u32[]{:S(2)}) copy-start(bf16[2,256,512]{2,1,0:T(8,128)(2,1)S(1)} %reshape.64.refs_0_) | copy-start | bytes 1572868
  1.3 16.4 %collective-permute-start.2 = (bf16[2,256,512]{2,1,0:T(8,128)(2,1)S(1)}, bf16[2,256,512]{2,1,0:T(8,128)(2,1)S(1)}, u32[]{:S(2)}, u32[]{:S(2)}) collective-permute-start(bf16[2,256,512]{2,1,0:T(8,128)(2,1)S(1)} %reshape.64.refs_0_), channel_id=1, source_target_pairs={{0,6},{2,8},{4,10},{6,12},{8,14},{10,16},{12,18},{14,20},{16,22},{... | collective-permute-start | bytes 1572872 | tf_op jit(solution)/shard_map/ppermute | solution.py:16
  3.8 27.8 %collective-permute-start.1 = (bf16[2,256,512]{2,1,0:T(8,128)(2,1)S(1)}, bf16[2,256,512]{2,1,0:T(8,128)(2,1)S(1)}, u32[]{:S(2)}, u32[]{:S(2)}) collective-permute-start(bf16[2,256,512]{2,1,0:T(8,128)(2,1)S(1)} %reshape.64.refs_0_), channel_id=1, source_target_pairs={{0,4},{2,6},{4,8},{6,10},{8,12},{10,14},{12,16},{14,18},{16,20},{1... | collective-permute-start | bytes 1572872 | tf_op jit(solution)/shard_map/ppermute | solution.py:16
  7.6 29.4 %collective-permute-start = (bf16[2,256,512]{2,1,0:T(8,128)(2,1)S(1)}, bf16[2,256,512]{2,1,0:T(8,128)(2,1)S(1)}, u32[]{:S(2)}, u32[]{:S(2)}) collective-permute-start(bf16[2,256,512]{2,1,0:T(8,128)(2,1)S(1)} %reshape.64.refs_0_), channel_id=1, source_target_pairs={{0,2},{2,4},{4,6},{6,8},{8,10},{10,12},{12,14},{14,16},{16,18},{18... | collective-permute-start | bytes 1572872 | tf_op jit(solution)/shard_map/ppermute | solution.py:16
  17.7 19.3 %copy-start.1 = (bf16[2,256,512]{2,1,0:T(8,128)(2,1)}, bf16[2,256,512]{2,1,0:T(8,128)(2,1)S(1)}, u32[]{:S(2)}) copy-start(bf16[2,256,512]{2,1,0:T(8,128)(2,1)S(1)} %collective-permute-done.2.refs_3_) | copy-start | bytes 1572868
  31.6 5.4 %copy-start.2 = (bf16[2,256,512]{2,1,0:T(8,128)(2,1)}, bf16[2,256,512]{2,1,0:T(8,128)(2,1)S(1)}, u32[]{:S(2)}) copy-start(bf16[2,256,512]{2,1,0:T(8,128)(2,1)S(1)} %collective-permute-done.1.refs_2_) | copy-start | bytes 1572868
  37.0 0.8 copy-start.3
  101.5 179.2 %collective-permute-start.3 = (bf16[128,4096]{1,0:T(8,128)(2,1)}, bf16[128,4096]{1,0:T(8,128)(2,1)S(1)}, u32[]{:S(2)}, u32[]{:S(2)}) collective-permute-start(bf16[128,4096]{1,0:T(8,128)(2,1)} %shard_map.38), channel_id=1, source_target_pairs={{0,1},{1,0},{2,3},{3,2},{4,5},{5,4},{6,7},{7,6},{8,9},{9,8},{10,11... | collective-permute-start | bytes 3145736 | tf_op jit(solution)/shard_map/ppermute | solution.py:16

commit v2 on v1

v2 whole, which is shorter than its diff:
```python
import functools

import jax
import jax.numpy as jnp
from jax import lax
from jax.experimental import pallas as pl
from jax.experimental.pallas import tpu as pltpu
from jax.sharding import PartitionSpec as P

STEPS = 4


def shifted(value, axis, steps):
    count = lax.axis_size(axis)
    pairs = [(source, (source + steps) % count) for source in range(count)]
    return lax.ppermute(value, axis, pairs)


def attend_kernel(info_ref, q_ref, *refs, span, group, head_size, steps, scale):
    kv_refs = refs[:steps]
    o_ref = refs[steps]
    s_ref, mx_ref, sm_ref, acc_ref = refs[steps + 1 :]
    query_span = info_ref[1]
    n = group * span

    mx_ref[...] = jnp.full(mx_ref.shape, -jnp.inf, jnp.float32)
    tiles = [(b, t) for b in range(steps) for t in range(2)]

    def score(idx, b, t, masked):
        k = kv_refs[b][0, t * span : (t + 1) * span, :]
        q = q_ref[...].reshape(n, head_size)
        s = lax.dot_general(
            q, k, (((1,), (1,)), ((), ())), preferred_element_type=jnp.float32
        ) * scale
        if masked:
            row = lax.broadcasted_iota(jnp.int32, (n, span), 0) % span
            col = lax.broadcasted_iota(jnp.int32, (n, span), 1)
            s = jnp.where(col <= row, s, -jnp.inf)
        s_ref[idx] = s
        mx_ref[...] = jnp.maximum(mx_ref[...], s)

    for idx, (b, t) in enumerate(tiles):
        key_span = info_ref[2 + idx]
        pl.when(key_span < query_span)(functools.partial(score, idx, b, t, False))
        if b == 0:
            pl.when(key_span == query_span)(functools.partial(score, idx, b, t, True))

    m = jnp.max(mx_ref[...], axis=1, keepdims=True)
    mx_ref[...] = jnp.broadcast_to(m, (n, span))
    sm_ref[...] = jnp.zeros(sm_ref.shape, jnp.float32)
    acc_ref[...] = jnp.zeros(acc_ref.shape, jnp.float32)

    def weigh(idx, b, t):
        p = jnp.exp(s_ref[idx] - mx_ref[...])
        sm_ref[...] += p
        v = kv_refs[b][1, t * span : (t + 1) * span, :]
        acc_ref[...] += jnp.dot(p.astype(jnp.bfloat16), v, preferred_element_type=jnp.float32)

    for idx, (b, t) in enumerate(tiles):
        key_span = info_ref[2 + idx]
        pl.when(key_span <= query_span)(functools.partial(weigh, idx, b, t))

    total = jnp.sum(sm_ref[...], axis=1, keepdims=True)
    result = acc_ref[...] / total
    for h in range(group):
        o_ref[:, h * head_size : (h + 1) * head_size] = result[
            h * span : (h + 1) * span, :
        ].astype(o_ref.dtype)


def attend_half(info, q2, blocks, *, span, group, kv_here, head_size, out_cols, out_block0):
    steps = len(blocks)
    width = group * head_size
    kernel = functools.partial(
        attend_kernel,
        span=span,
        group=group,
        head_size=head_size,
        steps=steps,
        scale=1.0 / head_size**0.5,
    )
    q_spec = pl.BlockSpec((group, span, head_size), lambda g, info: (g, info[0], 0))
    kv_spec = pl.BlockSpec((2, 2 * span, head_size), lambda g, info: (0, 0, g))
    o_spec = pl.BlockSpec((span, width), lambda g, info: (0, out_block0(info) + g))
    flops = 4 * span * 2 * span * steps * head_size * group * kv_here
    return pl.pallas_call(
        kernel,
        out_shape=jax.ShapeDtypeStruct((span, out_cols), jnp.bfloat16),
        grid_spec=pltpu.PrefetchScalarGridSpec(
            num_scalar_prefetch=1,
            grid=(kv_here,),
            in_specs=[q_spec] + [kv_spec] * steps,
            out_specs=o_spec,
            scratch_shapes=[
                pltpu.VMEM((2 * steps, group * span, span), jnp.float32),
                pltpu.VMEM((group * span, span), jnp.float32),
                pltpu.VMEM((group * span, span), jnp.float32),
                pltpu.VMEM((group * span, head_size), jnp.float32),
            ],
        ),
        compiler_params=pltpu.CompilerParams(dimension_semantics=("arbitrary",)),
        cost_estimate=pl.CostEstimate(
            flops=flops,
            transcendentals=flops // (4 * head_size),
            bytes_accessed=2 * span * width * kv_here * 2 + steps * 2 * 2 * span * kv_here * head_size * 2,
        ),
    )(info, q2, *blocks)


def body(queries, key_value, span_table):
    rows = queries.shape[0]
    heads_here = queries.shape[1]
    head_size = queries.shape[2]
    kv_here = key_value.shape[2]
    group = heads_here // kv_here
    span = rows // 2
    cycle = lax.axis_size("ctx")
    myself = lax.axis_index("ctx")
    half = lax.axis_index("kvh")
    table = span_table.reshape(cycle, 2)

    q2 = jnp.transpose(queries, (1, 0, 2))
    own = key_value.reshape(2, rows, kv_here * head_size)
    first = shifted(own, "ctx", 1)
    third = shifted(own, "ctx", 3)
    pairs = [(d, d ^ 1) for d in range(cycle)]
    second = lax.ppermute(jnp.where(myself % 2 == 0, first, third), "ctx", pairs)
    blocks = [own, first, second, third]

    sources = (myself - jnp.arange(STEPS, dtype=jnp.int32)) % cycle
    key_spans = table[sources].reshape(2 * STEPS)

    def info_for(qh):
        return jnp.concatenate(
            [jnp.stack([qh, table[myself, qh]]).astype(jnp.int32), key_spans]
        )

    width = heads_here * head_size
    sent_info = info_for(1 - half)
    kept_info = info_for(half)
    common = dict(span=span, group=group, kv_here=kv_here, head_size=head_size)
    sent = attend_half(sent_info, q2, blocks, out_cols=width, out_block0=lambda i: 0, **common)
    arrived = shifted(sent, "kvh", 1)
    out = attend_half(
        kept_info,
        q2,
        blocks,
        out_cols=2 * width,
        out_block0=lambda i: i[0] * kv_here,
        **common,
    )
    return lax.dynamic_update_slice(out, arrived, (0, (1 - half) * width))


def solution(mesh):
    in_specs = (P("ctx", "kvh", None), P(None, "ctx", "kvh", None), P())
    out_specs = P(("ctx", "kvh"), None)
    return jax.shard_map(body, mesh=mesh, in_specs=in_specs, out_specs=out_specs, check_vma=False)
```

time: 282 us -> 88.8 us (0.31)
  the two profiles are of different devices: /device:TPU:388 before, /device:TPU:1 now
where the time goes in v2:
time: 88.8 us; the launch traced here: 88.5 us
  waiting for transfers between devices  32.7 us (37%)
  Pallas kernels  29.3 us (33%)
  starting transfers between devices  17.4 us (20%)
  local copies, waits for them, and re-layouts  6.06 us (7%)
  other arithmetic  2.93 us (3%)
    ppermute x3, waiting for transfers between devices, shifted(): return lax.ppermute(value, axis, pairs)  32.7 us
    pallas_call x2, Pallas kernels, attend_half(): pl.pallas_call(kernel, out_shape=jax.ShapeDtypeStruct((span, out_cols), j...  29.3 us
    ppermute x3, starting transfers between devices, shifted(): return lax.ppermute(value, axis, pairs)  9.31 us
    ppermute x1, starting transfers between devices, body(): lax.ppermute(jnp.where(myself % 2 == 0, first, third), 'ctx', pairs)  8.05 us
    unnamed x9, local copies, waits for them, and re-layouts  2.17 us
    concatenate x1, other arithmetic, info_for(): jnp.concatenate([jnp.stack([qh, table[myself, qh]]).astype(jnp.int32), ke...  2 us
  transfers between devices with their start and end apart: 4, of which 2 were waited for; matrix products, arithmetic and copies ran while one was open for 6% of the time, Pallas kernels for 12%

profile of v2, /device:TPU:1, one launch (start us, length us, event | category | flops | bytes accessed | tf_op | source)
XLA Modules:
  0.0 88.5 jit_solution(7491019593589251870)
XLA Ops:
  0.0 1.4 %reshape.60.refs_0_ = bf16[2,256,512]{2,1,0:T(8,128)(2,1)S(1)} reshape(bf16[2,256,4,128]{3,2,1,0:T(4,128)(2,1)} %param.4) | data formatting | bytes 1048576 | tf_op jit(solution)/shard_map/reshape | solution.py:123
  1.4 0.0 copy-start.1
  1.4 4.6 %collective-permute-start.1 = (bf16[2,256,512]{2,1,0:T(8,128)(2,1)S(1)}, bf16[2,256,512]{2,1,0:T(8,128)(2,1)S(1)}, u32[]{:S(2)}, u32[]{:S(2)}) collective-permute-start(bf16[2,256,512]{2,1,0:T(8,128)(2,1)S(1)} %reshape.60.refs_0_), channel_id=1, source_target_pairs={{0,6},{2,8},{4,10},{6,12},{8,14},{10,16},{12,18},{14,20},{16,22},{... | collective-permute-start | bytes 1572872 | tf_op jit(solution)/shard_map/ppermute | solution.py:16
  6.0 2.8 %collective-permute-start = (bf16[2,256,512]{2,1,0:T(8,128)(2,1)S(1)}, bf16[2,256,512]{2,1,0:T(8,128)(2,1)}, u32[]{:S(2)}, u32[]{:S(2)}) collective-permute-start(bf16[2,256,512]{2,1,0:T(8,128)(2,1)S(1)} %reshape.60.refs_0_), channel_id=1, source_target_pairs={{0,2},{2,4},{4,6},{6,8},{8,10},{10,12},{12,14},{14,16},{16,18},{18... | collective-permute-start | bytes 1572872 | tf_op jit(solution)/shard_map/ppermute | solution.py:16
  8.8 21.3 %collective-permute-done.1.refs_3_ = bf16[2,256,512]{2,1,0:T(8,128)(2,1)S(1)} collective-permute-done((bf16[2,256,512]{2,1,0:T(8,128)(2,1)S(1)}, bf16[2,256,512]{2,1,0:T(8,128)(2,1)S(1)}, u32[]{:S(2)}, u32[]{:S(2)}) %collective-permute-start.1) | collective-permute-done | bytes 524320 | tf_op jit(solution)/shard_map/ppermute | solution.py:16
  30.1 0.0 collective-permute-done.refs_1_
  30.2 0.9 %broadcast_select_fusion = bf16[2,256,512]{2,1,0:T(8,128)(2,1)} fusion(bf16[2,256,512]{2,1,0:T(8,128)(2,1)} %collective-permute-done.refs_1_, bf16[2,256,512]{2,1,0:T(8,128)(2,1)S(1)} %collective-permute-done.1.refs_3_, pred[]{:T(512)S(6)} %eq.7), kind=kLoop, calls=%fused_computation.2 | loop fusion | flops 262144 | bytes 1572865 | tf_op jit(solution)/shard_map/jit(_where)/select_n | solution.py:127
  31.1 8.0 %collective-permute-start.2 = (bf16[2,256,512]{2,1,0:T(8,128)(2,1)}, bf16[2,256,512]{2,1,0:T(8,128)(2,1)}, u32[]{:S(2)}, u32[]{:S(2)}) collective-permute-start(bf16[2,256,512]{2,1,0:T(8,128)(2,1)} %broadcast_select_fusion), channel_id=1, source_target_pairs={{0,2},{2,0},{4,6},{6,4},{8,10},{10,8},{12,14},{14,12},{16,18},{18,... | collective-permute-start | bytes 1572872 | tf_op jit(solution)/shard_map/ppermute | solution.py:127
  39.1 0.0 copy-done.3
  39.1 0.1 reshape.58
  39.3 0.6 gather_fusion
  39.9 0.1 reshape.59
  40.0 0.0 copy-done
  40.0 2.2 %copy.7 = bf16[256,32,128]{2,0,1:T(8,128)(2,1)} copy(bf16[256,32,128]{2,1,0:T(8,128)(2,1)S(1)} %copy-done) | data formatting | bytes 4194304 | tf_op args[0]
  42.1 0.0 copy-done.1
  42.1 0.0 copy-done.2
  42.1 0.7 fusion.2
  42.8 2.0 %add_add_fusion.1 = (s32[10]{0:T(128)}, s32[10]{0:T(128)}) fusion(s32[1]{0:T(128)} %bitcast.5, s32[1]{0:T(128)} %bitcast.4, s32[8]{0:T(128)S(1)} %reshape.59, s32[1]{0:T(128)} %bitcast.1, s32[1]{0:T(128)} %bitcast), kind=kLoop, calls=%fused_computation.11 | loop fusion | flops 40 | bytes 128 | tf_op jit(solution)/shard_map/concatenate | solution.py:134
  44.8 0.0 collective-permute-done.2.refs_2_
  44.8 19.1 %shard_map.38 = bf16[128,4096]{1,0:T(8,128)(2,1)} custom-call(s32[10]{0:T(128)} %get-tuple-element.7.info_ref, bf16[32,256,128]{2,1,0:T(8,128)(2,1)} %bitcast.9, bf16[2,256,512]{2,1,0:T(8,128)(2,1)} %copy-done.1, bf16[2,256,512]{2,1,0:T(8,128)(2,1)} %collective-permute-done.refs_1_, bf16[2,256,512]{2,1,0:T(8,128)(2,1)} %collective-permute-done.2.refs_2_, ...), custom_call_target="tpu_custom_call" | custom-call | flops 2147483648 | bytes 4194304 | tf_op jit(solution)/shard_map/pallas_call | solution.py:86
  63.8 1.9 %collective-permute-start.3 = (bf16[128,4096]{1,0:T(8,128)(2,1)}, bf16[128,4096]{1,0:T(8,128)(2,1)S(1)}, u32[]{:S(2)}, u32[]{:S(2)}) collective-permute-start(bf16[128,4096]{1,0:T(8,128)(2,1)} %shard_map.38), channel_id=1, source_target_pairs={{0,1},{1,0},{2,3},{3,2},{4,5},{5,4},{6,7},{7,6},{8,9},{9,8},{10,11... | collective-permute-start | bytes 3145736 | tf_op jit(solution)/shard_map/ppermute | solution.py:16
  65.8 10.2 %shard_map.37 = bf16[128,8192]{1,0:T(8,128)(2,1)} custom-call(s32[10]{0:T(128)} %get-tuple-element.8.info_ref, bf16[32,256,128]{2,1,0:T(8,128)(2,1)} %bitcast.10, bf16[2,256,512]{2,1,0:T(8,128)(2,1)} %copy-done.1, bf16[2,256,512]{2,1,0:T(8,128)(2,1)} %collective-permute-done.refs_1_, bf16[2,256,512]{2,1,0:T(8,128)(2,1)} %collective-permute-done.2.refs_2_, ...), custom_call_target="tpu_custom_call" | custom-call | flops 2147483648 | bytes 4194304 | tf_op jit(solution)/shard_map/pallas_call | solution.py:86
  76.0 11.4 %collective-permute-done.3 = bf16[128,4096]{1,0:T(8,128)(2,1)S(1)} collective-permute-done((bf16[128,4096]{1,0:T(8,128)(2,1)}, bf16[128,4096]{1,0:T(8,128)(2,1)S(1)}, u32[]{:S(2)}, u32[]{:S(2)}) %collective-permute-start.3) | collective-permute-done | bytes 1048608 | tf_op jit(solution)/shard_map/ppermute | solution.py:16
  87.4 1.1 %constant_dynamic-update-slice_fusion = bf16[128,8192]{1,0:T(8,128)(2,1)} fusion(bf16[128,8192]{1,0:T(8,128)(2,1)} %shard_map.37, bf16[128,4096]{1,0:T(8,128)(2,1)S(1)} %collective-permute-done.3, s32[]{:T(128)S(6)} %select_n.59), kind=kLoop, calls=%fused_computation.12 | loop fusion | bytes 2097156 | tf_op jit(solution)/shard_map/dynamic_update_slice | solution.py:152
  (5 shorter events, 0.0 us)
Async XLA Ops:
  0.0 39.1 %copy-start.3 = (s32[512]{0:T(512)S(1)}, s32[512]{0:T(512)}, u32[]{:S(2)}) copy-start(s32[512]{0:T(512)} %param.5) | copy-start | bytes 6148
  0.0 40.0 %copy-start = (bf16[256,32,128]{2,1,0:T(8,128)(2,1)S(1)}, bf16[256,32,128]{2,1,0:T(8,128)(2,1)}, u32[]{:S(2)}) copy-start(bf16[256,32,128]{2,1,0:T(8,128)(2,1)} %param.3) | copy-start | bytes 6291460
  1.4 40.7 %copy-start.1 = (bf16[2,256,512]{2,1,0:T(8,128)(2,1)}, bf16[2,256,512]{2,1,0:T(8,128)(2,1)S(1)}, u32[]{:S(2)}) copy-start(bf16[2,256,512]{2,1,0:T(8,128)(2,1)S(1)} %reshape.60.refs_0_) | copy-start | bytes 1572868
  1.4 28.7 %collective-permute-start.1 = (bf16[2,256,512]{2,1,0:T(8,128)(2,1)S(1)}, bf16[2,256,512]{2,1,0:T(8,128)(2,1)S(1)}, u32[]{:S(2)}, u32[]{:S(2)}) collective-permute-start(bf16[2,256,512]{2,1,0:T(8,128)(2,1)S(1)} %reshape.60.refs_0_), channel_id=1, source_target_pairs={{0,6},{2,8},{4,10},{6,12},{8,14},{10,16},{12,18},{14,20},{16,22},{... | collective-permute-start | bytes 1572872 | tf_op jit(solution)/shard_map/ppermute | solution.py:16
  6.0 24.1 %collective-permute-start = (bf16[2,256,512]{2,1,0:T(8,128)(2,1)S(1)}, bf16[2,256,512]{2,1,0:T(8,128)(2,1)}, u32[]{:S(2)}, u32[]{:S(2)}) collective-permute-start(bf16[2,256,512]{2,1,0:T(8,128)(2,1)S(1)} %reshape.60.refs_0_), channel_id=1, source_target_pairs={{0,2},{2,4},{4,6},{6,8},{8,10},{10,12},{12,14},{14,16},{16,18},{18... | collective-permute-start | bytes 1572872 | tf_op jit(solution)/shard_map/ppermute | solution.py:16
  30.1 12.0 %copy-start.2 = (bf16[2,256,512]{2,1,0:T(8,128)(2,1)}, bf16[2,256,512]{2,1,0:T(8,128)(2,1)S(1)}, u32[]{:S(2)}) copy-start(bf16[2,256,512]{2,1,0:T(8,128)(2,1)S(1)} %collective-permute-done.1.refs_3_) | copy-start | bytes 1572868
  31.1 13.7 %collective-permute-start.2 = (bf16[2,256,512]{2,1,0:T(8,128)(2,1)}, bf16[2,256,512]{2,1,0:T(8,128)(2,1)}, u32[]{:S(2)}, u32[]{:S(2)}) collective-permute-start(bf16[2,256,512]{2,1,0:T(8,128)(2,1)} %broadcast_select_fusion), channel_id=1, source_target_pairs={{0,2},{2,0},{4,6},{6,4},{8,10},{10,8},{12,14},{14,12},{16,18},{18,... | collective-permute-start | bytes 1572872 | tf_op jit(solution)/shard_map/ppermute | solution.py:127
  63.8 23.5 %collective-permute-start.3 = (bf16[128,4096]{1,0:T(8,128)(2,1)}, bf16[128,4096]{1,0:T(8,128)(2,1)S(1)}, u32[]{:S(2)}, u32[]{:S(2)}) collective-permute-start(bf16[128,4096]{1,0:T(8,128)(2,1)} %shard_map.38), channel_id=1, source_target_pairs={{0,1},{1,0},{2,3},{3,2},{4,5},{5,4},{6,7},{7,6},{8,9},{9,8},{10,11... | collective-permute-start | bytes 3145736 | tf_op jit(solution)/shard_map/ppermute | solution.py:16

commit v3 on v2

--- a/solution.py
+++ b/solution.py
@@ -16,11 +16,16 @@
     return lax.ppermute(value, axis, pairs)
 
 
-def attend_kernel(info_ref, q_ref, *refs, span, group, head_size, steps, scale):
+def attend_kernel(table_ref, where_ref, q_ref, *refs, span, group, head_size, steps, scale):
     kv_refs = refs[:steps]
     o_ref = refs[steps]
     s_ref, mx_ref, sm_ref, acc_ref = refs[steps + 1 :]
-    query_span = info_ref[1]
+    cycle = table_ref.shape[0] // 2
+    myself = where_ref[1]
+    query_span = table_ref[2 * myself + where_ref[0]]
+    key_spans = [
+        table_ref[2 * ((myself + cycle - b) % cycle) + t] for b in range(steps) for t in range(2)
+    ]
     n = group * span
 
     mx_ref[...] = jnp.full(mx_ref.shape, -jnp.inf, jnp.float32)
@@ -40,7 +45,7 @@
         mx_ref[...] = jnp.maximum(mx_ref[...], s)
 
     for idx, (b, t) in enumerate(tiles):
-        key_span = info_ref[2 + idx]
+        key_span = key_spans[idx]
         pl.when(key_span < query_span)(functools.partial(score, idx, b, t, False))
         if b == 0:
             pl.when(key_span == query_span)(functools.partial(score, idx, b, t, True))
@@ -57,7 +62,7 @@
         acc_ref[...] += jnp.dot(p.astype(jnp.bfloat16), v, preferred_element_type=jnp.float32)
 
     for idx, (b, t) in enumerate(tiles):
-        key_span = info_ref[2 + idx]
+        key_span = key_spans[idx]
         pl.when(key_span <= query_span)(functools.partial(weigh, idx, b, t))
 
     total = jnp.sum(sm_ref[...], axis=1, keepdims=True)
@@ -68,7 +73,7 @@
         ].astype(o_ref.dtype)
 
 
-def attend_half(info, q2, blocks, *, span, group, kv_here, head_size, out_cols, out_block0):
+def attend_half(table, where, q2, blocks, *, span, group, head_size, first, count, out_cols, out_block0):
     steps = len(blocks)
     width = group * head_size
     kernel = functools.partial(
@@ -79,16 +84,16 @@
         steps=steps,
         scale=1.0 / head_size**0.5,
     )
-    q_spec = pl.BlockSpec((group, span, head_size), lambda g, info: (g, info[0], 0))
-    kv_spec = pl.BlockSpec((2, 2 * span, head_size), lambda g, info: (0, 0, g))
-    o_spec = pl.BlockSpec((span, width), lambda g, info: (0, out_block0(info) + g))
-    flops = 4 * span * 2 * span * steps * head_size * group * kv_here
+    q_spec = pl.BlockSpec((group, span, head_size), lambda g, tb, w: (g + first, w[0], 0))
+    kv_spec = pl.BlockSpec((2, 2 * span, head_size), lambda g, tb, w: (0, 0, g + first))
+    o_spec = pl.BlockSpec((span, width), lambda g, tb, w: (0, out_block0(w) + g))
+    flops = 4 * span * 2 * span * steps * head_size * group * count
     return pl.pallas_call(
         kernel,
         out_shape=jax.ShapeDtypeStruct((span, out_cols), jnp.bfloat16),
         grid_spec=pltpu.PrefetchScalarGridSpec(
-            num_scalar_prefetch=1,
-            grid=(kv_here,),
+            num_scalar_prefetch=2,
+            grid=(count,),
             in_specs=[q_spec] + [kv_spec] * steps,
             out_specs=o_spec,
             scratch_shapes=[
@@ -102,9 +107,9 @@
         cost_estimate=pl.CostEstimate(
             flops=flops,
             transcendentals=flops // (4 * head_size),
-            bytes_accessed=2 * span * width * kv_here * 2 + steps * 2 * 2 * span * kv_here * head_size * 2,
+            bytes_accessed=2 * span * width * count * 2 + steps * 2 * 2 * span * count * head_size * 2,
         ),
-    )(info, q2, *blocks)
+    )(table, where, q2, *blocks)
 
 
 def body(queries, key_value, span_table):
@@ -127,29 +132,29 @@
     second = lax.ppermute(jnp.where(myself % 2 == 0, first, third), "ctx", pairs)
     blocks = [own, first, second, third]
 
-    sources = (myself - jnp.arange(STEPS, dtype=jnp.int32)) % cycle
-    key_spans = table[sources].reshape(2 * STEPS)
-
-    def info_for(qh):
-        return jnp.concatenate(
-            [jnp.stack([qh, table[myself, qh]]).astype(jnp.int32), key_spans]
+    width = heads_here * head_size
+    lanes = jnp.arange(2, dtype=jnp.int32)
+    sent_where = jnp.where(lanes == 0, 1 - half, myself).astype(jnp.int32)
+    kept_where = jnp.where(lanes == 0, half, myself).astype(jnp.int32)
+    common = dict(span=span, group=group, head_size=head_size)
+    chunks = 2
+    per = kv_here // chunks
+    arrived = []
+    for j in range(chunks):
+        sent = attend_half(
+            span_table, sent_where, q2, blocks, first=j * per, count=per,
+            out_cols=per * group * head_size, out_block0=lambda w: 0, **common,
         )
-
-    width = heads_here * head_size
-    sent_info = info_for(1 - half)
-    kept_info = info_for(half)
-    common = dict(span=span, group=group, kv_here=kv_here, head_size=head_size)
-    sent = attend_half(sent_info, q2, blocks, out_cols=width, out_block0=lambda i: 0, **common)
-    arrived = shifted(sent, "kvh", 1)
+        arrived.append(shifted(sent, "kvh", 1))
     out = attend_half(
-        kept_info,
-        q2,
-        blocks,
-        out_cols=2 * width,
-        out_block0=lambda i: i[0] * kv_here,
-        **common,
+        span_table, kept_where, q2, blocks, first=0, count=kv_here,
+        out_cols=2 * width, out_block0=lambda w: w[0] * kv_here, **common,
     )
-    return lax.dynamic_update_slice(out, arrived, (0, (1 - half) * width))
+    for j in range(chunks):
+        out = lax.dynamic_update_slice(
+            out, arrived[j], (0, (1 - half) * width + j * per * group * head_size)
+        )
+    return out
 
 
 def solution(mesh):

time: 88.8 us -> 88.5 us (level)
  the two profiles are of different devices: /device:TPU:1 before, /device:TPU:4 now
where the time goes in v3:
time: 88.5 us; the launch traced here: 88 us
  Pallas kernels  30 us (34%)
  waiting for transfers between devices  26.5 us (30%)
  starting transfers between devices  22.8 us (26%)
  local copies, waits for them, and re-layouts  7.47 us (8%)
  other arithmetic  1.17 us (1%)
    pallas_call x3, Pallas kernels, attend_half(): pl.pallas_call(kernel, out_shape=jax.ShapeDtypeStruct((span, out_cols), j...  30 us
    ppermute x4, waiting for transfers between devices, shifted(): return lax.ppermute(value, axis, pairs)  26.5 us
    ppermute x4, starting transfers between devices, shifted(): return lax.ppermute(value, axis, pairs)  20.8 us
    unnamed x9, local copies, waits for them, and re-layouts  4.57 us
    ppermute x1, starting transfers between devices, body(): lax.ppermute(jnp.where(myself % 2 == 0, first, third), 'ctx', pairs)  1.92 us
  transfers between devices with their start and end apart: 5, of which 2 were waited for; matrix products, arithmetic and copies ran while one was open for 6% of the time, Pallas kernels for 28%

profile of v3, /device:TPU:4, one launch (start us, length us, event | category | flops | bytes accessed | tf_op | source)
XLA Modules:
  0.0 88.0 jit_solution(11040504850128028064)
XLA Ops:
  0.0 1.2 %reshape.3.refs_0_ = bf16[2,256,512]{2,1,0:T(8,128)(2,1)S(1)} reshape(bf16[2,256,4,128]{3,2,1,0:T(4,128)(2,1)} %param.4) | data formatting | bytes 1048576 | tf_op jit(solution)/shard_map/reshape | solution.py:128
  1.2 0.0 copy-start
  1.3 2.5 %collective-permute-start.1 = (bf16[2,256,512]{2,1,0:T(8,128)(2,1)S(1)}, bf16[2,256,512]{2,1,0:T(8,128)(2,1)S(1)}, u32[]{:S(2)}, u32[]{:S(2)}) collective-permute-start(bf16[2,256,512]{2,1,0:T(8,128)(2,1)S(1)} %reshape.3.refs_0_), channel_id=1, source_target_pairs={{0,6},{2,8},{4,10},{6,12},{8,14},{10,16},{12,18},{14,20},{16,22},{... | collective-permute-start | bytes 1572872 | tf_op jit(solution)/shard_map/ppermute | solution.py:16
  3.8 3.0 %collective-permute-start = (bf16[2,256,512]{2,1,0:T(8,128)(2,1)S(1)}, bf16[2,256,512]{2,1,0:T(8,128)(2,1)S(1)}, u32[]{:S(2)}, u32[]{:S(2)}) collective-permute-start(bf16[2,256,512]{2,1,0:T(8,128)(2,1)S(1)} %reshape.3.refs_0_), channel_id=1, source_target_pairs={{0,2},{2,4},{4,6},{6,8},{8,10},{10,12},{12,14},{14,16},{16,18},{18... | collective-permute-start | bytes 1572872 | tf_op jit(solution)/shard_map/ppermute | solution.py:16
  6.8 14.6 %collective-permute-done.1.refs_3_ = bf16[2,256,512]{2,1,0:T(8,128)(2,1)S(1)} collective-permute-done((bf16[2,256,512]{2,1,0:T(8,128)(2,1)S(1)}, bf16[2,256,512]{2,1,0:T(8,128)(2,1)S(1)}, u32[]{:S(2)}, u32[]{:S(2)}) %collective-permute-start.1) | collective-permute-done | bytes 524320 | tf_op jit(solution)/shard_map/ppermute | solution.py:16
  21.4 11.9 %collective-permute-done.refs_1_ = bf16[2,256,512]{2,1,0:T(8,128)(2,1)S(1)} collective-permute-done((bf16[2,256,512]{2,1,0:T(8,128)(2,1)S(1)}, bf16[2,256,512]{2,1,0:T(8,128)(2,1)S(1)}, u32[]{:S(2)}, u32[]{:S(2)}) %collective-permute-start) | collective-permute-done | bytes 524320 | tf_op jit(solution)/shard_map/ppermute | solution.py:16
  33.3 0.1 broadcast_select_fusion
  33.3 1.9 %collective-permute-start.2 = (bf16[2,256,512]{2,1,0:T(8,128)(2,1)S(1)}, bf16[2,256,512]{2,1,0:T(8,128)(2,1)S(1)}, u32[]{:S(2)}, u32[]{:S(2)}) collective-permute-start(bf16[2,256,512]{2,1,0:T(8,128)(2,1)S(1)} %broadcast_select_fusion), channel_id=1, source_target_pairs={{0,2},{2,0},{4,6},{6,4},{8,10},{10,8},{12,14},{14,12},{16,18},{18,... | collective-permute-start | bytes 1572872 | tf_op jit(solution)/shard_map/ppermute | solution.py:132
  35.3 3.7 %copy.6 = bf16[256,32,128]{2,0,1:T(8,128)(2,1)} copy(bf16[256,32,128]{2,1,0:T(8,128)(2,1)} %param.3) | data formatting | bytes 4194304 | tf_op args[0]
  39.0 0.0 copy-done
  39.0 0.0 copy-done.2
  39.0 0.5 compare_select_fusion.where_ref
  39.5 0.0 collective-permute-done.2.refs_2_
  39.5 0.8 copy-done.3
  40.4 5.5 %shard_map.38 = bf16[128,2048]{1,0:T(8,128)(2,1)} custom-call(s32[512]{0:T(512)} %table_ref.5, s32[2]{0:T(128)} %compare_select_fusion.where_ref, bf16[32,256,128]{2,1,0:T(8,128)(2,1)} %bitcast.3, bf16[2,256,512]{2,1,0:T(8,128)(2,1)} %copy-done, bf16[2,256,512]{2,1,0:T(8,128)(2,1)} %copy-done.2, bf16[2,256,512]{2,1,0:T(8,128)(2,1)} %copy-done.3, ...), custom_call_target="tpu_custom_call" | custom-call | flops 1073741824 | bytes 2097152 | tf_op jit(solution)/shard_map/pallas_call | solution.py:91
  45.8 8.1 %collective-permute-start.3 = (bf16[128,2048]{1,0:T(8,128)(2,1)}, bf16[128,2048]{1,0:T(8,128)(2,1)S(1)}, u32[]{:S(2)}, u32[]{:S(2)}) collective-permute-start(bf16[128,2048]{1,0:T(8,128)(2,1)} %shard_map.38), channel_id=1, source_target_pairs={{0,1},{1,0},{2,3},{3,2},{4,5},{5,4},{6,7},{7,6},{8,9},{9,8},{10,11... | collective-permute-start | bytes 1572872 | tf_op jit(solution)/shard_map/ppermute | solution.py:16
  53.9 5.5 %shard_map.39 = bf16[128,2048]{1,0:T(8,128)(2,1)} custom-call(s32[512]{0:T(512)} %table_ref.5, s32[2]{0:T(128)} %compare_select_fusion.where_ref, bf16[32,256,128]{2,1,0:T(8,128)(2,1)} %bitcast.4, bf16[2,256,512]{2,1,0:T(8,128)(2,1)} %copy-done, bf16[2,256,512]{2,1,0:T(8,128)(2,1)} %copy-done.2, bf16[2,256,512]{2,1,0:T(8,128)(2,1)} %copy-done.3, ...), custom_call_target="tpu_custom_call" | custom-call | flops 1073741824 | bytes 2097152 | tf_op jit(solution)/shard_map/pallas_call | solution.py:91
  59.4 7.3 %collective-permute-start.4 = (bf16[128,2048]{1,0:T(8,128)(2,1)}, bf16[128,2048]{1,0:T(8,128)(2,1)S(1)}, u32[]{:S(2)}, u32[]{:S(2)}) collective-permute-start(bf16[128,2048]{1,0:T(8,128)(2,1)} %shard_map.39), channel_id=1, source_target_pairs={{0,1},{1,0},{2,3},{3,2},{4,5},{5,4},{6,7},{7,6},{8,9},{9,8},{10,11... | collective-permute-start | bytes 1572872 | tf_op jit(solution)/shard_map/ppermute | solution.py:16
  66.6 0.6 compare_select_fusion.1.where_ref
  67.2 19.1 %shard_map.37 = bf16[128,8192]{1,0:T(8,128)(2,1)} custom-call(s32[512]{0:T(512)} %table_ref.5, s32[2]{0:T(128)} %compare_select_fusion.1.where_ref, bf16[32,256,128]{2,1,0:T(8,128)(2,1)} %bitcast.5, bf16[2,256,512]{2,1,0:T(8,128)(2,1)} %copy-done, bf16[2,256,512]{2,1,0:T(8,128)(2,1)} %copy-done.2, bf16[2,256,512]{2,1,0:T(8,128)(2,1)} %copy-done.3, ...), custom_call_target="tpu_custom_call" | custom-call | flops 2147483648 | bytes 4194304 | tf_op jit(solution)/shard_map/pallas_call | solution.py:91
  86.3 0.0 collective-permute-done.3
  86.3 0.8 constant_dynamic-update-slice_fusion.1
  87.2 0.0 collective-permute-done.4
  87.2 0.8 constant_dynamic-update-slice_fusion
  (4 shorter events, 0.0 us)
Async XLA Ops:
  1.2 37.8 %copy-start = (bf16[2,256,512]{2,1,0:T(8,128)(2,1)}, bf16[2,256,512]{2,1,0:T(8,128)(2,1)S(1)}, u32[]{:S(2)}) copy-start(bf16[2,256,512]{2,1,0:T(8,128)(2,1)S(1)} %reshape.3.refs_0_) | copy-start | bytes 1572868
  1.3 20.2 %collective-permute-start.1 = (bf16[2,256,512]{2,1,0:T(8,128)(2,1)S(1)}, bf16[2,256,512]{2,1,0:T(8,128)(2,1)S(1)}, u32[]{:S(2)}, u32[]{:S(2)}) collective-permute-start(bf16[2,256,512]{2,1,0:T(8,128)(2,1)S(1)} %reshape.3.refs_0_), channel_id=1, source_target_pairs={{0,6},{2,8},{4,10},{6,12},{8,14},{10,16},{12,18},{14,20},{16,22},{... | collective-permute-start | bytes 1572872 | tf_op jit(solution)/shard_map/ppermute | solution.py:16
  3.8 29.5 %collective-permute-start = (bf16[2,256,512]{2,1,0:T(8,128)(2,1)S(1)}, bf16[2,256,512]{2,1,0:T(8,128)(2,1)S(1)}, u32[]{:S(2)}, u32[]{:S(2)}) collective-permute-start(bf16[2,256,512]{2,1,0:T(8,128)(2,1)S(1)} %reshape.3.refs_0_), channel_id=1, source_target_pairs={{0,2},{2,4},{4,6},{6,8},{8,10},{10,12},{12,14},{14,16},{16,18},{18... | collective-permute-start | bytes 1572872 | tf_op jit(solution)/shard_map/ppermute | solution.py:16
  21.4 17.6 %copy-start.1 = (bf16[2,256,512]{2,1,0:T(8,128)(2,1)}, bf16[2,256,512]{2,1,0:T(8,128)(2,1)S(1)}, u32[]{:S(2)}) copy-start(bf16[2,256,512]{2,1,0:T(8,128)(2,1)S(1)} %collective-permute-done.1.refs_3_) | copy-start | bytes 1572868
  33.3 5.8 %copy-start.2 = (bf16[2,256,512]{2,1,0:T(8,128)(2,1)}, bf16[2,256,512]{2,1,0:T(8,128)(2,1)S(1)}, u32[]{:S(2)}) copy-start(bf16[2,256,512]{2,1,0:T(8,128)(2,1)S(1)} %collective-permute-done.refs_1_) | copy-start | bytes 1572868
  33.3 6.2 %collective-permute-start.2 = (bf16[2,256,512]{2,1,0:T(8,128)(2,1)S(1)}, bf16[2,256,512]{2,1,0:T(8,128)(2,1)S(1)}, u32[]{:S(2)}, u32[]{:S(2)}) collective-permute-start(bf16[2,256,512]{2,1,0:T(8,128)(2,1)S(1)} %broadcast_select_fusion), channel_id=1, source_target_pairs={{0,2},{2,0},{4,6},{6,4},{8,10},{10,8},{12,14},{14,12},{16,18},{18,... | collective-permute-start | bytes 1572872 | tf_op jit(solution)/shard_map/ppermute | solution.py:132
  39.5 0.8 copy-start.3
  45.8 40.5 %collective-permute-start.3 = (bf16[128,2048]{1,0:T(8,128)(2,1)}, bf16[128,2048]{1,0:T(8,128)(2,1)S(1)}, u32[]{:S(2)}, u32[]{:S(2)}) collective-permute-start(bf16[128,2048]{1,0:T(8,128)(2,1)} %shard_map.38), channel_id=1, source_target_pairs={{0,1},{1,0},{2,3},{3,2},{4,5},{5,4},{6,7},{7,6},{8,9},{9,8},{10,11... | collective-permute-start | bytes 1572872 | tf_op jit(solution)/shard_map/ppermute | solution.py:16
  59.4 27.8 %collective-permute-start.4 = (bf16[128,2048]{1,0:T(8,128)(2,1)}, bf16[128,2048]{1,0:T(8,128)(2,1)S(1)}, u32[]{:S(2)}, u32[]{:S(2)}) collective-permute-start(bf16[128,2048]{1,0:T(8,128)(2,1)} %shard_map.39), channel_id=1, source_target_pairs={{0,1},{1,0},{2,3},{3,2},{4,5},{5,4},{6,7},{7,6},{8,9},{9,8},{10,11... | collective-permute-start | bytes 1572872 | tf_op jit(solution)/shard_map/ppermute | solution.py:16

commit v4 on v3

--- a/solution.py
+++ b/solution.py
@@ -33,16 +33,13 @@
 
     def score(idx, b, t, masked):
         k = kv_refs[b][0, t * span : (t + 1) * span, :]
-        q = q_ref[...].reshape(n, head_size)
-        s = lax.dot_general(
-            q, k, (((1,), (1,)), ((), ())), preferred_element_type=jnp.float32
-        ) * scale
+        s = jnp.dot(k, q_ref[...], preferred_element_type=jnp.float32) * scale
         if masked:
-            row = lax.broadcasted_iota(jnp.int32, (n, span), 0) % span
-            col = lax.broadcasted_iota(jnp.int32, (n, span), 1)
-            s = jnp.where(col <= row, s, -jnp.inf)
+            key = lax.broadcasted_iota(jnp.int32, (span, n), 0)
+            query = lax.broadcasted_iota(jnp.int32, (span, n), 1) % span
+            s = jnp.where(key <= query, s, -jnp.inf)
         s_ref[idx] = s
-        mx_ref[...] = jnp.maximum(mx_ref[...], s)
+        mx_ref[...] = jnp.maximum(mx_ref[...], jnp.max(s, axis=0, keepdims=True))
 
     for idx, (b, t) in enumerate(tiles):
         key_span = key_spans[idx]
@@ -50,27 +47,27 @@
         if b == 0:
             pl.when(key_span == query_span)(functools.partial(score, idx, b, t, True))
 
-    m = jnp.max(mx_ref[...], axis=1, keepdims=True)
-    mx_ref[...] = jnp.broadcast_to(m, (n, span))
     sm_ref[...] = jnp.zeros(sm_ref.shape, jnp.float32)
     acc_ref[...] = jnp.zeros(acc_ref.shape, jnp.float32)
 
     def weigh(idx, b, t):
         p = jnp.exp(s_ref[idx] - mx_ref[...])
-        sm_ref[...] += p
+        sm_ref[...] += jnp.sum(p, axis=0, keepdims=True)
         v = kv_refs[b][1, t * span : (t + 1) * span, :]
-        acc_ref[...] += jnp.dot(p.astype(jnp.bfloat16), v, preferred_element_type=jnp.float32)
+        acc_ref[...] += lax.dot_general(
+            v, p.astype(jnp.bfloat16), (((0,), (0,)), ((), ())),
+            preferred_element_type=jnp.float32,
+        )
 
     for idx, (b, t) in enumerate(tiles):
         key_span = key_spans[idx]
         pl.when(key_span <= query_span)(functools.partial(weigh, idx, b, t))
 
-    total = jnp.sum(sm_ref[...], axis=1, keepdims=True)
-    result = acc_ref[...] / total
+    result = acc_ref[...] / sm_ref[...]
     for h in range(group):
-        o_ref[:, h * head_size : (h + 1) * head_size] = result[
-            h * span : (h + 1) * span, :
-        ].astype(o_ref.dtype)
+        o_ref[:, h * head_size : (h + 1) * head_size] = (
+            result[:, h * span : (h + 1) * span].T.astype(o_ref.dtype)
+        )
 
 
 def attend_half(table, where, q2, blocks, *, span, group, head_size, first, count, out_cols, out_block0):
@@ -84,7 +81,7 @@
         steps=steps,
         scale=1.0 / head_size**0.5,
     )
-    q_spec = pl.BlockSpec((group, span, head_size), lambda g, tb, w: (g + first, w[0], 0))
+    q_spec = pl.BlockSpec((None, head_size, group * span), lambda g, tb, w: (w[0], 0, g + first))
     kv_spec = pl.BlockSpec((2, 2 * span, head_size), lambda g, tb, w: (0, 0, g + first))
     o_spec = pl.BlockSpec((span, width), lambda g, tb, w: (0, out_block0(w) + g))
     flops = 4 * span * 2 * span * steps * head_size * group * count
@@ -97,10 +94,10 @@
             in_specs=[q_spec] + [kv_spec] * steps,
             out_specs=o_spec,
             scratch_shapes=[
-                pltpu.VMEM((2 * steps, group * span, span), jnp.float32),
-                pltpu.VMEM((group * span, span), jnp.float32),
-                pltpu.VMEM((group * span, span), jnp.float32),
-                pltpu.VMEM((group * span, head_size), jnp.float32),
+                pltpu.VMEM((2 * steps, span, group * span), jnp.float32),
+                pltpu.VMEM((1, group * span), jnp.float32),
+                pltpu.VMEM((1, group * span), jnp.float32),
+                pltpu.VMEM((head_size, group * span), jnp.float32),
             ],
         ),
         compiler_params=pltpu.CompilerParams(dimension_semantics=("arbitrary",)),
@@ -124,7 +121,11 @@
     half = lax.axis_index("kvh")
     table = span_table.reshape(cycle, 2)
 
-    q2 = jnp.transpose(queries, (1, 0, 2))
+    q2 = (
+        queries.reshape(2, span, heads_here, head_size)
+        .transpose(0, 3, 2, 1)
+        .reshape(2, head_size, heads_here * span)
+    )
     own = key_value.reshape(2, rows, kv_here * head_size)
     first = shifted(own, "ctx", 1)
     third = shifted(own, "ctx", 3)

time: 88.5 us -> 91.9 us (1.038)
  the two profiles are of different devices: /device:TPU:4 before, /device:TPU:5 now
where the time goes in v4:
time: 91.9 us; the launch traced here: 91.4 us
  starting transfers between devices  31.4 us (34%)
  Pallas kernels  27.5 us (30%)
  waiting for transfers between devices  20.9 us (23%)
  local copies, waits for them, and re-layouts  9.48 us (10%)
  other arithmetic  1.95 us (2%)
    pallas_call x3, Pallas kernels, attend_half(): pl.pallas_call(kernel, out_shape=jax.ShapeDtypeStruct((span, out_cols), j...  27.5 us
    ppermute x4, starting transfers between devices, shifted(): return lax.ppermute(value, axis, pairs)  24.4 us
    ppermute x4, waiting for transfers between devices, shifted(): return lax.ppermute(value, axis, pairs)  20.9 us
    ppermute x1, starting transfers between devices, body(): lax.ppermute(jnp.where(myself % 2 == 0, first, third), 'ctx', pairs)  7.07 us
    reshape x1, local copies, waits for them, and re-layouts, body(): queries.reshape(2, span, heads_here, head_size).transpose(0, 3, 2, 1)  4.28 us
    reshape x1, local copies, waits for them, and re-layouts, body(): q2 = queries.reshape(2, span, heads_here, head_size).transpose(0, 3, 2, 1...  2.29 us
  transfers between devices with their start and end apart: 5, of which 1 were waited for; matrix products, arithmetic and copies ran while one was open for 9% of the time, Pallas kernels for 26%

profile of v4, /device:TPU:5, one launch (start us, length us, event | category | flops | bytes accessed | tf_op | source)
XLA Modules:
  0.0 91.4 jit_solution(15561756789853115024)
XLA Ops:
  0.0 1.2 %reshape.11.refs_0_ = bf16[2,256,512]{2,1,0:T(8,128)(2,1)S(1)} reshape(bf16[2,256,4,128]{3,2,1,0:T(4,128)(2,1)} %param.4) | data formatting | bytes 1048576 | tf_op jit(solution)/shard_map/reshape | solution.py:129
  1.2 0.0 copy-start
  1.3 3.8 %collective-permute-start.1 = (bf16[2,256,512]{2,1,0:T(8,128)(2,1)S(1)}, bf16[2,256,512]{2,1,0:T(8,128)(2,1)S(1)}, u32[]{:S(2)}, u32[]{:S(2)}) collective-permute-start(bf16[2,256,512]{2,1,0:T(8,128)(2,1)S(1)} %reshape.11.refs_0_), channel_id=1, source_target_pairs={{0,6},{2,8},{4,10},{6,12},{8,14},{10,16},{12,18},{14,20},{16,22},{... | collective-permute-start | bytes 1572872 | tf_op jit(solution)/shard_map/ppermute | solution.py:16
  5.0 2.8 %collective-permute-start = (bf16[2,256,512]{2,1,0:T(8,128)(2,1)S(1)}, bf16[2,256,512]{2,1,0:T(8,128)(2,1)S(1)}, u32[]{:S(2)}, u32[]{:S(2)}) collective-permute-start(bf16[2,256,512]{2,1,0:T(8,128)(2,1)S(1)} %reshape.11.refs_0_), channel_id=1, source_target_pairs={{0,2},{2,4},{4,6},{6,8},{8,10},{10,12},{12,14},{14,16},{16,18},{18... | collective-permute-start | bytes 1572872 | tf_op jit(solution)/shard_map/ppermute | solution.py:16
  7.9 20.9 %collective-permute-done.1.refs_3_ = bf16[2,256,512]{2,1,0:T(8,128)(2,1)S(1)} collective-permute-done((bf16[2,256,512]{2,1,0:T(8,128)(2,1)S(1)}, bf16[2,256,512]{2,1,0:T(8,128)(2,1)S(1)}, u32[]{:S(2)}, u32[]{:S(2)}) %collective-permute-start.1) | collective-permute-done | bytes 524320 | tf_op jit(solution)/shard_map/ppermute | solution.py:16
  28.8 0.0 collective-permute-done.refs_1_
  28.8 0.9 broadcast_select_fusion
  29.7 7.1 %collective-permute-start.2 = (bf16[2,256,512]{2,1,0:T(8,128)(2,1)}, bf16[2,256,512]{2,1,0:T(8,128)(2,1)}, u32[]{:S(2)}, u32[]{:S(2)}) collective-permute-start(bf16[2,256,512]{2,1,0:T(8,128)(2,1)} %broadcast_select_fusion), channel_id=1, source_target_pairs={{0,2},{2,0},{4,6},{6,4},{8,10},{10,8},{12,14},{14,12},{16,18},{18,... | collective-permute-start | bytes 1572872 | tf_op jit(solution)/shard_map/ppermute | solution.py:133
  36.8 0.0 copy-done.2
  36.8 4.3 %copy.4 = bf16[2,128,32,128]{1,2,3,0:T(8,128)(2,1)S(1)} copy(bf16[2,128,32,128]{3,2,1,0:T(8,128)(2,1)} %bitcast.5) | data formatting | bytes 4194304 | tf_op jit(solution)/shard_map/reshape | solution.py:125
  41.1 0.0 copy-done
  41.1 2.3 %reshape.10.q_ref = bf16[2,128,4096]{2,1,0:T(8,128)(2,1)} reshape(bf16[2,128,32,128]{3,2,1,0:T(8,128)(2,1)S(1)} %bitcast.4) | data formatting | bytes 4194304 | tf_op jit(solution)/shard_map/reshape | solution.py:127
  43.4 0.5 compare_select_fusion.where_ref
  43.9 0.0 collective-permute-done.2.refs_2_
  43.9 4.2 %shard_map.38 = bf16[128,2048]{1,0:T(8,128)(2,1)} custom-call(s32[512]{0:T(512)} %table_ref.5, s32[2]{0:T(128)} %compare_select_fusion.where_ref, bf16[2,128,4096]{2,1,0:T(8,128)(2,1)} %reshape.10.q_ref, bf16[2,256,512]{2,1,0:T(8,128)(2,1)} %copy-done, bf16[2,256,512]{2,1,0:T(8,128)(2,1)} %copy-done.2, bf16[2,256,512]{2,1,0:T(8,128)(2,1)} %collective-permute-done.2.refs_2_, ...), custom_call_target="tpu_custom_call" | custom-call | flops 1073741824 | bytes 2097152 | tf_op jit(solution)/shard_map/pallas_call | solution.py:88
  48.1 9.1 %collective-permute-start.3 = (bf16[128,2048]{1,0:T(8,128)(2,1)}, bf16[128,2048]{1,0:T(8,128)(2,1)S(1)}, u32[]{:S(2)}, u32[]{:S(2)}) collective-permute-start(bf16[128,2048]{1,0:T(8,128)(2,1)} %shard_map.38), channel_id=1, source_target_pairs={{0,1},{1,0},{2,3},{3,2},{4,5},{5,4},{6,7},{7,6},{8,9},{9,8},{10,11... | collective-permute-start | bytes 1572872 | tf_op jit(solution)/shard_map/ppermute | solution.py:16
  57.2 4.1 %shard_map.39 = bf16[128,2048]{1,0:T(8,128)(2,1)} custom-call(s32[512]{0:T(512)} %table_ref.5, s32[2]{0:T(128)} %compare_select_fusion.where_ref, bf16[2,128,4096]{2,1,0:T(8,128)(2,1)} %reshape.10.q_ref, bf16[2,256,512]{2,1,0:T(8,128)(2,1)} %copy-done, bf16[2,256,512]{2,1,0:T(8,128)(2,1)} %copy-done.2, bf16[2,256,512]{2,1,0:T(8,128)(2,1)} %collective-permute-done.2.refs_2_, ...), custom_call_target="tpu_custom_call" | custom-call | flops 1073741824 | bytes 2097152 | tf_op jit(solution)/shard_map/pallas_call | solution.py:88
  61.3 8.7 %collective-permute-start.4 = (bf16[128,2048]{1,0:T(8,128)(2,1)}, bf16[128,2048]{1,0:T(8,128)(2,1)S(1)}, u32[]{:S(2)}, u32[]{:S(2)}) collective-permute-start(bf16[128,2048]{1,0:T(8,128)(2,1)} %shard_map.39), channel_id=1, source_target_pairs={{0,1},{1,0},{2,3},{3,2},{4,5},{5,4},{6,7},{7,6},{8,9},{9,8},{10,11... | collective-permute-start | bytes 1572872 | tf_op jit(solution)/shard_map/ppermute | solution.py:16
  70.0 0.5 compare_select_fusion.1.where_ref
  70.5 19.2 %shard_map.37 = bf16[128,8192]{1,0:T(8,128)(2,1)} custom-call(s32[512]{0:T(512)} %table_ref.5, s32[2]{0:T(128)} %compare_select_fusion.1.where_ref, bf16[2,128,4096]{2,1,0:T(8,128)(2,1)} %reshape.10.q_ref, bf16[2,256,512]{2,1,0:T(8,128)(2,1)} %copy-done, bf16[2,256,512]{2,1,0:T(8,128)(2,1)} %copy-done.2, ...), custom_call_target="tpu_custom_call" | custom-call | flops 2147483648 | bytes 4194304 | tf_op jit(solution)/shard_map/pallas_call | solution.py:88
  89.7 0.0 collective-permute-done.3
  89.7 0.8 constant_dynamic-update-slice_fusion.1
  90.5 0.0 collective-permute-done.4
  90.5 0.8 constant_dynamic-update-slice_fusion
  (3 shorter events, 0.0 us)
Async XLA Ops:
  1.2 39.8 %copy-start = (bf16[2,256,512]{2,1,0:T(8,128)(2,1)}, bf16[2,256,512]{2,1,0:T(8,128)(2,1)S(1)}, u32[]{:S(2)}) copy-start(bf16[2,256,512]{2,1,0:T(8,128)(2,1)S(1)} %reshape.11.refs_0_) | copy-start | bytes 1572868
  1.3 27.5 %collective-permute-start.1 = (bf16[2,256,512]{2,1,0:T(8,128)(2,1)S(1)}, bf16[2,256,512]{2,1,0:T(8,128)(2,1)S(1)}, u32[]{:S(2)}, u32[]{:S(2)}) collective-permute-start(bf16[2,256,512]{2,1,0:T(8,128)(2,1)S(1)} %reshape.11.refs_0_), channel_id=1, source_target_pairs={{0,6},{2,8},{4,10},{6,12},{8,14},{10,16},{12,18},{14,20},{16,22},{... | collective-permute-start | bytes 1572872 | tf_op jit(solution)/shard_map/ppermute | solution.py:16
  5.0 23.7 %collective-permute-start = (bf16[2,256,512]{2,1,0:T(8,128)(2,1)S(1)}, bf16[2,256,512]{2,1,0:T(8,128)(2,1)S(1)}, u32[]{:S(2)}, u32[]{:S(2)}) collective-permute-start(bf16[2,256,512]{2,1,0:T(8,128)(2,1)S(1)} %reshape.11.refs_0_), channel_id=1, source_target_pairs={{0,2},{2,4},{4,6},{6,8},{8,10},{10,12},{12,14},{14,16},{16,18},{18... | collective-permute-start | bytes 1572872 | tf_op jit(solution)/shard_map/ppermute | solution.py:16
  28.8 12.3 %copy-start.1 = (bf16[2,256,512]{2,1,0:T(8,128)(2,1)}, bf16[2,256,512]{2,1,0:T(8,128)(2,1)S(1)}, u32[]{:S(2)}) copy-start(bf16[2,256,512]{2,1,0:T(8,128)(2,1)S(1)} %collective-permute-done.1.refs_3_) | copy-start | bytes 1572868
  28.8 8.0 %copy-start.2 = (bf16[2,256,512]{2,1,0:T(8,128)(2,1)}, bf16[2,256,512]{2,1,0:T(8,128)(2,1)S(1)}, u32[]{:S(2)}) copy-start(bf16[2,256,512]{2,1,0:T(8,128)(2,1)S(1)} %collective-permute-done.refs_1_) | copy-start | bytes 1572868
  29.7 14.2 %collective-permute-start.2 = (bf16[2,256,512]{2,1,0:T(8,128)(2,1)}, bf16[2,256,512]{2,1,0:T(8,128)(2,1)}, u32[]{:S(2)}, u32[]{:S(2)}) collective-permute-start(bf16[2,256,512]{2,1,0:T(8,128)(2,1)} %broadcast_select_fusion), channel_id=1, source_target_pairs={{0,2},{2,0},{4,6},{6,4},{8,10},{10,8},{12,14},{14,12},{16,18},{18,... | collective-permute-start | bytes 1572872 | tf_op jit(solution)/shard_map/ppermute | solution.py:133
  48.1 41.7 %collective-permute-start.3 = (bf16[128,2048]{1,0:T(8,128)(2,1)}, bf16[128,2048]{1,0:T(8,128)(2,1)S(1)}, u32[]{:S(2)}, u32[]{:S(2)}) collective-permute-start(bf16[128,2048]{1,0:T(8,128)(2,1)} %shard_map.38), channel_id=1, source_target_pairs={{0,1},{1,0},{2,3},{3,2},{4,5},{5,4},{6,7},{7,6},{8,9},{9,8},{10,11... | collective-permute-start | bytes 1572872 | tf_op jit(solution)/shard_map/ppermute | solution.py:16
  61.3 29.2 %collective-permute-start.4 = (bf16[128,2048]{1,0:T(8,128)(2,1)}, bf16[128,2048]{1,0:T(8,128)(2,1)S(1)}, u32[]{:S(2)}, u32[]{:S(2)}) collective-permute-start(bf16[128,2048]{1,0:T(8,128)(2,1)} %shard_map.39), channel_id=1, source_target_pairs={{0,1},{1,0},{2,3},{3,2},{4,5},{5,4},{6,7},{7,6},{8,9},{9,8},{10,11... | collective-permute-start | bytes 1572872 | tf_op jit(solution)/shard_map/ppermute | solution.py:16

commit v5 on v4

--- a/solution.py
+++ b/solution.py
@@ -19,7 +19,7 @@
 def attend_kernel(table_ref, where_ref, q_ref, *refs, span, group, head_size, steps, scale):
     kv_refs = refs[:steps]
     o_ref = refs[steps]
-    s_ref, mx_ref, sm_ref, acc_ref = refs[steps + 1 :]
+    s_ref, mx_ref, sm_ref, acc_ref, qt_ref = refs[steps + 1 :]
     cycle = table_ref.shape[0] // 2
     myself = where_ref[1]
     query_span = table_ref[2 * myself + where_ref[0]]
@@ -29,11 +29,12 @@
     n = group * span
 
     mx_ref[...] = jnp.full(mx_ref.shape, -jnp.inf, jnp.float32)
+    qt_ref[...] = q_ref[...].reshape(n, head_size).T
     tiles = [(b, t) for b in range(steps) for t in range(2)]
 
     def score(idx, b, t, masked):
         k = kv_refs[b][0, t * span : (t + 1) * span, :]
-        s = jnp.dot(k, q_ref[...], preferred_element_type=jnp.float32) * scale
+        s = jnp.dot(k, qt_ref[...], preferred_element_type=jnp.float32) * scale
         if masked:
             key = lax.broadcasted_iota(jnp.int32, (span, n), 0)
             query = lax.broadcasted_iota(jnp.int32, (span, n), 1) % span
@@ -54,10 +55,7 @@
         p = jnp.exp(s_ref[idx] - mx_ref[...])
         sm_ref[...] += jnp.sum(p, axis=0, keepdims=True)
         v = kv_refs[b][1, t * span : (t + 1) * span, :]
-        acc_ref[...] += lax.dot_general(
-            v, p.astype(jnp.bfloat16), (((0,), (0,)), ((), ())),
-            preferred_element_type=jnp.float32,
-        )
+        acc_ref[...] += jnp.dot(v.T, p.astype(jnp.bfloat16), preferred_element_type=jnp.float32)
 
     for idx, (b, t) in enumerate(tiles):
         key_span = key_spans[idx]
@@ -81,7 +79,7 @@
         steps=steps,
         scale=1.0 / head_size**0.5,
     )
-    q_spec = pl.BlockSpec((None, head_size, group * span), lambda g, tb, w: (w[0], 0, g + first))
+    q_spec = pl.BlockSpec((group, span, head_size), lambda g, tb, w: (g + first, w[0], 0))
     kv_spec = pl.BlockSpec((2, 2 * span, head_size), lambda g, tb, w: (0, 0, g + first))
     o_spec = pl.BlockSpec((span, width), lambda g, tb, w: (0, out_block0(w) + g))
     flops = 4 * span * 2 * span * steps * head_size * group * count
@@ -98,6 +96,7 @@
                 pltpu.VMEM((1, group * span), jnp.float32),
                 pltpu.VMEM((1, group * span), jnp.float32),
                 pltpu.VMEM((head_size, group * span), jnp.float32),
+                pltpu.VMEM((head_size, group * span), jnp.bfloat16),
             ],
         ),
         compiler_params=pltpu.CompilerParams(dimension_semantics=("arbitrary",)),
@@ -121,11 +120,7 @@
     half = lax.axis_index("kvh")
     table = span_table.reshape(cycle, 2)
 
-    q2 = (
-        queries.reshape(2, span, heads_here, head_size)
-        .transpose(0, 3, 2, 1)
-        .reshape(2, head_size, heads_here * span)
-    )
+    q2 = jnp.transpose(queries, (1, 0, 2))
     own = key_value.reshape(2, rows, kv_here * head_size)
     first = shifted(own, "ctx", 1)
     third = shifted(own, "ctx", 3)

time: 91.9 us -> 89.9 us (0.978)
  Pallas kernels: 27.5 us -> 30.2 us
  local copies, waits for them, and re-layouts: 9.48 us -> 7.47 us
  starting transfers between devices: 31.4 us -> 29.6 us
    reshape x2 -> x0, local copies, waits for them, and re-layouts: 6.57 us -> none  [the longest x1 4.28 us: body(): queries.reshape(2, span, heads_here, head_size).transpose(0, 3, 2, 1)]
    unnamed x6 -> x9, local copies, waits for them, and re-layouts: 0.01 us -> 4.57 us
    pallas_call x3, Pallas kernels: 27.5 us -> 30.2 us  [attend_half(): pl.pallas_call(kernel, out_shape=jax.ShapeDtypeStruct((span, out_cols), j...]
    ppermute x4, starting transfers between devices: 24.4 us -> 22.5 us  [shifted(): return lax.ppermute(value, axis, pairs)]
  transfers between devices with their start and end apart: 5 -> 5, of which waited for: 1 -> 1; matrix products, arithmetic and copies ran while one was open for 9% -> 6% of each run, Pallas kernels for 26% -> 28%
where the time goes in v5:
time: 89.9 us; the launch traced here: 89.4 us
  Pallas kernels  30.2 us (34%)
  starting transfers between devices  29.6 us (33%)
  waiting for transfers between devices  20.9 us (23%)
  local copies, waits for them, and re-layouts  7.47 us (8%)
  other arithmetic  1.17 us (1%)
    pallas_call x3, Pallas kernels, attend_half(): pl.pallas_call(kernel, out_shape=jax.ShapeDtypeStruct((span, out_cols), j...  30.2 us
    ppermute x4, starting transfers between devices, shifted(): return lax.ppermute(value, axis, pairs)  22.5 us
    ppermute x4, waiting for transfers between devices, shifted(): return lax.ppermute(value, axis, pairs)  20.9 us
    ppermute x1, starting transfers between devices, body(): lax.ppermute(jnp.where(myself % 2 == 0, first, third), 'ctx', pairs)  7.09 us
    unnamed x9, local copies, waits for them, and re-layouts  4.57 us
  transfers between devices with their start and end apart: 5, of which 1 were waited for; matrix products, arithmetic and copies ran while one was open for 6% of the time, Pallas kernels for 28%

profile of v5, /device:TPU:5, one launch (start us, length us, event | category | flops | bytes accessed | tf_op | source)
XLA Modules:
  0.0 89.4 jit_solution(3504923820401990746)
XLA Ops:
  0.0 1.2 %reshape.3.refs_0_ = bf16[2,256,512]{2,1,0:T(8,128)(2,1)S(1)} reshape(bf16[2,256,4,128]{3,2,1,0:T(4,128)(2,1)} %param.4) | data formatting | bytes 1048576 | tf_op jit(solution)/shard_map/reshape | solution.py:124
  1.2 0.0 copy-start
  1.3 3.8 %collective-permute-start.1 = (bf16[2,256,512]{2,1,0:T(8,128)(2,1)S(1)}, bf16[2,256,512]{2,1,0:T(8,128)(2,1)S(1)}, u32[]{:S(2)}, u32[]{:S(2)}) collective-permute-start(bf16[2,256,512]{2,1,0:T(8,128)(2,1)S(1)} %reshape.3.refs_0_), channel_id=1, source_target_pairs={{0,6},{2,8},{4,10},{6,12},{8,14},{10,16},{12,18},{14,20},{16,22},{... | collective-permute-start | bytes 1572872 | tf_op jit(solution)/shard_map/ppermute | solution.py:16
  5.0 2.8 %collective-permute-start = (bf16[2,256,512]{2,1,0:T(8,128)(2,1)S(1)}, bf16[2,256,512]{2,1,0:T(8,128)(2,1)S(1)}, u32[]{:S(2)}, u32[]{:S(2)}) collective-permute-start(bf16[2,256,512]{2,1,0:T(8,128)(2,1)S(1)} %reshape.3.refs_0_), channel_id=1, source_target_pairs={{0,2},{2,4},{4,6},{6,8},{8,10},{10,12},{12,14},{14,16},{16,18},{18... | collective-permute-start | bytes 1572872 | tf_op jit(solution)/shard_map/ppermute | solution.py:16
  7.9 20.9 %collective-permute-done.1.refs_3_ = bf16[2,256,512]{2,1,0:T(8,128)(2,1)S(1)} collective-permute-done((bf16[2,256,512]{2,1,0:T(8,128)(2,1)S(1)}, bf16[2,256,512]{2,1,0:T(8,128)(2,1)S(1)}, u32[]{:S(2)}, u32[]{:S(2)}) %collective-permute-start.1) | collective-permute-done | bytes 524320 | tf_op jit(solution)/shard_map/ppermute | solution.py:16
  28.8 0.0 collective-permute-done.refs_1_
  28.8 0.1 broadcast_select_fusion
  28.8 7.1 %collective-permute-start.2 = (bf16[2,256,512]{2,1,0:T(8,128)(2,1)S(1)}, bf16[2,256,512]{2,1,0:T(8,128)(2,1)S(1)}, u32[]{:S(2)}, u32[]{:S(2)}) collective-permute-start(bf16[2,256,512]{2,1,0:T(8,128)(2,1)S(1)} %broadcast_select_fusion), channel_id=1, source_target_pairs={{0,2},{2,0},{4,6},{6,4},{8,10},{10,8},{12,14},{14,12},{16,18},{18,... | collective-permute-start | bytes 1572872 | tf_op jit(solution)/shard_map/ppermute | solution.py:128
  35.9 3.7 %copy.6 = bf16[256,32,128]{2,0,1:T(8,128)(2,1)} copy(bf16[256,32,128]{2,1,0:T(8,128)(2,1)} %param.3) | data formatting | bytes 4194304 | tf_op args[0]
  39.7 0.0 copy-done
  39.7 0.0 copy-done.1
  39.7 0.5 compare_select_fusion.where_ref
  40.2 0.0 collective-permute-done.2.refs_2_
  40.2 0.8 copy-done.3
  41.0 5.3 %shard_map.38 = bf16[128,2048]{1,0:T(8,128)(2,1)} custom-call(s32[512]{0:T(512)} %table_ref.5, s32[2]{0:T(128)} %compare_select_fusion.where_ref, bf16[32,256,128]{2,1,0:T(8,128)(2,1)} %bitcast.3, bf16[2,256,512]{2,1,0:T(8,128)(2,1)} %copy-done, bf16[2,256,512]{2,1,0:T(8,128)(2,1)} %copy-done.2, bf16[2,256,512]{2,1,0:T(8,128)(2,1)} %copy-done.3, ...), custom_call_target="tpu_custom_call" | custom-call | flops 1073741824 | bytes 2097152 | tf_op jit(solution)/shard_map/pallas_call | solution.py:86
  46.3 8.2 %collective-permute-start.3 = (bf16[128,2048]{1,0:T(8,128)(2,1)}, bf16[128,2048]{1,0:T(8,128)(2,1)S(1)}, u32[]{:S(2)}, u32[]{:S(2)}) collective-permute-start(bf16[128,2048]{1,0:T(8,128)(2,1)} %shard_map.38), channel_id=1, source_target_pairs={{0,1},{1,0},{2,3},{3,2},{4,5},{5,4},{6,7},{7,6},{8,9},{9,8},{10,11... | collective-permute-start | bytes 1572872 | tf_op jit(solution)/shard_map/ppermute | solution.py:16
  54.5 5.3 %shard_map.39 = bf16[128,2048]{1,0:T(8,128)(2,1)} custom-call(s32[512]{0:T(512)} %table_ref.5, s32[2]{0:T(128)} %compare_select_fusion.where_ref, bf16[32,256,128]{2,1,0:T(8,128)(2,1)} %bitcast.4, bf16[2,256,512]{2,1,0:T(8,128)(2,1)} %copy-done, bf16[2,256,512]{2,1,0:T(8,128)(2,1)} %copy-done.2, bf16[2,256,512]{2,1,0:T(8,128)(2,1)} %copy-done.3, ...), custom_call_target="tpu_custom_call" | custom-call | flops 1073741824 | bytes 2097152 | tf_op jit(solution)/shard_map/pallas_call | solution.py:86
  59.8 7.7 %collective-permute-start.4 = (bf16[128,2048]{1,0:T(8,128)(2,1)}, bf16[128,2048]{1,0:T(8,128)(2,1)S(1)}, u32[]{:S(2)}, u32[]{:S(2)}) collective-permute-start(bf16[128,2048]{1,0:T(8,128)(2,1)} %shard_map.39), channel_id=1, source_target_pairs={{0,1},{1,0},{2,3},{3,2},{4,5},{5,4},{6,7},{7,6},{8,9},{9,8},{10,11... | collective-permute-start | bytes 1572872 | tf_op jit(solution)/shard_map/ppermute | solution.py:16
  67.5 0.6 compare_select_fusion.1.where_ref
  68.1 19.6 %shard_map.37 = bf16[128,8192]{1,0:T(8,128)(2,1)} custom-call(s32[512]{0:T(512)} %table_ref.5, s32[2]{0:T(128)} %compare_select_fusion.1.where_ref, bf16[32,256,128]{2,1,0:T(8,128)(2,1)} %bitcast.5, bf16[2,256,512]{2,1,0:T(8,128)(2,1)} %copy-done, bf16[2,256,512]{2,1,0:T(8,128)(2,1)} %copy-done.2, bf16[2,256,512]{2,1,0:T(8,128)(2,1)} %copy-done.3, ...), custom_call_target="tpu_custom_call" | custom-call | flops 2147483648 | bytes 4194304 | tf_op jit(solution)/shard_map/pallas_call | solution.py:86
  87.7 0.0 collective-permute-done.3
  87.7 0.8 constant_dynamic-update-slice_fusion.1
  88.6 0.0 collective-permute-done.4
  88.6 0.8 constant_dynamic-update-slice_fusion
  (4 shorter events, 0.0 us)
Async XLA Ops:
  1.2 38.4 %copy-start = (bf16[2,256,512]{2,1,0:T(8,128)(2,1)}, bf16[2,256,512]{2,1,0:T(8,128)(2,1)S(1)}, u32[]{:S(2)}) copy-start(bf16[2,256,512]{2,1,0:T(8,128)(2,1)S(1)} %reshape.3.refs_0_) | copy-start | bytes 1572868
  1.3 27.5 %collective-permute-start.1 = (bf16[2,256,512]{2,1,0:T(8,128)(2,1)S(1)}, bf16[2,256,512]{2,1,0:T(8,128)(2,1)S(1)}, u32[]{:S(2)}, u32[]{:S(2)}) collective-permute-start(bf16[2,256,512]{2,1,0:T(8,128)(2,1)S(1)} %reshape.3.refs_0_), channel_id=1, source_target_pairs={{0,6},{2,8},{4,10},{6,12},{8,14},{10,16},{12,18},{14,20},{16,22},{... | collective-permute-start | bytes 1572872 | tf_op jit(solution)/shard_map/ppermute | solution.py:16
  5.0 23.7 %collective-permute-start = (bf16[2,256,512]{2,1,0:T(8,128)(2,1)S(1)}, bf16[2,256,512]{2,1,0:T(8,128)(2,1)S(1)}, u32[]{:S(2)}, u32[]{:S(2)}) collective-permute-start(bf16[2,256,512]{2,1,0:T(8,128)(2,1)S(1)} %reshape.3.refs_0_), channel_id=1, source_target_pairs={{0,2},{2,4},{4,6},{6,8},{8,10},{10,12},{12,14},{14,16},{16,18},{18... | collective-permute-start | bytes 1572872 | tf_op jit(solution)/shard_map/ppermute | solution.py:16
  28.8 10.9 %copy-start.1 = (bf16[2,256,512]{2,1,0:T(8,128)(2,1)}, bf16[2,256,512]{2,1,0:T(8,128)(2,1)S(1)}, u32[]{:S(2)}) copy-start(bf16[2,256,512]{2,1,0:T(8,128)(2,1)S(1)} %collective-permute-done.1.refs_3_) | copy-start | bytes 1572868
  28.8 10.9 %copy-start.2 = (bf16[2,256,512]{2,1,0:T(8,128)(2,1)}, bf16[2,256,512]{2,1,0:T(8,128)(2,1)S(1)}, u32[]{:S(2)}) copy-start(bf16[2,256,512]{2,1,0:T(8,128)(2,1)S(1)} %collective-permute-done.refs_1_) | copy-start | bytes 1572868
  28.8 11.4 %collective-permute-start.2 = (bf16[2,256,512]{2,1,0:T(8,128)(2,1)S(1)}, bf16[2,256,512]{2,1,0:T(8,128)(2,1)S(1)}, u32[]{:S(2)}, u32[]{:S(2)}) collective-permute-start(bf16[2,256,512]{2,1,0:T(8,128)(2,1)S(1)} %broadcast_select_fusion), channel_id=1, source_target_pairs={{0,2},{2,0},{4,6},{6,4},{8,10},{10,8},{12,14},{14,12},{16,18},{18,... | collective-permute-start | bytes 1572872 | tf_op jit(solution)/shard_map/ppermute | solution.py:128
  40.2 0.8 copy-start.3
  46.3 41.4 %collective-permute-start.3 = (bf16[128,2048]{1,0:T(8,128)(2,1)}, bf16[128,2048]{1,0:T(8,128)(2,1)S(1)}, u32[]{:S(2)}, u32[]{:S(2)}) collective-permute-start(bf16[128,2048]{1,0:T(8,128)(2,1)} %shard_map.38), channel_id=1, source_target_pairs={{0,1},{1,0},{2,3},{3,2},{4,5},{5,4},{6,7},{7,6},{8,9},{9,8},{10,11... | collective-permute-start | bytes 1572872 | tf_op jit(solution)/shard_map/ppermute | solution.py:16
  59.8 28.8 %collective-permute-start.4 = (bf16[128,2048]{1,0:T(8,128)(2,1)}, bf16[128,2048]{1,0:T(8,128)(2,1)S(1)}, u32[]{:S(2)}, u32[]{:S(2)}) collective-permute-start(bf16[128,2048]{1,0:T(8,128)(2,1)} %shard_map.39), channel_id=1, source_target_pairs={{0,1},{1,0},{2,3},{3,2},{4,5},{5,4},{6,7},{7,6},{8,9},{9,8},{10,11... | collective-permute-start | bytes 1572872 | tf_op jit(solution)/shard_map/ppermute | solution.py:16

commit v6 on v3

--- a/solution.py
+++ b/solution.py
@@ -19,7 +19,7 @@
 def attend_kernel(table_ref, where_ref, q_ref, *refs, span, group, head_size, steps, scale):
     kv_refs = refs[:steps]
     o_ref = refs[steps]
-    s_ref, mx_ref, sm_ref, acc_ref = refs[steps + 1 :]
+    mx_ref, sm_ref, acc_ref = refs[steps + 1 :]
     cycle = table_ref.shape[0] // 2
     myself = where_ref[1]
     query_span = table_ref[2 * myself + where_ref[0]]
@@ -28,42 +28,45 @@
     ]
     n = group * span
 
-    mx_ref[...] = jnp.full(mx_ref.shape, -jnp.inf, jnp.float32)
     tiles = [(b, t) for b in range(steps) for t in range(2)]
+    row = lax.broadcasted_iota(jnp.int32, (n, span), 0) % span
+    col = lax.broadcasted_iota(jnp.int32, (n, span), 1)
 
-    def score(idx, b, t, masked):
+    def scores(idx, b, t):
         k = kv_refs[b][0, t * span : (t + 1) * span, :]
         q = q_ref[...].reshape(n, head_size)
         s = lax.dot_general(
             q, k, (((1,), (1,)), ((), ())), preferred_element_type=jnp.float32
         ) * scale
-        if masked:
-            row = lax.broadcasted_iota(jnp.int32, (n, span), 0) % span
-            col = lax.broadcasted_iota(jnp.int32, (n, span), 1)
-            s = jnp.where(col <= row, s, -jnp.inf)
-        s_ref[idx] = s
-        mx_ref[...] = jnp.maximum(mx_ref[...], s)
+        if b == 0:
+            s = jnp.where((col <= row) | (key_spans[idx] < query_span), s, -jnp.inf)
+        return s
 
-    for idx, (b, t) in enumerate(tiles):
-        key_span = key_spans[idx]
-        pl.when(key_span < query_span)(functools.partial(score, idx, b, t, False))
-        if b == 0:
-            pl.when(key_span == query_span)(functools.partial(score, idx, b, t, True))
+    mx_ref[...] = scores(0, 0, 0)
+
+    def widen(idx, b, t):
+        mx_ref[...] = jnp.maximum(mx_ref[...], scores(idx, b, t))
+
+    for idx, (b, t) in enumerate(tiles[1:], start=1):
+        pl.when(key_spans[idx] <= query_span)(functools.partial(widen, idx, b, t))
 
     m = jnp.max(mx_ref[...], axis=1, keepdims=True)
     mx_ref[...] = jnp.broadcast_to(m, (n, span))
-    sm_ref[...] = jnp.zeros(sm_ref.shape, jnp.float32)
-    acc_ref[...] = jnp.zeros(acc_ref.shape, jnp.float32)
 
-    def weigh(idx, b, t):
-        p = jnp.exp(s_ref[idx] - mx_ref[...])
-        sm_ref[...] += p
+    def weigh(idx, b, t, first):
+        p = jnp.exp(scores(idx, b, t) - mx_ref[...])
         v = kv_refs[b][1, t * span : (t + 1) * span, :]
-        acc_ref[...] += jnp.dot(p.astype(jnp.bfloat16), v, preferred_element_type=jnp.float32)
+        out = jnp.dot(p.astype(jnp.bfloat16), v, preferred_element_type=jnp.float32)
+        if first:
+            sm_ref[...] = p
+            acc_ref[...] = out
+        else:
+            sm_ref[...] += p
+            acc_ref[...] += out
 
-    for idx, (b, t) in enumerate(tiles):
-        key_span = key_spans[idx]
-        pl.when(key_span <= query_span)(functools.partial(weigh, idx, b, t))
+    weigh(0, 0, 0, True)
+    for idx, (b, t) in enumerate(tiles[1:], start=1):
+        pl.when(key_spans[idx] <= query_span)(functools.partial(weigh, idx, b, t, False))
 
     total = jnp.sum(sm_ref[...], axis=1, keepdims=True)
     result = acc_ref[...] / total
@@ -97,7 +100,6 @@
             in_specs=[q_spec] + [kv_spec] * steps,
             out_specs=o_spec,
             scratch_shapes=[
-                pltpu.VMEM((2 * steps, group * span, span), jnp.float32),
                 pltpu.VMEM((group * span, span), jnp.float32),
                 pltpu.VMEM((group * span, span), jnp.float32),
                 pltpu.VMEM((group * span, head_size), jnp.float32),

time: 88.5 us -> 98.8 us (1.12)
  Pallas kernels: 30 us -> 38.1 us
  starting transfers between devices: 22.8 us -> 24.9 us
    pallas_call x3, Pallas kernels: 30 us -> 38.1 us  [attend_half(): pl.pallas_call(kernel, out_shape=jax.ShapeDtypeStruct((span, out_cols), j...]
    ppermute x4, starting transfers between devices: 20.8 us -> 23 us  [shifted(): return lax.ppermute(value, axis, pairs)]
  transfers between devices with their start and end apart: 5 -> 5, of which waited for: 2 -> 2; matrix products, arithmetic and copies ran while one was open for 6% -> 6% of each run, Pallas kernels for 28% -> 32%
where the time goes in v6:
time: 98.8 us; the launch traced here: 98.3 us
  Pallas kernels  38.1 us (39%)
  waiting for transfers between devices  26.5 us (27%)
  starting transfers between devices  24.9 us (25%)
  local copies, waits for them, and re-layouts  7.47 us (8%)
  other arithmetic  1.17 us (1%)
    pallas_call x3, Pallas kernels, attend_half(): pl.pallas_call(kernel, out_shape=jax.ShapeDtypeStruct((span, out_cols), j...  38.1 us
    ppermute x4, waiting for transfers between devices, shifted(): return lax.ppermute(value, axis, pairs)  26.5 us
    ppermute x4, starting transfers between devices, shifted(): return lax.ppermute(value, axis, pairs)  23 us
    unnamed x9, local copies, waits for them, and re-layouts  4.57 us
  transfers between devices with their start and end apart: 5, of which 2 were waited for; matrix products, arithmetic and copies ran while one was open for 6% of the time, Pallas kernels for 32%

profile of v6, /device:TPU:4, one launch (start us, length us, event | category | flops | bytes accessed | tf_op | source)
XLA Modules:
  0.0 98.3 jit_solution(700374278905879977)
XLA Ops:
  0.0 1.2 %reshape.3.refs_0_ = bf16[2,256,512]{2,1,0:T(8,128)(2,1)S(1)} reshape(bf16[2,256,4,128]{3,2,1,0:T(4,128)(2,1)} %param.4) | data formatting | bytes 1048576 | tf_op jit(solution)/shard_map/reshape | solution.py:130
  1.2 0.0 copy-start
  1.3 2.5 %collective-permute-start.1 = (bf16[2,256,512]{2,1,0:T(8,128)(2,1)S(1)}, bf16[2,256,512]{2,1,0:T(8,128)(2,1)S(1)}, u32[]{:S(2)}, u32[]{:S(2)}) collective-permute-start(bf16[2,256,512]{2,1,0:T(8,128)(2,1)S(1)} %reshape.3.refs_0_), channel_id=1, source_target_pairs={{0,6},{2,8},{4,10},{6,12},{8,14},{10,16},{12,18},{14,20},{16,22},{... | collective-permute-start | bytes 1572872 | tf_op jit(solution)/shard_map/ppermute | solution.py:16
  3.8 3.0 %collective-permute-start = (bf16[2,256,512]{2,1,0:T(8,128)(2,1)S(1)}, bf16[2,256,512]{2,1,0:T(8,128)(2,1)S(1)}, u32[]{:S(2)}, u32[]{:S(2)}) collective-permute-start(bf16[2,256,512]{2,1,0:T(8,128)(2,1)S(1)} %reshape.3.refs_0_), channel_id=1, source_target_pairs={{0,2},{2,4},{4,6},{6,8},{8,10},{10,12},{12,14},{14,16},{16,18},{18... | collective-permute-start | bytes 1572872 | tf_op jit(solution)/shard_map/ppermute | solution.py:16
  6.8 14.6 %collective-permute-done.1.refs_3_ = bf16[2,256,512]{2,1,0:T(8,128)(2,1)S(1)} collective-permute-done((bf16[2,256,512]{2,1,0:T(8,128)(2,1)S(1)}, bf16[2,256,512]{2,1,0:T(8,128)(2,1)S(1)}, u32[]{:S(2)}, u32[]{:S(2)}) %collective-permute-start.1) | collective-permute-done | bytes 524320 | tf_op jit(solution)/shard_map/ppermute | solution.py:16
  21.4 11.9 %collective-permute-done.refs_1_ = bf16[2,256,512]{2,1,0:T(8,128)(2,1)S(1)} collective-permute-done((bf16[2,256,512]{2,1,0:T(8,128)(2,1)S(1)}, bf16[2,256,512]{2,1,0:T(8,128)(2,1)S(1)}, u32[]{:S(2)}, u32[]{:S(2)}) %collective-permute-start) | collective-permute-done | bytes 524320 | tf_op jit(solution)/shard_map/ppermute | solution.py:16
  33.3 0.1 broadcast_select_fusion
  33.3 1.9 %collective-permute-start.2 = (bf16[2,256,512]{2,1,0:T(8,128)(2,1)S(1)}, bf16[2,256,512]{2,1,0:T(8,128)(2,1)S(1)}, u32[]{:S(2)}, u32[]{:S(2)}) collective-permute-start(bf16[2,256,512]{2,1,0:T(8,128)(2,1)S(1)} %broadcast_select_fusion), channel_id=1, source_target_pairs={{0,2},{2,0},{4,6},{6,4},{8,10},{10,8},{12,14},{14,12},{16,18},{18,... | collective-permute-start | bytes 1572872 | tf_op jit(solution)/shard_map/ppermute | solution.py:134
  35.3 3.7 %copy.6 = bf16[256,32,128]{2,0,1:T(8,128)(2,1)} copy(bf16[256,32,128]{2,1,0:T(8,128)(2,1)} %param.3) | data formatting | bytes 4194304 | tf_op args[0]
  39.0 0.0 copy-done
  39.0 0.0 copy-done.1
  39.0 0.5 compare_select_fusion.where_ref
  39.5 0.0 collective-permute-done.2.refs_2_
  39.5 0.8 copy-done.3
  40.4 7.0 %shard_map.38 = bf16[128,2048]{1,0:T(8,128)(2,1)} custom-call(s32[512]{0:T(512)} %table_ref.5, s32[2]{0:T(128)} %compare_select_fusion.where_ref, bf16[32,256,128]{2,1,0:T(8,128)(2,1)} %bitcast.3, bf16[2,256,512]{2,1,0:T(8,128)(2,1)} %copy-done, bf16[2,256,512]{2,1,0:T(8,128)(2,1)} %copy-done.2, bf16[2,256,512]{2,1,0:T(8,128)(2,1)} %copy-done.3, ...), custom_call_target="tpu_custom_call" | custom-call | flops 1073741824 | bytes 2097152 | tf_op jit(solution)/shard_map/pallas_call | solution.py:94
  47.4 9.0 %collective-permute-start.3 = (bf16[128,2048]{1,0:T(8,128)(2,1)}, bf16[128,2048]{1,0:T(8,128)(2,1)S(1)}, u32[]{:S(2)}, u32[]{:S(2)}) collective-permute-start(bf16[128,2048]{1,0:T(8,128)(2,1)} %shard_map.38), channel_id=1, source_target_pairs={{0,1},{1,0},{2,3},{3,2},{4,5},{5,4},{6,7},{7,6},{8,9},{9,8},{10,11... | collective-permute-start | bytes 1572872 | tf_op jit(solution)/shard_map/ppermute | solution.py:16
  56.4 7.0 %shard_map.39 = bf16[128,2048]{1,0:T(8,128)(2,1)} custom-call(s32[512]{0:T(512)} %table_ref.5, s32[2]{0:T(128)} %compare_select_fusion.where_ref, bf16[32,256,128]{2,1,0:T(8,128)(2,1)} %bitcast.4, bf16[2,256,512]{2,1,0:T(8,128)(2,1)} %copy-done, bf16[2,256,512]{2,1,0:T(8,128)(2,1)} %copy-done.2, bf16[2,256,512]{2,1,0:T(8,128)(2,1)} %copy-done.3, ...), custom_call_target="tpu_custom_call" | custom-call | flops 1073741824 | bytes 2097152 | tf_op jit(solution)/shard_map/pallas_call | solution.py:94
  63.4 8.4 %collective-permute-start.4 = (bf16[128,2048]{1,0:T(8,128)(2,1)}, bf16[128,2048]{1,0:T(8,128)(2,1)S(1)}, u32[]{:S(2)}, u32[]{:S(2)}) collective-permute-start(bf16[128,2048]{1,0:T(8,128)(2,1)} %shard_map.39), channel_id=1, source_target_pairs={{0,1},{1,0},{2,3},{3,2},{4,5},{5,4},{6,7},{7,6},{8,9},{9,8},{10,11... | collective-permute-start | bytes 1572872 | tf_op jit(solution)/shard_map/ppermute | solution.py:16
  71.9 0.6 compare_select_fusion.1.where_ref
  72.5 24.1 %shard_map.37 = bf16[128,8192]{1,0:T(8,128)(2,1)} custom-call(s32[512]{0:T(512)} %table_ref.5, s32[2]{0:T(128)} %compare_select_fusion.1.where_ref, bf16[32,256,128]{2,1,0:T(8,128)(2,1)} %bitcast.5, bf16[2,256,512]{2,1,0:T(8,128)(2,1)} %copy-done, bf16[2,256,512]{2,1,0:T(8,128)(2,1)} %copy-done.2, bf16[2,256,512]{2,1,0:T(8,128)(2,1)} %copy-done.3, ...), custom_call_target="tpu_custom_call" | custom-call | flops 2147483648 | bytes 4194304 | tf_op jit(solution)/shard_map/pallas_call | solution.py:94
  96.6 0.0 collective-permute-done.3
  96.6 0.8 constant_dynamic-update-slice_fusion.1
  97.4 0.0 collective-permute-done.4
  97.4 0.8 constant_dynamic-update-slice_fusion
  (4 shorter events, 0.0 us)
Async XLA Ops:
  1.2 37.8 %copy-start = (bf16[2,256,512]{2,1,0:T(8,128)(2,1)}, bf16[2,256,512]{2,1,0:T(8,128)(2,1)S(1)}, u32[]{:S(2)}) copy-start(bf16[2,256,512]{2,1,0:T(8,128)(2,1)S(1)} %reshape.3.refs_0_) | copy-start | bytes 1572868
  1.3 20.2 %collective-permute-start.1 = (bf16[2,256,512]{2,1,0:T(8,128)(2,1)S(1)}, bf16[2,256,512]{2,1,0:T(8,128)(2,1)S(1)}, u32[]{:S(2)}, u32[]{:S(2)}) collective-permute-start(bf16[2,256,512]{2,1,0:T(8,128)(2,1)S(1)} %reshape.3.refs_0_), channel_id=1, source_target_pairs={{0,6},{2,8},{4,10},{6,12},{8,14},{10,16},{12,18},{14,20},{16,22},{... | collective-permute-start | bytes 1572872 | tf_op jit(solution)/shard_map/ppermute | solution.py:16
  3.8 29.5 %collective-permute-start = (bf16[2,256,512]{2,1,0:T(8,128)(2,1)S(1)}, bf16[2,256,512]{2,1,0:T(8,128)(2,1)S(1)}, u32[]{:S(2)}, u32[]{:S(2)}) collective-permute-start(bf16[2,256,512]{2,1,0:T(8,128)(2,1)S(1)} %reshape.3.refs_0_), channel_id=1, source_target_pairs={{0,2},{2,4},{4,6},{6,8},{8,10},{10,12},{12,14},{14,16},{16,18},{18... | collective-permute-start | bytes 1572872 | tf_op jit(solution)/shard_map/ppermute | solution.py:16
  21.4 17.6 %copy-start.1 = (bf16[2,256,512]{2,1,0:T(8,128)(2,1)}, bf16[2,256,512]{2,1,0:T(8,128)(2,1)S(1)}, u32[]{:S(2)}) copy-start(bf16[2,256,512]{2,1,0:T(8,128)(2,1)S(1)} %collective-permute-done.1.refs_3_) | copy-start | bytes 1572868
  33.3 5.8 %copy-start.2 = (bf16[2,256,512]{2,1,0:T(8,128)(2,1)}, bf16[2,256,512]{2,1,0:T(8,128)(2,1)S(1)}, u32[]{:S(2)}) copy-start(bf16[2,256,512]{2,1,0:T(8,128)(2,1)S(1)} %collective-permute-done.refs_1_) | copy-start | bytes 1572868
  33.3 6.2 %collective-permute-start.2 = (bf16[2,256,512]{2,1,0:T(8,128)(2,1)S(1)}, bf16[2,256,512]{2,1,0:T(8,128)(2,1)S(1)}, u32[]{:S(2)}, u32[]{:S(2)}) collective-permute-start(bf16[2,256,512]{2,1,0:T(8,128)(2,1)S(1)} %broadcast_select_fusion), channel_id=1, source_target_pairs={{0,2},{2,0},{4,6},{6,4},{8,10},{10,8},{12,14},{14,12},{16,18},{18,... | collective-permute-start | bytes 1572872 | tf_op jit(solution)/shard_map/ppermute | solution.py:134
  39.5 0.8 copy-start.3
  47.4 49.2 %collective-permute-start.3 = (bf16[128,2048]{1,0:T(8,128)(2,1)}, bf16[128,2048]{1,0:T(8,128)(2,1)S(1)}, u32[]{:S(2)}, u32[]{:S(2)}) collective-permute-start(bf16[128,2048]{1,0:T(8,128)(2,1)} %shard_map.38), channel_id=1, source_target_pairs={{0,1},{1,0},{2,3},{3,2},{4,5},{5,4},{6,7},{7,6},{8,9},{9,8},{10,11... | collective-permute-start | bytes 1572872 | tf_op jit(solution)/shard_map/ppermute | solution.py:16
  63.4 34.0 %collective-permute-start.4 = (bf16[128,2048]{1,0:T(8,128)(2,1)}, bf16[128,2048]{1,0:T(8,128)(2,1)S(1)}, u32[]{:S(2)}, u32[]{:S(2)}) collective-permute-start(bf16[128,2048]{1,0:T(8,128)(2,1)} %shard_map.39), channel_id=1, source_target_pairs={{0,1},{1,0},{2,3},{3,2},{4,5},{5,4},{6,7},{7,6},{8,9},{9,8},{10,11... | collective-permute-start | bytes 1572872 | tf_op jit(solution)/shard_map/ppermute | solution.py:16

commit v7 on v6

--- a/solution.py
+++ b/solution.py
@@ -19,7 +19,7 @@
 def attend_kernel(table_ref, where_ref, q_ref, *refs, span, group, head_size, steps, scale):
     kv_refs = refs[:steps]
     o_ref = refs[steps]
-    mx_ref, sm_ref, acc_ref = refs[steps + 1 :]
+    s_ref, mx_ref, sm_ref, acc_ref = refs[steps + 1 :]
     cycle = table_ref.shape[0] // 2
     myself = where_ref[1]
     query_span = table_ref[2 * myself + where_ref[0]]
@@ -29,32 +29,30 @@
     n = group * span
 
     tiles = [(b, t) for b in range(steps) for t in range(2)]
-    row = lax.broadcasted_iota(jnp.int32, (n, span), 0) % span
-    col = lax.broadcasted_iota(jnp.int32, (n, span), 1)
 
-    def scores(idx, b, t):
+    def score(idx, b, t, first):
         k = kv_refs[b][0, t * span : (t + 1) * span, :]
         q = q_ref[...].reshape(n, head_size)
-        s = lax.dot_general(
-            q, k, (((1,), (1,)), ((), ())), preferred_element_type=jnp.float32
-        ) * scale
+        s = jnp.dot(q, k.T, preferred_element_type=jnp.float32) * scale
         if b == 0:
+            row = lax.broadcasted_iota(jnp.int32, (n, span), 0) % span
+            col = lax.broadcasted_iota(jnp.int32, (n, span), 1)
             s = jnp.where((col <= row) | (key_spans[idx] < query_span), s, -jnp.inf)
-        return s
+        s_ref[idx] = s
+        if first:
+            mx_ref[...] = s
+        else:
+            mx_ref[...] = jnp.maximum(mx_ref[...], s)
 
-    mx_ref[...] = scores(0, 0, 0)
-
-    def widen(idx, b, t):
-        mx_ref[...] = jnp.maximum(mx_ref[...], scores(idx, b, t))
-
+    score(0, 0, 0, True)
     for idx, (b, t) in enumerate(tiles[1:], start=1):
-        pl.when(key_spans[idx] <= query_span)(functools.partial(widen, idx, b, t))
+        pl.when(key_spans[idx] <= query_span)(functools.partial(score, idx, b, t, False))
 
     m = jnp.max(mx_ref[...], axis=1, keepdims=True)
     mx_ref[...] = jnp.broadcast_to(m, (n, span))
 
     def weigh(idx, b, t, first):
-        p = jnp.exp(scores(idx, b, t) - mx_ref[...])
+        p = jnp.exp(s_ref[idx] - mx_ref[...])
         v = kv_refs[b][1, t * span : (t + 1) * span, :]
         out = jnp.dot(p.astype(jnp.bfloat16), v, preferred_element_type=jnp.float32)
         if first:
@@ -100,6 +98,7 @@
             in_specs=[q_spec] + [kv_spec] * steps,
             out_specs=o_spec,
             scratch_shapes=[
+                pltpu.VMEM((2 * steps, group * span, span), jnp.float32),
                 pltpu.VMEM((group * span, span), jnp.float32),
                 pltpu.VMEM((group * span, span), jnp.float32),
                 pltpu.VMEM((group * span, head_size), jnp.float32),

time: 98.8 us -> 81.6 us (0.83)
  the two profiles are of different devices: /device:TPU:4 before, /device:TPU:260 now
where the time goes in v7:
time: 81.6 us; the launch traced here: 81.1 us
  Pallas kernels  27.5 us (34%)
  starting transfers between devices  24.7 us (30%)
  waiting for transfers between devices  20.2 us (25%)
  local copies, waits for them, and re-layouts  7.47 us (9%)
  other arithmetic  1.17 us (1%)
    pallas_call x3, Pallas kernels, attend_half(): pl.pallas_call(kernel, out_shape=jax.ShapeDtypeStruct((span, out_cols), j...  27.5 us
    ppermute x4, starting transfers between devices, shifted(): return lax.ppermute(value, axis, pairs)  22.7 us
    ppermute x4, waiting for transfers between devices, shifted(): return lax.ppermute(value, axis, pairs)  20.2 us
    unnamed x9, local copies, waits for them, and re-layouts  4.57 us
    ppermute x1, starting transfers between devices, body(): lax.ppermute(jnp.where(myself % 2 == 0, first, third), 'ctx', pairs)  1.92 us
    dynamic_update_slice x2, local copies, waits for them, and re-layouts, body(): lax.dynamic_update_slice(out, arrived[j], (0, (1 - half) * width + j * pe...  1.65 us
  transfers between devices with their start and end apart: 5, of which 2 were waited for; matrix products, arithmetic and copies ran while one was open for 7% of the time, Pallas kernels for 29%

profile of v7, /device:TPU:260, one launch (start us, length us, event | category | flops | bytes accessed | tf_op | source)
XLA Modules:
  0.0 81.1 jit_solution(3598938945030176481)
XLA Ops:
  0.0 1.2 %reshape.3.refs_0_ = bf16[2,256,512]{2,1,0:T(8,128)(2,1)S(1)} reshape(bf16[2,256,4,128]{3,2,1,0:T(4,128)(2,1)} %param.4) | data formatting | bytes 1048576 | tf_op jit(solution)/shard_map/reshape | solution.py:129
  1.2 0.0 copy-start
  1.3 2.5 %collective-permute-start.1 = (bf16[2,256,512]{2,1,0:T(8,128)(2,1)S(1)}, bf16[2,256,512]{2,1,0:T(8,128)(2,1)S(1)}, u32[]{:S(2)}, u32[]{:S(2)}) collective-permute-start(bf16[2,256,512]{2,1,0:T(8,128)(2,1)S(1)} %reshape.3.refs_0_), channel_id=1, source_target_pairs={{0,6},{2,8},{4,10},{6,12},{8,14},{10,16},{12,18},{14,20},{16,22},{... | collective-permute-start | bytes 1572872 | tf_op jit(solution)/shard_map/ppermute | solution.py:16
  3.8 3.0 %collective-permute-start = (bf16[2,256,512]{2,1,0:T(8,128)(2,1)S(1)}, bf16[2,256,512]{2,1,0:T(8,128)(2,1)S(1)}, u32[]{:S(2)}, u32[]{:S(2)}) collective-permute-start(bf16[2,256,512]{2,1,0:T(8,128)(2,1)S(1)} %reshape.3.refs_0_), channel_id=1, source_target_pairs={{0,2},{2,4},{4,6},{6,8},{8,10},{10,12},{12,14},{14,16},{16,18},{18... | collective-permute-start | bytes 1572872 | tf_op jit(solution)/shard_map/ppermute | solution.py:16
  6.8 8.3 %collective-permute-done.1.refs_3_ = bf16[2,256,512]{2,1,0:T(8,128)(2,1)S(1)} collective-permute-done((bf16[2,256,512]{2,1,0:T(8,128)(2,1)S(1)}, bf16[2,256,512]{2,1,0:T(8,128)(2,1)S(1)}, u32[]{:S(2)}, u32[]{:S(2)}) %collective-permute-start.1) | collective-permute-done | bytes 524320 | tf_op jit(solution)/shard_map/ppermute | solution.py:16
  15.1 11.9 %collective-permute-done.refs_1_ = bf16[2,256,512]{2,1,0:T(8,128)(2,1)S(1)} collective-permute-done((bf16[2,256,512]{2,1,0:T(8,128)(2,1)S(1)}, bf16[2,256,512]{2,1,0:T(8,128)(2,1)S(1)}, u32[]{:S(2)}, u32[]{:S(2)}) %collective-permute-start) | collective-permute-done | bytes 524320 | tf_op jit(solution)/shard_map/ppermute | solution.py:16
  26.9 0.1 broadcast_select_fusion
  27.0 1.9 %collective-permute-start.2 = (bf16[2,256,512]{2,1,0:T(8,128)(2,1)S(1)}, bf16[2,256,512]{2,1,0:T(8,128)(2,1)S(1)}, u32[]{:S(2)}, u32[]{:S(2)}) collective-permute-start(bf16[2,256,512]{2,1,0:T(8,128)(2,1)S(1)} %broadcast_select_fusion), channel_id=1, source_target_pairs={{0,2},{2,0},{4,6},{6,4},{8,10},{10,8},{12,14},{14,12},{16,18},{18,... | collective-permute-start | bytes 1572872 | tf_op jit(solution)/shard_map/ppermute | solution.py:133
  28.9 3.7 %copy.6 = bf16[256,32,128]{2,0,1:T(8,128)(2,1)} copy(bf16[256,32,128]{2,1,0:T(8,128)(2,1)} %param.3) | data formatting | bytes 4194304 | tf_op args[0]
  32.7 0.0 copy-done
  32.7 0.0 copy-done.1
  32.7 0.5 compare_select_fusion.where_ref
  33.2 0.0 collective-permute-done.2.refs_2_
  33.2 0.8 %copy-done.3 = bf16[2,256,512]{2,1,0:T(8,128)(2,1)} copy-done((bf16[2,256,512]{2,1,0:T(8,128)(2,1)}, bf16[2,256,512]{2,1,0:T(8,128)(2,1)S(1)}, u32[]{:S(2)}) %copy-start.3) | copy-done | bytes 524312
  34.0 4.4 %shard_map.38 = bf16[128,2048]{1,0:T(8,128)(2,1)} custom-call(s32[512]{0:T(512)} %table_ref.5, s32[2]{0:T(128)} %compare_select_fusion.where_ref, bf16[32,256,128]{2,1,0:T(8,128)(2,1)} %bitcast.3, bf16[2,256,512]{2,1,0:T(8,128)(2,1)} %copy-done, bf16[2,256,512]{2,1,0:T(8,128)(2,1)} %copy-done.2, bf16[2,256,512]{2,1,0:T(8,128)(2,1)} %copy-done.3, ...), custom_call_target="tpu_custom_call" | custom-call | flops 1073741824 | bytes 2097152 | tf_op jit(solution)/shard_map/pallas_call | solution.py:92
  38.4 9.0 %collective-permute-start.3 = (bf16[128,2048]{1,0:T(8,128)(2,1)}, bf16[128,2048]{1,0:T(8,128)(2,1)S(1)}, u32[]{:S(2)}, u32[]{:S(2)}) collective-permute-start(bf16[128,2048]{1,0:T(8,128)(2,1)} %shard_map.38), channel_id=1, source_target_pairs={{0,1},{1,0},{2,3},{3,2},{4,5},{5,4},{6,7},{7,6},{8,9},{9,8},{10,11... | collective-permute-start | bytes 1572872 | tf_op jit(solution)/shard_map/ppermute | solution.py:16
  47.4 4.4 %shard_map.39 = bf16[128,2048]{1,0:T(8,128)(2,1)} custom-call(s32[512]{0:T(512)} %table_ref.5, s32[2]{0:T(128)} %compare_select_fusion.where_ref, bf16[32,256,128]{2,1,0:T(8,128)(2,1)} %bitcast.4, bf16[2,256,512]{2,1,0:T(8,128)(2,1)} %copy-done, bf16[2,256,512]{2,1,0:T(8,128)(2,1)} %copy-done.2, bf16[2,256,512]{2,1,0:T(8,128)(2,1)} %copy-done.3, ...), custom_call_target="tpu_custom_call" | custom-call | flops 1073741824 | bytes 2097152 | tf_op jit(solution)/shard_map/pallas_call | solution.py:92
  51.8 8.2 %collective-permute-start.4 = (bf16[128,2048]{1,0:T(8,128)(2,1)}, bf16[128,2048]{1,0:T(8,128)(2,1)S(1)}, u32[]{:S(2)}, u32[]{:S(2)}) collective-permute-start(bf16[128,2048]{1,0:T(8,128)(2,1)} %shard_map.39), channel_id=1, source_target_pairs={{0,1},{1,0},{2,3},{3,2},{4,5},{5,4},{6,7},{7,6},{8,9},{9,8},{10,11... | collective-permute-start | bytes 1572872 | tf_op jit(solution)/shard_map/ppermute | solution.py:16
  60.0 0.6 compare_select_fusion.1.where_ref
  60.6 18.8 %shard_map.37 = bf16[128,8192]{1,0:T(8,128)(2,1)} custom-call(s32[512]{0:T(512)} %table_ref.5, s32[2]{0:T(128)} %compare_select_fusion.1.where_ref, bf16[32,256,128]{2,1,0:T(8,128)(2,1)} %bitcast.5, bf16[2,256,512]{2,1,0:T(8,128)(2,1)} %copy-done, bf16[2,256,512]{2,1,0:T(8,128)(2,1)} %copy-done.2, bf16[2,256,512]{2,1,0:T(8,128)(2,1)} %copy-done.3, ...), custom_call_target="tpu_custom_call" | custom-call | flops 2147483648 | bytes 4194304 | tf_op jit(solution)/shard_map/pallas_call | solution.py:92
  79.4 0.0 collective-permute-done.3
  79.4 0.8 %constant_dynamic-update-slice_fusion.1 = bf16[128,8192]{1,0:T(8,128)(2,1)} fusion(bf16[128,8192]{1,0:T(8,128)(2,1)} %shard_map.37, bf16[128,2048]{1,0:T(8,128)(2,1)S(1)} %collective-permute-done.3, s32[]{:T(128)S(6)} %select_n.33), kind=kLoop, calls=%fused_computation.5 | loop fusion | bytes 1048580 | tf_op jit(solution)/shard_map/dynamic_update_slice | solution.py:155
  80.2 0.0 collective-permute-done.4
  80.2 0.8 %constant_dynamic-update-slice_fusion = bf16[128,8192]{1,0:T(8,128)(2,1)} fusion(bf16[128,8192]{1,0:T(8,128)(2,1)} %constant_dynamic-update-slice_fusion.1, bf16[128,2048]{1,0:T(8,128)(2,1)S(1)} %collective-permute-done.4, s32[]{:T(128)S(6)} %select_n.34), kind=kLoop, calls=%fused_computation.4 | loop fusion | bytes 1048580 | tf_op jit(solution)/shard_map/dynamic_update_slice | solution.py:155
  (4 shorter events, 0.0 us)
Async XLA Ops:
  1.2 31.4 %copy-start = (bf16[2,256,512]{2,1,0:T(8,128)(2,1)}, bf16[2,256,512]{2,1,0:T(8,128)(2,1)S(1)}, u32[]{:S(2)}) copy-start(bf16[2,256,512]{2,1,0:T(8,128)(2,1)S(1)} %reshape.3.refs_0_) | copy-start | bytes 1572868
  1.3 13.8 %collective-permute-start.1 = (bf16[2,256,512]{2,1,0:T(8,128)(2,1)S(1)}, bf16[2,256,512]{2,1,0:T(8,128)(2,1)S(1)}, u32[]{:S(2)}, u32[]{:S(2)}) collective-permute-start(bf16[2,256,512]{2,1,0:T(8,128)(2,1)S(1)} %reshape.3.refs_0_), channel_id=1, source_target_pairs={{0,6},{2,8},{4,10},{6,12},{8,14},{10,16},{12,18},{14,20},{16,22},{... | collective-permute-start | bytes 1572872 | tf_op jit(solution)/shard_map/ppermute | solution.py:16
  3.8 23.1 %collective-permute-start = (bf16[2,256,512]{2,1,0:T(8,128)(2,1)S(1)}, bf16[2,256,512]{2,1,0:T(8,128)(2,1)S(1)}, u32[]{:S(2)}, u32[]{:S(2)}) collective-permute-start(bf16[2,256,512]{2,1,0:T(8,128)(2,1)S(1)} %reshape.3.refs_0_), channel_id=1, source_target_pairs={{0,2},{2,4},{4,6},{6,8},{8,10},{10,12},{12,14},{14,16},{16,18},{18... | collective-permute-start | bytes 1572872 | tf_op jit(solution)/shard_map/ppermute | solution.py:16
  15.1 17.6 %copy-start.1 = (bf16[2,256,512]{2,1,0:T(8,128)(2,1)}, bf16[2,256,512]{2,1,0:T(8,128)(2,1)S(1)}, u32[]{:S(2)}) copy-start(bf16[2,256,512]{2,1,0:T(8,128)(2,1)S(1)} %collective-permute-done.1.refs_3_) | copy-start | bytes 1572868
  26.9 5.8 %copy-start.2 = (bf16[2,256,512]{2,1,0:T(8,128)(2,1)}, bf16[2,256,512]{2,1,0:T(8,128)(2,1)S(1)}, u32[]{:S(2)}) copy-start(bf16[2,256,512]{2,1,0:T(8,128)(2,1)S(1)} %collective-permute-done.refs_1_) | copy-start | bytes 1572868
  27.0 6.2 %collective-permute-start.2 = (bf16[2,256,512]{2,1,0:T(8,128)(2,1)S(1)}, bf16[2,256,512]{2,1,0:T(8,128)(2,1)S(1)}, u32[]{:S(2)}, u32[]{:S(2)}) collective-permute-start(bf16[2,256,512]{2,1,0:T(8,128)(2,1)S(1)} %broadcast_select_fusion), channel_id=1, source_target_pairs={{0,2},{2,0},{4,6},{6,4},{8,10},{10,8},{12,14},{14,12},{16,18},{18,... | collective-permute-start | bytes 1572872 | tf_op jit(solution)/shard_map/ppermute | solution.py:133
  33.2 0.8 %copy-start.3 = (bf16[2,256,512]{2,1,0:T(8,128)(2,1)}, bf16[2,256,512]{2,1,0:T(8,128)(2,1)S(1)}, u32[]{:S(2)}) copy-start(bf16[2,256,512]{2,1,0:T(8,128)(2,1)S(1)} %collective-permute-done.2.refs_2_) | copy-start | bytes 1572868
  38.4 41.0 %collective-permute-start.3 = (bf16[128,2048]{1,0:T(8,128)(2,1)}, bf16[128,2048]{1,0:T(8,128)(2,1)S(1)}, u32[]{:S(2)}, u32[]{:S(2)}) collective-permute-start(bf16[128,2048]{1,0:T(8,128)(2,1)} %shard_map.38), channel_id=1, source_target_pairs={{0,1},{1,0},{2,3},{3,2},{4,5},{5,4},{6,7},{7,6},{8,9},{9,8},{10,11... | collective-permute-start | bytes 1572872 | tf_op jit(solution)/shard_map/ppermute | solution.py:16
  51.8 28.4 %collective-permute-start.4 = (bf16[128,2048]{1,0:T(8,128)(2,1)}, bf16[128,2048]{1,0:T(8,128)(2,1)S(1)}, u32[]{:S(2)}, u32[]{:S(2)}) collective-permute-start(bf16[128,2048]{1,0:T(8,128)(2,1)} %shard_map.39), channel_id=1, source_target_pairs={{0,1},{1,0},{2,3},{3,2},{4,5},{5,4},{6,7},{7,6},{8,9},{9,8},{10,11... | collective-permute-start | bytes 1572872 | tf_op jit(solution)/shard_map/ppermute | solution.py:16

commit v8 on v7

--- a/solution.py
+++ b/solution.py
@@ -129,6 +129,7 @@
     own = key_value.reshape(2, rows, kv_here * head_size)
     first = shifted(own, "ctx", 1)
     third = shifted(own, "ctx", 3)
+    first, third, q2 = lax.optimization_barrier((first, third, q2))
     pairs = [(d, d ^ 1) for d in range(cycle)]
     second = lax.ppermute(jnp.where(myself % 2 == 0, first, third), "ctx", pairs)
     blocks = [own, first, second, third]

time: 81.6 us -> 85.5 us (1.048)
  the two profiles are of different devices: /device:TPU:260 before, /device:TPU:7 now
where the time goes in v8:
time: 85.5 us; the launch traced here: 85 us
  starting transfers between devices  36.1 us (42%)
  Pallas kernels  27.5 us (32%)
  waiting for transfers between devices  12.6 us (15%)
  local copies, waits for them, and re-layouts  7.47 us (9%)
  other arithmetic  1.17 us (1%)
    pallas_call x3, Pallas kernels, attend_half(): pl.pallas_call(kernel, out_shape=jax.ShapeDtypeStruct((span, out_cols), j...  27.5 us
    ppermute x4, starting transfers between devices, shifted(): return lax.ppermute(value, axis, pairs)  23.5 us
    ppermute x1, starting transfers between devices, body(): lax.ppermute(jnp.where(myself % 2 == 0, first, third), 'ctx', pairs)  12.6 us
    ppermute x4, waiting for transfers between devices, shifted(): return lax.ppermute(value, axis, pairs)  11.6 us
    unnamed x9, local copies, waits for them, and re-layouts  4.57 us
  transfers between devices with their start and end apart: 5, of which 3 were waited for; matrix products, arithmetic and copies ran while one was open for 7% of the time, Pallas kernels for 27%

profile of v8, /device:TPU:7, one launch (start us, length us, event | category | flops | bytes accessed | tf_op | source)
XLA Modules:
  0.0 85.0 jit_solution(2661733413302983339)
XLA Ops:
  0.0 1.2 %reshape.3.refs_0_ = bf16[2,256,512]{2,1,0:T(8,128)(2,1)S(1)} reshape(bf16[2,256,4,128]{3,2,1,0:T(4,128)(2,1)} %param.4) | data formatting | bytes 1048576 | tf_op jit(solution)/shard_map/reshape | solution.py:129
  1.2 0.0 copy-start
  1.3 4.0 %collective-permute-start = (bf16[2,256,512]{2,1,0:T(8,128)(2,1)S(1)}, bf16[2,256,512]{2,1,0:T(8,128)(2,1)S(1)}, u32[]{:S(2)}, u32[]{:S(2)}) collective-permute-start(bf16[2,256,512]{2,1,0:T(8,128)(2,1)S(1)} %reshape.3.refs_0_), channel_id=1, source_target_pairs={{0,2},{2,4},{4,6},{6,8},{8,10},{10,12},{12,14},{14,16},{16,18},{18... | collective-permute-start | bytes 1572872 | tf_op jit(solution)/shard_map/ppermute | solution.py:16
  5.3 1.9 %collective-permute-start.1 = (bf16[2,256,512]{2,1,0:T(8,128)(2,1)S(1)}, bf16[2,256,512]{2,1,0:T(8,128)(2,1)S(1)}, u32[]{:S(2)}, u32[]{:S(2)}) collective-permute-start(bf16[2,256,512]{2,1,0:T(8,128)(2,1)S(1)} %reshape.3.refs_0_), channel_id=1, source_target_pairs={{0,6},{2,8},{4,10},{6,12},{8,14},{10,16},{12,18},{14,20},{16,22},{... | collective-permute-start | bytes 1572872 | tf_op jit(solution)/shard_map/ppermute | solution.py:16
  7.2 3.7 %copy.6 = bf16[256,32,128]{2,0,1:T(8,128)(2,1)} copy(bf16[256,32,128]{2,1,0:T(8,128)(2,1)} %param.3) | data formatting | bytes 4194304 | tf_op args[0]
  11.0 0.0 copy-done
  11.0 2.5 %collective-permute-done.refs_1_ = bf16[2,256,512]{2,1,0:T(8,128)(2,1)S(1)} collective-permute-done((bf16[2,256,512]{2,1,0:T(8,128)(2,1)S(1)}, bf16[2,256,512]{2,1,0:T(8,128)(2,1)S(1)}, u32[]{:S(2)}, u32[]{:S(2)}) %collective-permute-start) | collective-permute-done | bytes 524320 | tf_op jit(solution)/shard_map/ppermute | solution.py:16
  13.5 9.1 %collective-permute-done.1.refs_3_ = bf16[2,256,512]{2,1,0:T(8,128)(2,1)S(1)} collective-permute-done((bf16[2,256,512]{2,1,0:T(8,128)(2,1)S(1)}, bf16[2,256,512]{2,1,0:T(8,128)(2,1)S(1)}, u32[]{:S(2)}, u32[]{:S(2)}) %collective-permute-start.1) | collective-permute-done | bytes 524320 | tf_op jit(solution)/shard_map/ppermute | solution.py:16
  22.6 0.1 broadcast_select_fusion
  22.7 12.6 %collective-permute-start.2 = (bf16[2,256,512]{2,1,0:T(8,128)(2,1)S(1)}, bf16[2,256,512]{2,1,0:T(8,128)(2,1)S(1)}, u32[]{:S(2)}, u32[]{:S(2)}) collective-permute-start(bf16[2,256,512]{2,1,0:T(8,128)(2,1)S(1)} %broadcast_select_fusion), channel_id=1, source_target_pairs={{0,2},{2,0},{4,6},{6,4},{8,10},{10,8},{12,14},{14,12},{16,18},{18,... | collective-permute-start | bytes 1572872 | tf_op jit(solution)/shard_map/ppermute | solution.py:134
  35.3 0.5 compare_select_fusion.where_ref
  35.8 1.0 %collective-permute-done.2.refs_2_ = bf16[2,256,512]{2,1,0:T(8,128)(2,1)S(1)} collective-permute-done((bf16[2,256,512]{2,1,0:T(8,128)(2,1)S(1)}, bf16[2,256,512]{2,1,0:T(8,128)(2,1)S(1)}, u32[]{:S(2)}, u32[]{:S(2)}) %collective-permute-start.2) | collective-permute-done | bytes 524320 | tf_op jit(solution)/shard_map/ppermute | solution.py:134
  36.8 0.0 copy-done.1
  36.8 0.8 copy-done.3
  37.6 4.4 %shard_map.38 = bf16[128,2048]{1,0:T(8,128)(2,1)} custom-call(s32[512]{0:T(512)} %table_ref.5, s32[2]{0:T(128)} %compare_select_fusion.where_ref, bf16[32,256,128]{2,1,0:T(8,128)(2,1)} %bitcast.3, bf16[2,256,512]{2,1,0:T(8,128)(2,1)} %copy-done, bf16[2,256,512]{2,1,0:T(8,128)(2,1)} %copy-done.1, bf16[2,256,512]{2,1,0:T(8,128)(2,1)} %copy-done.3, ...), custom_call_target="tpu_custom_call" | custom-call | flops 1073741824 | bytes 2097152 | tf_op jit(solution)/shard_map/pallas_call | solution.py:92
  42.0 9.3 %collective-permute-start.3 = (bf16[128,2048]{1,0:T(8,128)(2,1)}, bf16[128,2048]{1,0:T(8,128)(2,1)S(1)}, u32[]{:S(2)}, u32[]{:S(2)}) collective-permute-start(bf16[128,2048]{1,0:T(8,128)(2,1)} %shard_map.38), channel_id=1, source_target_pairs={{0,1},{1,0},{2,3},{3,2},{4,5},{5,4},{6,7},{7,6},{8,9},{9,8},{10,11... | collective-permute-start | bytes 1572872 | tf_op jit(solution)/shard_map/ppermute | solution.py:16
  51.4 4.4 %shard_map.39 = bf16[128,2048]{1,0:T(8,128)(2,1)} custom-call(s32[512]{0:T(512)} %table_ref.5, s32[2]{0:T(128)} %compare_select_fusion.where_ref, bf16[32,256,128]{2,1,0:T(8,128)(2,1)} %bitcast.4, bf16[2,256,512]{2,1,0:T(8,128)(2,1)} %copy-done, bf16[2,256,512]{2,1,0:T(8,128)(2,1)} %copy-done.1, bf16[2,256,512]{2,1,0:T(8,128)(2,1)} %copy-done.3, ...), custom_call_target="tpu_custom_call" | custom-call | flops 1073741824 | bytes 2097152 | tf_op jit(solution)/shard_map/pallas_call | solution.py:92
  55.7 8.2 %collective-permute-start.4 = (bf16[128,2048]{1,0:T(8,128)(2,1)}, bf16[128,2048]{1,0:T(8,128)(2,1)S(1)}, u32[]{:S(2)}, u32[]{:S(2)}) collective-permute-start(bf16[128,2048]{1,0:T(8,128)(2,1)} %shard_map.39), channel_id=1, source_target_pairs={{0,1},{1,0},{2,3},{3,2},{4,5},{5,4},{6,7},{7,6},{8,9},{9,8},{10,11... | collective-permute-start | bytes 1572872 | tf_op jit(solution)/shard_map/ppermute | solution.py:16
  63.9 0.6 compare_select_fusion.1.where_ref
  64.5 18.8 %shard_map.37 = bf16[128,8192]{1,0:T(8,128)(2,1)} custom-call(s32[512]{0:T(512)} %table_ref.5, s32[2]{0:T(128)} %compare_select_fusion.1.where_ref, bf16[32,256,128]{2,1,0:T(8,128)(2,1)} %bitcast.5, bf16[2,256,512]{2,1,0:T(8,128)(2,1)} %copy-done, bf16[2,256,512]{2,1,0:T(8,128)(2,1)} %copy-done.1, bf16[2,256,512]{2,1,0:T(8,128)(2,1)} %copy-done.3, ...), custom_call_target="tpu_custom_call" | custom-call | flops 2147483648 | bytes 4194304 | tf_op jit(solution)/shard_map/pallas_call | solution.py:92
  83.3 0.0 collective-permute-done.3
  83.4 0.8 constant_dynamic-update-slice_fusion.1
  84.2 0.0 collective-permute-done.4
  84.2 0.8 constant_dynamic-update-slice_fusion
  (4 shorter events, 0.0 us)
Async XLA Ops:
  1.2 9.7 %copy-start = (bf16[2,256,512]{2,1,0:T(8,128)(2,1)}, bf16[2,256,512]{2,1,0:T(8,128)(2,1)S(1)}, u32[]{:S(2)}) copy-start(bf16[2,256,512]{2,1,0:T(8,128)(2,1)S(1)} %reshape.3.refs_0_) | copy-start | bytes 1572868
  1.3 12.3 %collective-permute-start = (bf16[2,256,512]{2,1,0:T(8,128)(2,1)S(1)}, bf16[2,256,512]{2,1,0:T(8,128)(2,1)S(1)}, u32[]{:S(2)}, u32[]{:S(2)}) collective-permute-start(bf16[2,256,512]{2,1,0:T(8,128)(2,1)S(1)} %reshape.3.refs_0_), channel_id=1, source_target_pairs={{0,2},{2,4},{4,6},{6,8},{8,10},{10,12},{12,14},{14,16},{16,18},{18... | collective-permute-start | bytes 1572872 | tf_op jit(solution)/shard_map/ppermute | solution.py:16
  5.3 17.3 %collective-permute-start.1 = (bf16[2,256,512]{2,1,0:T(8,128)(2,1)S(1)}, bf16[2,256,512]{2,1,0:T(8,128)(2,1)S(1)}, u32[]{:S(2)}, u32[]{:S(2)}) collective-permute-start(bf16[2,256,512]{2,1,0:T(8,128)(2,1)S(1)} %reshape.3.refs_0_), channel_id=1, source_target_pairs={{0,6},{2,8},{4,10},{6,12},{8,14},{10,16},{12,18},{14,20},{16,22},{... | collective-permute-start | bytes 1572872 | tf_op jit(solution)/shard_map/ppermute | solution.py:16
  13.5 23.3 %copy-start.1 = (bf16[2,256,512]{2,1,0:T(8,128)(2,1)}, bf16[2,256,512]{2,1,0:T(8,128)(2,1)S(1)}, u32[]{:S(2)}) copy-start(bf16[2,256,512]{2,1,0:T(8,128)(2,1)S(1)} %collective-permute-done.refs_1_) | copy-start | bytes 1572868
  22.6 14.2 %copy-start.2 = (bf16[2,256,512]{2,1,0:T(8,128)(2,1)}, bf16[2,256,512]{2,1,0:T(8,128)(2,1)S(1)}, u32[]{:S(2)}) copy-start(bf16[2,256,512]{2,1,0:T(8,128)(2,1)S(1)} %collective-permute-done.1.refs_3_) | copy-start | bytes 1572868
  22.7 14.1 %collective-permute-start.2 = (bf16[2,256,512]{2,1,0:T(8,128)(2,1)S(1)}, bf16[2,256,512]{2,1,0:T(8,128)(2,1)S(1)}, u32[]{:S(2)}, u32[]{:S(2)}) collective-permute-start(bf16[2,256,512]{2,1,0:T(8,128)(2,1)S(1)} %broadcast_select_fusion), channel_id=1, source_target_pairs={{0,2},{2,0},{4,6},{6,4},{8,10},{10,8},{12,14},{14,12},{16,18},{18,... | collective-permute-start | bytes 1572872 | tf_op jit(solution)/shard_map/ppermute | solution.py:134
  36.8 0.8 copy-start.3
  42.0 41.4 %collective-permute-start.3 = (bf16[128,2048]{1,0:T(8,128)(2,1)}, bf16[128,2048]{1,0:T(8,128)(2,1)S(1)}, u32[]{:S(2)}, u32[]{:S(2)}) collective-permute-start(bf16[128,2048]{1,0:T(8,128)(2,1)} %shard_map.38), channel_id=1, source_target_pairs={{0,1},{1,0},{2,3},{3,2},{4,5},{5,4},{6,7},{7,6},{8,9},{9,8},{10,11... | collective-permute-start | bytes 1572872 | tf_op jit(solution)/shard_map/ppermute | solution.py:16
  55.7 28.5 %collective-permute-start.4 = (bf16[128,2048]{1,0:T(8,128)(2,1)}, bf16[128,2048]{1,0:T(8,128)(2,1)S(1)}, u32[]{:S(2)}, u32[]{:S(2)}) collective-permute-start(bf16[128,2048]{1,0:T(8,128)(2,1)} %shard_map.39), channel_id=1, source_target_pairs={{0,1},{1,0},{2,3},{3,2},{4,5},{5,4},{6,7},{7,6},{8,9},{9,8},{10,11... | collective-permute-start | bytes 1572872 | tf_op jit(solution)/shard_map/ppermute | solution.py:16

commit v9 on v7

--- a/solution.py
+++ b/solution.py
@@ -129,14 +129,17 @@
     own = key_value.reshape(2, rows, kv_here * head_size)
     first = shifted(own, "ctx", 1)
     third = shifted(own, "ctx", 3)
-    pairs = [(d, d ^ 1) for d in range(cycle)]
-    second = lax.ppermute(jnp.where(myself % 2 == 0, first, third), "ctx", pairs)
-    blocks = [own, first, second, third]
 
     width = heads_here * head_size
     lanes = jnp.arange(2, dtype=jnp.int32)
     sent_where = jnp.where(lanes == 0, 1 - half, myself).astype(jnp.int32)
     kept_where = jnp.where(lanes == 0, half, myself).astype(jnp.int32)
+    first, third, q2, sent_where, kept_where = lax.optimization_barrier(
+        (first, third, q2, sent_where, kept_where)
+    )
+    pairs = [(d, d ^ 1) for d in range(cycle)]
+    second = lax.ppermute(jnp.where(myself % 2 == 0, first, third), "ctx", pairs)
+    blocks = [own, first, second, third]
     common = dict(span=span, group=group, head_size=head_size)
     chunks = 2
     per = kv_here // chunks

time: 81.6 us -> 84.9 us (1.040)
  the two profiles are of different devices: /device:TPU:260 before, /device:TPU:7 now
where the time goes in v9:
time: 84.9 us; the launch traced here: 84.4 us
  starting transfers between devices  34.3 us (40%)
  Pallas kernels  29.3 us (35%)
  waiting for transfers between devices  12.6 us (15%)
  local copies, waits for them, and re-layouts  7.46 us (9%)
    pallas_call x3, Pallas kernels, attend_half(): pl.pallas_call(kernel, out_shape=jax.ShapeDtypeStruct((span, out_cols), j...  29.3 us
    ppermute x4, starting transfers between devices, shifted(): return lax.ppermute(value, axis, pairs)  21.7 us
    ppermute x1, starting transfers between devices, body(): lax.ppermute(jnp.where(myself % 2 == 0, first, third), 'ctx', pairs)  12.6 us
    ppermute x4, waiting for transfers between devices, shifted(): return lax.ppermute(value, axis, pairs)  11.1 us
    unnamed x9, local copies, waits for them, and re-layouts  4.55 us
  transfers between devices with their start and end apart: 5, of which 3 were waited for; matrix products, arithmetic and copies ran while one was open for 6% of the time, Pallas kernels for 28%

profile of v9, /device:TPU:7, one launch (start us, length us, event | category | flops | bytes accessed | tf_op | source)
XLA Modules:
  0.0 84.4 jit_solution(4999404624172661977)
XLA Ops:
  0.0 1.2 %reshape.3.refs_0_ = bf16[2,256,512]{2,1,0:T(8,128)(2,1)S(1)} reshape(bf16[2,256,4,128]{3,2,1,0:T(4,128)(2,1)} %param.4) | data formatting | bytes 1048576 | tf_op jit(solution)/shard_map/reshape | solution.py:129
  1.2 0.0 copy-start
  1.3 4.0 %collective-permute-start = (bf16[2,256,512]{2,1,0:T(8,128)(2,1)S(1)}, bf16[2,256,512]{2,1,0:T(8,128)(2,1)S(1)}, u32[]{:S(2)}, u32[]{:S(2)}) collective-permute-start(bf16[2,256,512]{2,1,0:T(8,128)(2,1)S(1)} %reshape.3.refs_0_), channel_id=1, source_target_pairs={{0,2},{2,4},{4,6},{6,8},{8,10},{10,12},{12,14},{14,16},{16,18},{18... | collective-permute-start | bytes 1572872 | tf_op jit(solution)/shard_map/ppermute | solution.py:16
  5.3 1.9 %collective-permute-start.1 = (bf16[2,256,512]{2,1,0:T(8,128)(2,1)S(1)}, bf16[2,256,512]{2,1,0:T(8,128)(2,1)S(1)}, u32[]{:S(2)}, u32[]{:S(2)}) collective-permute-start(bf16[2,256,512]{2,1,0:T(8,128)(2,1)S(1)} %reshape.3.refs_0_), channel_id=1, source_target_pairs={{0,6},{2,8},{4,10},{6,12},{8,14},{10,16},{12,18},{14,20},{16,22},{... | collective-permute-start | bytes 1572872 | tf_op jit(solution)/shard_map/ppermute | solution.py:16
  7.2 3.7 %copy.6 = bf16[256,32,128]{2,0,1:T(8,128)(2,1)} copy(bf16[256,32,128]{2,1,0:T(8,128)(2,1)} %param.3) | data formatting | bytes 4194304 | tf_op args[0]
  11.0 0.0 copy-done
  11.0 0.5 compare_select_fusion
  11.5 2.0 %collective-permute-done.refs_1_ = bf16[2,256,512]{2,1,0:T(8,128)(2,1)S(1)} collective-permute-done((bf16[2,256,512]{2,1,0:T(8,128)(2,1)S(1)}, bf16[2,256,512]{2,1,0:T(8,128)(2,1)S(1)}, u32[]{:S(2)}, u32[]{:S(2)}) %collective-permute-start) | collective-permute-done | bytes 524320 | tf_op jit(solution)/shard_map/ppermute | solution.py:16
  13.5 9.1 %collective-permute-done.1.refs_3_ = bf16[2,256,512]{2,1,0:T(8,128)(2,1)S(1)} collective-permute-done((bf16[2,256,512]{2,1,0:T(8,128)(2,1)S(1)}, bf16[2,256,512]{2,1,0:T(8,128)(2,1)S(1)}, u32[]{:S(2)}, u32[]{:S(2)}) %collective-permute-start.1) | collective-permute-done | bytes 524320 | tf_op jit(solution)/shard_map/ppermute | solution.py:16
  22.6 0.1 broadcast_select_fusion
  22.7 12.6 %collective-permute-start.2 = (bf16[2,256,512]{2,1,0:T(8,128)(2,1)S(1)}, bf16[2,256,512]{2,1,0:T(8,128)(2,1)S(1)}, u32[]{:S(2)}, u32[]{:S(2)}) collective-permute-start(bf16[2,256,512]{2,1,0:T(8,128)(2,1)S(1)} %broadcast_select_fusion), channel_id=1, source_target_pairs={{0,2},{2,0},{4,6},{6,4},{8,10},{10,8},{12,14},{14,12},{16,18},{18,... | collective-permute-start | bytes 1572872 | tf_op jit(solution)/shard_map/ppermute | solution.py:141
  35.3 1.5 %collective-permute-done.2.refs_2_ = bf16[2,256,512]{2,1,0:T(8,128)(2,1)S(1)} collective-permute-done((bf16[2,256,512]{2,1,0:T(8,128)(2,1)S(1)}, bf16[2,256,512]{2,1,0:T(8,128)(2,1)S(1)}, u32[]{:S(2)}, u32[]{:S(2)}) %collective-permute-start.2) | collective-permute-done | bytes 524320 | tf_op jit(solution)/shard_map/ppermute | solution.py:141
  36.8 0.0 copy-done.1
  36.8 0.0 copy-done.2
  36.8 0.8 copy-done.3
  37.6 5.3 %shard_map.38 = bf16[128,2048]{1,0:T(8,128)(2,1)} custom-call(s32[512]{0:T(512)} %table_ref.5, s32[2]{0:T(128)} %get-tuple-element.14.where_ref, bf16[32,256,128]{2,1,0:T(8,128)(2,1)} %bitcast.3, bf16[2,256,512]{2,1,0:T(8,128)(2,1)} %copy-done, bf16[2,256,512]{2,1,0:T(8,128)(2,1)} %copy-done.1, bf16[2,256,512]{2,1,0:T(8,128)(2,1)} %copy-done.3, ...), custom_call_target="tpu_custom_call" | custom-call | flops 1073741824 | bytes 2097152 | tf_op jit(solution)/shard_map/pallas_call | solution.py:92
  42.9 8.4 %collective-permute-start.3 = (bf16[128,2048]{1,0:T(8,128)(2,1)}, bf16[128,2048]{1,0:T(8,128)(2,1)S(1)}, u32[]{:S(2)}, u32[]{:S(2)}) collective-permute-start(bf16[128,2048]{1,0:T(8,128)(2,1)} %shard_map.38), channel_id=1, source_target_pairs={{0,1},{1,0},{2,3},{3,2},{4,5},{5,4},{6,7},{7,6},{8,9},{9,8},{10,11... | collective-permute-start | bytes 1572872 | tf_op jit(solution)/shard_map/ppermute | solution.py:16
  51.3 5.3 %shard_map.39 = bf16[128,2048]{1,0:T(8,128)(2,1)} custom-call(s32[512]{0:T(512)} %table_ref.5, s32[2]{0:T(128)} %get-tuple-element.14.where_ref, bf16[32,256,128]{2,1,0:T(8,128)(2,1)} %bitcast.4, bf16[2,256,512]{2,1,0:T(8,128)(2,1)} %copy-done, bf16[2,256,512]{2,1,0:T(8,128)(2,1)} %copy-done.1, bf16[2,256,512]{2,1,0:T(8,128)(2,1)} %copy-done.3, ...), custom_call_target="tpu_custom_call" | custom-call | flops 1073741824 | bytes 2097152 | tf_op jit(solution)/shard_map/pallas_call | solution.py:92
  56.6 7.3 %collective-permute-start.4 = (bf16[128,2048]{1,0:T(8,128)(2,1)}, bf16[128,2048]{1,0:T(8,128)(2,1)S(1)}, u32[]{:S(2)}, u32[]{:S(2)}) collective-permute-start(bf16[128,2048]{1,0:T(8,128)(2,1)} %shard_map.39), channel_id=1, source_target_pairs={{0,1},{1,0},{2,3},{3,2},{4,5},{5,4},{6,7},{7,6},{8,9},{9,8},{10,11... | collective-permute-start | bytes 1572872 | tf_op jit(solution)/shard_map/ppermute | solution.py:16
  63.9 18.8 %shard_map.37 = bf16[128,8192]{1,0:T(8,128)(2,1)} custom-call(s32[512]{0:T(512)} %table_ref.5, s32[2]{0:T(128)} %get-tuple-element.10.where_ref, bf16[32,256,128]{2,1,0:T(8,128)(2,1)} %bitcast.5, bf16[2,256,512]{2,1,0:T(8,128)(2,1)} %copy-done, bf16[2,256,512]{2,1,0:T(8,128)(2,1)} %copy-done.1, bf16[2,256,512]{2,1,0:T(8,128)(2,1)} %copy-done.3, ...), custom_call_target="tpu_custom_call" | custom-call | flops 2147483648 | bytes 4194304 | tf_op jit(solution)/shard_map/pallas_call | solution.py:92
  82.7 0.0 collective-permute-done.3
  82.7 0.8 constant_dynamic-update-slice_fusion.1
  83.5 0.0 collective-permute-done.4
  83.6 0.8 constant_dynamic-update-slice_fusion
  (3 shorter events, 0.0 us)
Async XLA Ops:
  1.2 9.7 %copy-start = (bf16[2,256,512]{2,1,0:T(8,128)(2,1)}, bf16[2,256,512]{2,1,0:T(8,128)(2,1)S(1)}, u32[]{:S(2)}) copy-start(bf16[2,256,512]{2,1,0:T(8,128)(2,1)S(1)} %reshape.3.refs_0_) | copy-start | bytes 1572868
  1.3 12.3 %collective-permute-start = (bf16[2,256,512]{2,1,0:T(8,128)(2,1)S(1)}, bf16[2,256,512]{2,1,0:T(8,128)(2,1)S(1)}, u32[]{:S(2)}, u32[]{:S(2)}) collective-permute-start(bf16[2,256,512]{2,1,0:T(8,128)(2,1)S(1)} %reshape.3.refs_0_), channel_id=1, source_target_pairs={{0,2},{2,4},{4,6},{6,8},{8,10},{10,12},{12,14},{14,16},{16,18},{18... | collective-permute-start | bytes 1572872 | tf_op jit(solution)/shard_map/ppermute | solution.py:16
  5.3 17.3 %collective-permute-start.1 = (bf16[2,256,512]{2,1,0:T(8,128)(2,1)S(1)}, bf16[2,256,512]{2,1,0:T(8,128)(2,1)S(1)}, u32[]{:S(2)}, u32[]{:S(2)}) collective-permute-start(bf16[2,256,512]{2,1,0:T(8,128)(2,1)S(1)} %reshape.3.refs_0_), channel_id=1, source_target_pairs={{0,6},{2,8},{4,10},{6,12},{8,14},{10,16},{12,18},{14,20},{16,22},{... | collective-permute-start | bytes 1572872 | tf_op jit(solution)/shard_map/ppermute | solution.py:16
  13.5 23.3 %copy-start.1 = (bf16[2,256,512]{2,1,0:T(8,128)(2,1)}, bf16[2,256,512]{2,1,0:T(8,128)(2,1)S(1)}, u32[]{:S(2)}) copy-start(bf16[2,256,512]{2,1,0:T(8,128)(2,1)S(1)} %collective-permute-done.refs_1_) | copy-start | bytes 1572868
  22.6 14.2 %copy-start.2 = (bf16[2,256,512]{2,1,0:T(8,128)(2,1)}, bf16[2,256,512]{2,1,0:T(8,128)(2,1)S(1)}, u32[]{:S(2)}) copy-start(bf16[2,256,512]{2,1,0:T(8,128)(2,1)S(1)} %collective-permute-done.1.refs_3_) | copy-start | bytes 1572868
  22.7 14.1 %collective-permute-start.2 = (bf16[2,256,512]{2,1,0:T(8,128)(2,1)S(1)}, bf16[2,256,512]{2,1,0:T(8,128)(2,1)S(1)}, u32[]{:S(2)}, u32[]{:S(2)}) collective-permute-start(bf16[2,256,512]{2,1,0:T(8,128)(2,1)S(1)} %broadcast_select_fusion), channel_id=1, source_target_pairs={{0,2},{2,0},{4,6},{6,4},{8,10},{10,8},{12,14},{14,12},{16,18},{18,... | collective-permute-start | bytes 1572872 | tf_op jit(solution)/shard_map/ppermute | solution.py:141
  36.8 0.8 copy-start.3
  42.9 39.8 %collective-permute-start.3 = (bf16[128,2048]{1,0:T(8,128)(2,1)}, bf16[128,2048]{1,0:T(8,128)(2,1)S(1)}, u32[]{:S(2)}, u32[]{:S(2)}) collective-permute-start(bf16[128,2048]{1,0:T(8,128)(2,1)} %shard_map.38), channel_id=1, source_target_pairs={{0,1},{1,0},{2,3},{3,2},{4,5},{5,4},{6,7},{7,6},{8,9},{9,8},{10,11... | collective-permute-start | bytes 1572872 | tf_op jit(solution)/shard_map/ppermute | solution.py:16
  56.6 27.0 %collective-permute-start.4 = (bf16[128,2048]{1,0:T(8,128)(2,1)}, bf16[128,2048]{1,0:T(8,128)(2,1)S(1)}, u32[]{:S(2)}, u32[]{:S(2)}) collective-permute-start(bf16[128,2048]{1,0:T(8,128)(2,1)} %shard_map.39), channel_id=1, source_target_pairs={{0,1},{1,0},{2,3},{3,2},{4,5},{5,4},{6,7},{7,6},{8,9},{9,8},{10,11... | collective-permute-start | bytes 1572872 | tf_op jit(solution)/shard_map/ppermute | solution.py:16

commit v10 on v3

--- a/solution.py
+++ b/solution.py
@@ -19,58 +19,75 @@
 def attend_kernel(table_ref, where_ref, q_ref, *refs, span, group, head_size, steps, scale):
     kv_refs = refs[:steps]
     o_ref = refs[steps]
-    s_ref, mx_ref, sm_ref, acc_ref = refs[steps + 1 :]
+    s_ref, mx_ref, sm_ref, p_ref, v_ref = refs[steps + 1 :]
     cycle = table_ref.shape[0] // 2
+    half = where_ref[0]
     myself = where_ref[1]
-    query_span = table_ref[2 * myself + where_ref[0]]
-    key_spans = [
-        table_ref[2 * ((myself + cycle - b) % cycle) + t] for b in range(steps) for t in range(2)
-    ]
+    query_span = table_ref[2 * myself + half]
     n = group * span
 
-    mx_ref[...] = jnp.full(mx_ref.shape, -jnp.inf, jnp.float32)
-    tiles = [(b, t) for b in range(steps) for t in range(2)]
+    def key_span(b, t):
+        return table_ref[2 * ((myself + cycle - b) % cycle) + t]
 
-    def score(idx, b, t, masked):
-        k = kv_refs[b][0, t * span : (t + 1) * span, :]
-        q = q_ref[...].reshape(n, head_size)
-        s = lax.dot_general(
-            q, k, (((1,), (1,)), ((), ())), preferred_element_type=jnp.float32
-        ) * scale
-        if masked:
-            row = lax.broadcasted_iota(jnp.int32, (n, span), 0) % span
-            col = lax.broadcasted_iota(jnp.int32, (n, span), 1)
-            s = jnp.where(col <= row, s, -jnp.inf)
-        s_ref[idx] = s
-        mx_ref[...] = jnp.maximum(mx_ref[...], s)
+    def run(tiles, always, diag):
+        def score(idx, b, t, first):
+            k = kv_refs[b][0, t * span : (t + 1) * span, :]
+            q = q_ref[...].reshape(n, head_size)
+            s = jnp.dot(q, k.T, preferred_element_type=jnp.float32) * scale
+            if idx == diag:
+                row = lax.broadcasted_iota(jnp.int32, (n, span), 0) % span
+                col = lax.broadcasted_iota(jnp.int32, (n, span), 1)
+                s = jnp.where(col <= row, s, -jnp.inf)
+            s_ref[idx] = s
+            if first:
+                mx_ref[...] = s
+            else:
+                mx_ref[...] = jnp.maximum(mx_ref[...], s)
 
-    for idx, (b, t) in enumerate(tiles):
-        key_span = key_spans[idx]
-        pl.when(key_span < query_span)(functools.partial(score, idx, b, t, False))
-        if b == 0:
-            pl.when(key_span == query_span)(functools.partial(score, idx, b, t, True))
+        def weigh(idx, first):
+            p = jnp.exp(s_ref[idx] - mx_ref[...])
+            p_ref[:, idx * span : (idx + 1) * span] = p.astype(jnp.bfloat16)
+            if first:
+                sm_ref[...] = p
+            else:
+                sm_ref[...] += p
 
-    m = jnp.max(mx_ref[...], axis=1, keepdims=True)
-    mx_ref[...] = jnp.broadcast_to(m, (n, span))
-    sm_ref[...] = jnp.zeros(sm_ref.shape, jnp.float32)
-    acc_ref[...] = jnp.zeros(acc_ref.shape, jnp.float32)
+        def hide(idx):
+            p_ref[:, idx * span : (idx + 1) * span] = jnp.zeros((n, span), jnp.bfloat16)
 
-    def weigh(idx, b, t):
-        p = jnp.exp(s_ref[idx] - mx_ref[...])
-        sm_ref[...] += p
-        v = kv_refs[b][1, t * span : (t + 1) * span, :]
-        acc_ref[...] += jnp.dot(p.astype(jnp.bfloat16), v, preferred_element_type=jnp.float32)
+        score(0, *tiles[0], True)
+        for idx, (b, t) in enumerate(tiles[1:], start=1):
+            if always[idx]:
+                score(idx, b, t, False)
+            else:
+                pl.when(key_span(b, t) < query_span)(functools.partial(score, idx, b, t, False))
 
-    for idx, (b, t) in enumerate(tiles):
-        key_span = key_spans[idx]
-        pl.when(key_span <= query_span)(functools.partial(weigh, idx, b, t))
+        m = jnp.max(mx_ref[...], axis=1, keepdims=True)
+        mx_ref[...] = jnp.broadcast_to(m, (n, span))
 
-    total = jnp.sum(sm_ref[...], axis=1, keepdims=True)
-    result = acc_ref[...] / total
-    for h in range(group):
-        o_ref[:, h * head_size : (h + 1) * head_size] = result[
-            h * span : (h + 1) * span, :
-        ].astype(o_ref.dtype)
+        weigh(0, True)
+        for idx, (b, t) in enumerate(tiles[1:], start=1):
+            if always[idx]:
+                weigh(idx, False)
+            else:
+                visible = key_span(b, t) < query_span
+                pl.when(visible)(functools.partial(weigh, idx, False))
+                pl.when(jnp.logical_not(visible))(functools.partial(hide, idx))
+        for idx, (b, t) in enumerate(tiles):
+            v_ref[idx * span : (idx + 1) * span, :] = kv_refs[b][1, t * span : (t + 1) * span, :]
+        width = len(tiles) * span
+        acc = jnp.dot(p_ref[:, :width], v_ref[:width, :], preferred_element_type=jnp.float32)
+        total = jnp.sum(sm_ref[...], axis=1, keepdims=True)
+        result = acc / total
+        for h in range(group):
+            o_ref[:, h * head_size : (h + 1) * head_size] = result[
+                h * span : (h + 1) * span, :
+            ].astype(o_ref.dtype)
+
+    early = [(b, 0) for b in range(steps)]
+    late = early + [(b, 1) for b in range(steps)]
+    pl.when(half == 0)(lambda: run(early, [b == 0 for b, t in early], 0))
+    pl.when(half == 1)(lambda: run(late, [t == 0 or b == 0 for b, t in late], steps))
 
 
 def attend_half(table, where, q2, blocks, *, span, group, head_size, first, count, out_cols, out_block0):
@@ -100,7 +117,8 @@
                 pltpu.VMEM((2 * steps, group * span, span), jnp.float32),
                 pltpu.VMEM((group * span, span), jnp.float32),
                 pltpu.VMEM((group * span, span), jnp.float32),
-                pltpu.VMEM((group * span, head_size), jnp.float32),
+                pltpu.VMEM((group * span, 2 * steps * span), jnp.bfloat16),
+                pltpu.VMEM((2 * steps * span, head_size), jnp.bfloat16),
             ],
         ),
         compiler_params=pltpu.CompilerParams(dimension_semantics=("arbitrary",)),

time: 88.5 us -> 78.9 us (0.89)
  Pallas kernels: 30 us -> 24 us
  starting transfers between devices: 22.8 us -> 19.2 us
    pallas_call x3, Pallas kernels: 30 us -> 24 us  [attend_half(): pl.pallas_call(kernel, out_shape=jax.ShapeDtypeStruct((span, out_cols), j...]
    ppermute x4, starting transfers between devices: 20.8 us -> 17.3 us  [shifted(): return lax.ppermute(value, axis, pairs)]
  transfers between devices with their start and end apart: 5 -> 5, of which waited for: 2 -> 2; matrix products, arithmetic and copies ran while one was open for 6% -> 7% of each run, Pallas kernels for 28% -> 24%
where the time goes in v10:
time: 78.9 us; the launch traced here: 78.4 us
  waiting for transfers between devices  26.5 us (34%)
  Pallas kernels  24 us (30%)
  starting transfers between devices  19.2 us (24%)
  local copies, waits for them, and re-layouts  7.47 us (9%)
  other arithmetic  1.17 us (1%)
    ppermute x4, waiting for transfers between devices, shifted(): return lax.ppermute(value, axis, pairs)  26.5 us
    pallas_call x3, Pallas kernels, attend_half(): pl.pallas_call(kernel, out_shape=jax.ShapeDtypeStruct((span, out_cols), j...  24 us
    ppermute x4, starting transfers between devices, shifted(): return lax.ppermute(value, axis, pairs)  17.3 us
    unnamed x9, local copies, waits for them, and re-layouts  4.57 us
    ppermute x1, starting transfers between devices, body(): lax.ppermute(jnp.where(myself % 2 == 0, first, third), 'ctx', pairs)  1.92 us
    dynamic_update_slice x2, local copies, waits for them, and re-layouts, body(): lax.dynamic_update_slice(out, arrived[j], (0, (1 - half) * width + j * pe...  1.65 us
  transfers between devices with their start and end apart: 5, of which 2 were waited for; matrix products, arithmetic and copies ran while one was open for 7% of the time, Pallas kernels for 24%

profile of v10, /device:TPU:4, one launch (start us, length us, event | category | flops | bytes accessed | tf_op | source)
XLA Modules:
  0.0 78.4 jit_solution(12153991250018771408)
XLA Ops:
  0.0 1.2 %reshape.3.refs_0_ = bf16[2,256,512]{2,1,0:T(8,128)(2,1)S(1)} reshape(bf16[2,256,4,128]{3,2,1,0:T(4,128)(2,1)} %param.4) | data formatting | bytes 1048576 | tf_op jit(solution)/shard_map/reshape | solution.py:146
  1.2 0.0 copy-start
  1.3 2.5 %collective-permute-start.1 = (bf16[2,256,512]{2,1,0:T(8,128)(2,1)S(1)}, bf16[2,256,512]{2,1,0:T(8,128)(2,1)S(1)}, u32[]{:S(2)}, u32[]{:S(2)}) collective-permute-start(bf16[2,256,512]{2,1,0:T(8,128)(2,1)S(1)} %reshape.3.refs_0_), channel_id=1, source_target_pairs={{0,6},{2,8},{4,10},{6,12},{8,14},{10,16},{12,18},{14,20},{16,22},{... | collective-permute-start | bytes 1572872 | tf_op jit(solution)/shard_map/ppermute | solution.py:16
  3.8 3.0 %collective-permute-start = (bf16[2,256,512]{2,1,0:T(8,128)(2,1)S(1)}, bf16[2,256,512]{2,1,0:T(8,128)(2,1)S(1)}, u32[]{:S(2)}, u32[]{:S(2)}) collective-permute-start(bf16[2,256,512]{2,1,0:T(8,128)(2,1)S(1)} %reshape.3.refs_0_), channel_id=1, source_target_pairs={{0,2},{2,4},{4,6},{6,8},{8,10},{10,12},{12,14},{14,16},{16,18},{18... | collective-permute-start | bytes 1572872 | tf_op jit(solution)/shard_map/ppermute | solution.py:16
  6.8 14.6 %collective-permute-done.1.refs_3_ = bf16[2,256,512]{2,1,0:T(8,128)(2,1)S(1)} collective-permute-done((bf16[2,256,512]{2,1,0:T(8,128)(2,1)S(1)}, bf16[2,256,512]{2,1,0:T(8,128)(2,1)S(1)}, u32[]{:S(2)}, u32[]{:S(2)}) %collective-permute-start.1) | collective-permute-done | bytes 524320 | tf_op jit(solution)/shard_map/ppermute | solution.py:16
  21.4 11.9 %collective-permute-done.refs_1_ = bf16[2,256,512]{2,1,0:T(8,128)(2,1)S(1)} collective-permute-done((bf16[2,256,512]{2,1,0:T(8,128)(2,1)S(1)}, bf16[2,256,512]{2,1,0:T(8,128)(2,1)S(1)}, u32[]{:S(2)}, u32[]{:S(2)}) %collective-permute-start) | collective-permute-done | bytes 524320 | tf_op jit(solution)/shard_map/ppermute | solution.py:16
  33.3 0.1 broadcast_select_fusion
  33.3 1.9 %collective-permute-start.2 = (bf16[2,256,512]{2,1,0:T(8,128)(2,1)S(1)}, bf16[2,256,512]{2,1,0:T(8,128)(2,1)S(1)}, u32[]{:S(2)}, u32[]{:S(2)}) collective-permute-start(bf16[2,256,512]{2,1,0:T(8,128)(2,1)S(1)} %broadcast_select_fusion), channel_id=1, source_target_pairs={{0,2},{2,0},{4,6},{6,4},{8,10},{10,8},{12,14},{14,12},{16,18},{18,... | collective-permute-start | bytes 1572872 | tf_op jit(solution)/shard_map/ppermute | solution.py:150
  35.3 3.7 %copy.6 = bf16[256,32,128]{2,0,1:T(8,128)(2,1)} copy(bf16[256,32,128]{2,1,0:T(8,128)(2,1)} %param.3) | data formatting | bytes 4194304 | tf_op args[0]
  39.0 0.0 copy-done
  39.0 0.0 copy-done.1
  39.0 0.5 compare_select_fusion.where_ref
  39.5 0.0 collective-permute-done.2.refs_2_
  39.5 0.8 %copy-done.3 = bf16[2,256,512]{2,1,0:T(8,128)(2,1)} copy-done((bf16[2,256,512]{2,1,0:T(8,128)(2,1)}, bf16[2,256,512]{2,1,0:T(8,128)(2,1)S(1)}, u32[]{:S(2)}) %copy-start.3) | copy-done | bytes 524312
  40.4 4.9 %shard_map.38 = bf16[128,2048]{1,0:T(8,128)(2,1)} custom-call(s32[512]{0:T(512)} %table_ref.5, s32[2]{0:T(128)} %compare_select_fusion.where_ref, bf16[32,256,128]{2,1,0:T(8,128)(2,1)} %bitcast.3, bf16[2,256,512]{2,1,0:T(8,128)(2,1)} %copy-done, bf16[2,256,512]{2,1,0:T(8,128)(2,1)} %copy-done.2, bf16[2,256,512]{2,1,0:T(8,128)(2,1)} %copy-done.3, ...), custom_call_target="tpu_custom_call" | custom-call | flops 1073741824 | bytes 2097152 | tf_op jit(solution)/shard_map/pallas_call | solution.py:108
  45.3 6.2 %collective-permute-start.3 = (bf16[128,2048]{1,0:T(8,128)(2,1)}, bf16[128,2048]{1,0:T(8,128)(2,1)S(1)}, u32[]{:S(2)}, u32[]{:S(2)}) collective-permute-start(bf16[128,2048]{1,0:T(8,128)(2,1)} %shard_map.38), channel_id=1, source_target_pairs={{0,1},{1,0},{2,3},{3,2},{4,5},{5,4},{6,7},{7,6},{8,9},{9,8},{10,11... | collective-permute-start | bytes 1572872 | tf_op jit(solution)/shard_map/ppermute | solution.py:16
  51.4 4.9 %shard_map.39 = bf16[128,2048]{1,0:T(8,128)(2,1)} custom-call(s32[512]{0:T(512)} %table_ref.5, s32[2]{0:T(128)} %compare_select_fusion.where_ref, bf16[32,256,128]{2,1,0:T(8,128)(2,1)} %bitcast.4, bf16[2,256,512]{2,1,0:T(8,128)(2,1)} %copy-done, bf16[2,256,512]{2,1,0:T(8,128)(2,1)} %copy-done.2, bf16[2,256,512]{2,1,0:T(8,128)(2,1)} %copy-done.3, ...), custom_call_target="tpu_custom_call" | custom-call | flops 1073741824 | bytes 2097152 | tf_op jit(solution)/shard_map/pallas_call | solution.py:108
  56.3 5.6 %collective-permute-start.4 = (bf16[128,2048]{1,0:T(8,128)(2,1)}, bf16[128,2048]{1,0:T(8,128)(2,1)S(1)}, u32[]{:S(2)}, u32[]{:S(2)}) collective-permute-start(bf16[128,2048]{1,0:T(8,128)(2,1)} %shard_map.39), channel_id=1, source_target_pairs={{0,1},{1,0},{2,3},{3,2},{4,5},{5,4},{6,7},{7,6},{8,9},{9,8},{10,11... | collective-permute-start | bytes 1572872 | tf_op jit(solution)/shard_map/ppermute | solution.py:16
  61.9 0.6 compare_select_fusion.1.where_ref
  62.5 14.2 %shard_map.37 = bf16[128,8192]{1,0:T(8,128)(2,1)} custom-call(s32[512]{0:T(512)} %table_ref.5, s32[2]{0:T(128)} %compare_select_fusion.1.where_ref, bf16[32,256,128]{2,1,0:T(8,128)(2,1)} %bitcast.5, bf16[2,256,512]{2,1,0:T(8,128)(2,1)} %copy-done, bf16[2,256,512]{2,1,0:T(8,128)(2,1)} %copy-done.2, bf16[2,256,512]{2,1,0:T(8,128)(2,1)} %copy-done.3, ...), custom_call_target="tpu_custom_call" | custom-call | flops 2147483648 | bytes 4194304 | tf_op jit(solution)/shard_map/pallas_call | solution.py:108
  76.7 0.0 collective-permute-done.3
  76.7 0.8 %constant_dynamic-update-slice_fusion.1 = bf16[128,8192]{1,0:T(8,128)(2,1)} fusion(bf16[128,8192]{1,0:T(8,128)(2,1)} %shard_map.37, bf16[128,2048]{1,0:T(8,128)(2,1)S(1)} %collective-permute-done.3, s32[]{:T(128)S(6)} %select_n.33), kind=kLoop, calls=%fused_computation.5 | loop fusion | bytes 1048580 | tf_op jit(solution)/shard_map/dynamic_update_slice | solution.py:172
  77.6 0.0 collective-permute-done.4
  77.6 0.8 %constant_dynamic-update-slice_fusion = bf16[128,8192]{1,0:T(8,128)(2,1)} fusion(bf16[128,8192]{1,0:T(8,128)(2,1)} %constant_dynamic-update-slice_fusion.1, bf16[128,2048]{1,0:T(8,128)(2,1)S(1)} %collective-permute-done.4, s32[]{:T(128)S(6)} %select_n.34), kind=kLoop, calls=%fused_computation.4 | loop fusion | bytes 1048580 | tf_op jit(solution)/shard_map/dynamic_update_slice | solution.py:172
  (4 shorter events, 0.0 us)
Async XLA Ops:
  1.2 37.8 %copy-start = (bf16[2,256,512]{2,1,0:T(8,128)(2,1)}, bf16[2,256,512]{2,1,0:T(8,128)(2,1)S(1)}, u32[]{:S(2)}) copy-start(bf16[2,256,512]{2,1,0:T(8,128)(2,1)S(1)} %reshape.3.refs_0_) | copy-start | bytes 1572868
  1.3 20.2 %collective-permute-start.1 = (bf16[2,256,512]{2,1,0:T(8,128)(2,1)S(1)}, bf16[2,256,512]{2,1,0:T(8,128)(2,1)S(1)}, u32[]{:S(2)}, u32[]{:S(2)}) collective-permute-start(bf16[2,256,512]{2,1,0:T(8,128)(2,1)S(1)} %reshape.3.refs_0_), channel_id=1, source_target_pairs={{0,6},{2,8},{4,10},{6,12},{8,14},{10,16},{12,18},{14,20},{16,22},{... | collective-permute-start | bytes 1572872 | tf_op jit(solution)/shard_map/ppermute | solution.py:16
  3.8 29.5 %collective-permute-start = (bf16[2,256,512]{2,1,0:T(8,128)(2,1)S(1)}, bf16[2,256,512]{2,1,0:T(8,128)(2,1)S(1)}, u32[]{:S(2)}, u32[]{:S(2)}) collective-permute-start(bf16[2,256,512]{2,1,0:T(8,128)(2,1)S(1)} %reshape.3.refs_0_), channel_id=1, source_target_pairs={{0,2},{2,4},{4,6},{6,8},{8,10},{10,12},{12,14},{14,16},{16,18},{18... | collective-permute-start | bytes 1572872 | tf_op jit(solution)/shard_map/ppermute | solution.py:16
  21.4 17.6 %copy-start.1 = (bf16[2,256,512]{2,1,0:T(8,128)(2,1)}, bf16[2,256,512]{2,1,0:T(8,128)(2,1)S(1)}, u32[]{:S(2)}) copy-start(bf16[2,256,512]{2,1,0:T(8,128)(2,1)S(1)} %collective-permute-done.1.refs_3_) | copy-start | bytes 1572868
  33.3 5.8 %copy-start.2 = (bf16[2,256,512]{2,1,0:T(8,128)(2,1)}, bf16[2,256,512]{2,1,0:T(8,128)(2,1)S(1)}, u32[]{:S(2)}) copy-start(bf16[2,256,512]{2,1,0:T(8,128)(2,1)S(1)} %collective-permute-done.refs_1_) | copy-start | bytes 1572868
  33.3 6.2 %collective-permute-start.2 = (bf16[2,256,512]{2,1,0:T(8,128)(2,1)S(1)}, bf16[2,256,512]{2,1,0:T(8,128)(2,1)S(1)}, u32[]{:S(2)}, u32[]{:S(2)}) collective-permute-start(bf16[2,256,512]{2,1,0:T(8,128)(2,1)S(1)} %broadcast_select_fusion), channel_id=1, source_target_pairs={{0,2},{2,0},{4,6},{6,4},{8,10},{10,8},{12,14},{14,12},{16,18},{18,... | collective-permute-start | bytes 1572872 | tf_op jit(solution)/shard_map/ppermute | solution.py:150
  39.5 0.8 %copy-start.3 = (bf16[2,256,512]{2,1,0:T(8,128)(2,1)}, bf16[2,256,512]{2,1,0:T(8,128)(2,1)S(1)}, u32[]{:S(2)}) copy-start(bf16[2,256,512]{2,1,0:T(8,128)(2,1)S(1)} %collective-permute-done.2.refs_2_) | copy-start | bytes 1572868
  45.3 31.5 %collective-permute-start.3 = (bf16[128,2048]{1,0:T(8,128)(2,1)}, bf16[128,2048]{1,0:T(8,128)(2,1)S(1)}, u32[]{:S(2)}, u32[]{:S(2)}) collective-permute-start(bf16[128,2048]{1,0:T(8,128)(2,1)} %shard_map.38), channel_id=1, source_target_pairs={{0,1},{1,0},{2,3},{3,2},{4,5},{5,4},{6,7},{7,6},{8,9},{9,8},{10,11... | collective-permute-start | bytes 1572872 | tf_op jit(solution)/shard_map/ppermute | solution.py:16
  56.3 21.2 %collective-permute-start.4 = (bf16[128,2048]{1,0:T(8,128)(2,1)}, bf16[128,2048]{1,0:T(8,128)(2,1)S(1)}, u32[]{:S(2)}, u32[]{:S(2)}) collective-permute-start(bf16[128,2048]{1,0:T(8,128)(2,1)} %shard_map.39), channel_id=1, source_target_pairs={{0,1},{1,0},{2,3},{3,2},{4,5},{5,4},{6,7},{7,6},{8,9},{9,8},{10,11... | collective-permute-start | bytes 1572872 | tf_op jit(solution)/shard_map/ppermute | solution.py:16

commit v11 on v10

--- a/solution.py
+++ b/solution.py
@@ -155,7 +155,7 @@
     sent_where = jnp.where(lanes == 0, 1 - half, myself).astype(jnp.int32)
     kept_where = jnp.where(lanes == 0, half, myself).astype(jnp.int32)
     common = dict(span=span, group=group, head_size=head_size)
-    chunks = 2
+    chunks = 1
     per = kv_here // chunks
     arrived = []
     for j in range(chunks):

time: 78.9 us -> 81.6 us (1.034)
  waiting for transfers between devices: 26.5 us -> 34.9 us
  starting transfers between devices: 19.2 us -> 15.9 us
  local copies, waits for them, and re-layouts: 7.47 us -> 4.63 us
  other arithmetic: 1.17 us -> 3.08 us
  Pallas kernels: 24 us -> 22.7 us
    ppermute x4 -> x3, waiting for transfers between devices: 26.5 us -> 34.9 us  [shifted(): return lax.ppermute(value, axis, pairs)]
    ppermute x4 -> x3, starting transfers between devices: 17.3 us -> 13.9 us  [shifted(): return lax.ppermute(value, axis, pairs)]
    unnamed x9 -> x7, local copies, waits for them, and re-layouts: 4.57 us -> 2.18 us
    select_n x1, other arithmetic: 0.06 us -> 1.89 us  [body(): jnp.where(myself % 2 == 0, first, third)]
    pallas_call x3 -> x2, Pallas kernels: 24 us -> 22.7 us  [attend_half(): pl.pallas_call(kernel, out_shape=jax.ShapeDtypeStruct((span, out_cols), j...]
    dynamic_update_slice x2 -> x1, local copies, waits for them, and re-layouts: 1.65 us -> 1.06 us  [body(): lax.dynamic_update_slice(out, arrived[j], (0, (1 - half) * width + j * pe...]
  transfers between devices with their start and end apart: 5 -> 4, of which waited for: 2 -> 3; matrix products, arithmetic and copies ran while one was open for 7% -> 4% of each run, Pallas kernels for 24% -> 17%
where the time goes in v11:
time: 81.6 us; the launch traced here: 81.2 us
  waiting for transfers between devices  34.9 us (43%)
  Pallas kernels  22.7 us (28%)
  starting transfers between devices  15.9 us (19%)
  local copies, waits for them, and re-layouts  4.63 us (6%)
  other arithmetic  3.08 us (4%)
    ppermute x3, waiting for transfers between devices, shifted(): return lax.ppermute(value, axis, pairs)  34.9 us
    pallas_call x2, Pallas kernels, attend_half(): pl.pallas_call(kernel, out_shape=jax.ShapeDtypeStruct((span, out_cols), j...  22.7 us
    ppermute x3, starting transfers between devices, shifted(): return lax.ppermute(value, axis, pairs)  13.9 us
    unnamed x7, local copies, waits for them, and re-layouts  2.18 us
    ppermute x1, starting transfers between devices, body(): lax.ppermute(jnp.where(myself % 2 == 0, first, third), 'ctx', pairs)  1.91 us
    select_n x1, other arithmetic, body(): jnp.where(myself % 2 == 0, first, third)  1.89 us
  transfers between devices with their start and end apart: 4, of which 3 were waited for; matrix products, arithmetic and copies ran while one was open for 4% of the time, Pallas kernels for 17%

profile of v11, /device:TPU:4, one launch (start us, length us, event | category | flops | bytes accessed | tf_op | source)
XLA Modules:
  0.0 81.2 jit_solution(1587629553322557244)
XLA Ops:
  0.0 0.0 copy-start
  0.0 1.4 %reshape.3.refs_0_ = bf16[2,256,512]{2,1,0:T(8,128)(2,1)S(1)} reshape(bf16[2,256,4,128]{3,2,1,0:T(4,128)(2,1)} %param.4) | data formatting | bytes 1048576 | tf_op jit(solution)/shard_map/reshape | solution.py:146
  1.4 0.0 copy-start.1
  1.4 2.5 %collective-permute-start.1 = (bf16[2,256,512]{2,1,0:T(8,128)(2,1)S(1)}, bf16[2,256,512]{2,1,0:T(8,128)(2,1)S(1)}, u32[]{:S(2)}, u32[]{:S(2)}) collective-permute-start(bf16[2,256,512]{2,1,0:T(8,128)(2,1)S(1)} %reshape.3.refs_0_), channel_id=1, source_target_pairs={{0,6},{2,8},{4,10},{6,12},{8,14},{10,16},{12,18},{14,20},{16,22},{... | collective-permute-start | bytes 1572872 | tf_op jit(solution)/shard_map/ppermute | solution.py:16
  4.0 3.0 %collective-permute-start = (bf16[2,256,512]{2,1,0:T(8,128)(2,1)S(1)}, bf16[2,256,512]{2,1,0:T(8,128)(2,1)}, u32[]{:S(2)}, u32[]{:S(2)}) collective-permute-start(bf16[2,256,512]{2,1,0:T(8,128)(2,1)S(1)} %reshape.3.refs_0_), channel_id=1, source_target_pairs={{0,2},{2,4},{4,6},{6,8},{8,10},{10,12},{12,14},{14,16},{16,18},{18... | collective-permute-start | bytes 1572872 | tf_op jit(solution)/shard_map/ppermute | solution.py:16
  6.9 14.6 %collective-permute-done.1.refs_3_ = bf16[2,256,512]{2,1,0:T(8,128)(2,1)S(1)} collective-permute-done((bf16[2,256,512]{2,1,0:T(8,128)(2,1)S(1)}, bf16[2,256,512]{2,1,0:T(8,128)(2,1)S(1)}, u32[]{:S(2)}, u32[]{:S(2)}) %collective-permute-start.1) | collective-permute-done | bytes 524320 | tf_op jit(solution)/shard_map/ppermute | solution.py:16
  21.6 0.0 copy-start.2
  21.6 12.0 %collective-permute-done.refs_1_ = bf16[2,256,512]{2,1,0:T(8,128)(2,1)} collective-permute-done((bf16[2,256,512]{2,1,0:T(8,128)(2,1)S(1)}, bf16[2,256,512]{2,1,0:T(8,128)(2,1)}, u32[]{:S(2)}, u32[]{:S(2)}) %collective-permute-start) | collective-permute-done | bytes 524320 | tf_op jit(solution)/shard_map/ppermute | solution.py:16
  33.5 1.9 %broadcast_select_fusion = bf16[2,256,512]{2,1,0:T(8,128)(2,1)} fusion(bf16[2,256,512]{2,1,0:T(8,128)(2,1)} %collective-permute-done.refs_1_, bf16[2,256,512]{2,1,0:T(8,128)(2,1)S(1)} %collective-permute-done.1.refs_3_, pred[]{:T(512)S(6)} %eq.12), kind=kLoop, calls=%fused_computation.1 | loop fusion | flops 262144 | bytes 1572865 | tf_op jit(solution)/shard_map/jit(_where)/select_n | solution.py:150
  35.4 1.9 %collective-permute-start.2 = (bf16[2,256,512]{2,1,0:T(8,128)(2,1)}, bf16[2,256,512]{2,1,0:T(8,128)(2,1)}, u32[]{:S(2)}, u32[]{:S(2)}) collective-permute-start(bf16[2,256,512]{2,1,0:T(8,128)(2,1)} %broadcast_select_fusion), channel_id=1, source_target_pairs={{0,2},{2,0},{4,6},{6,4},{8,10},{10,8},{12,14},{14,12},{16,18},{18,... | collective-permute-start | bytes 1572872 | tf_op jit(solution)/shard_map/ppermute | solution.py:150
  37.3 0.0 copy-done
  37.4 2.2 %copy.6 = bf16[256,32,128]{2,0,1:T(8,128)(2,1)} copy(bf16[256,32,128]{2,1,0:T(8,128)(2,1)S(1)} %copy-done) | data formatting | bytes 4194304 | tf_op args[0]
  39.5 0.0 copy-done.1
  39.5 0.0 copy-done.2
  39.5 0.6 compare_select_fusion.where_ref
  40.1 0.0 collective-permute-done.2.refs_2_
  40.1 8.5 %shard_map.38 = bf16[128,4096]{1,0:T(8,128)(2,1)} custom-call(s32[512]{0:T(512)} %table_ref.3, s32[2]{0:T(128)} %compare_select_fusion.where_ref, bf16[32,256,128]{2,1,0:T(8,128)(2,1)} %bitcast.3, bf16[2,256,512]{2,1,0:T(8,128)(2,1)} %copy-done.1, bf16[2,256,512]{2,1,0:T(8,128)(2,1)} %collective-permute-done.refs_1_, ...), custom_call_target="tpu_custom_call" | custom-call | flops 2147483648 | bytes 4194304 | tf_op jit(solution)/shard_map/pallas_call | solution.py:108
  48.6 8.4 %collective-permute-start.3 = (bf16[128,4096]{1,0:T(8,128)(2,1)}, bf16[128,4096]{1,0:T(8,128)(2,1)S(1)}, u32[]{:S(2)}, u32[]{:S(2)}) collective-permute-start(bf16[128,4096]{1,0:T(8,128)(2,1)} %shard_map.38), channel_id=1, source_target_pairs={{0,1},{1,0},{2,3},{3,2},{4,5},{5,4},{6,7},{7,6},{8,9},{9,8},{10,11... | collective-permute-start | bytes 3145736 | tf_op jit(solution)/shard_map/ppermute | solution.py:16
  57.0 0.6 compare_select_fusion.1.where_ref
  57.6 14.2 %shard_map.37 = bf16[128,8192]{1,0:T(8,128)(2,1)} custom-call(s32[512]{0:T(512)} %table_ref.3, s32[2]{0:T(128)} %compare_select_fusion.1.where_ref, bf16[32,256,128]{2,1,0:T(8,128)(2,1)} %bitcast.4, bf16[2,256,512]{2,1,0:T(8,128)(2,1)} %copy-done.1, bf16[2,256,512]{2,1,0:T(8,128)(2,1)} %collective-permute-done.refs_1_, ...), custom_call_target="tpu_custom_call" | custom-call | flops 2147483648 | bytes 4194304 | tf_op jit(solution)/shard_map/pallas_call | solution.py:108
  71.8 8.3 %collective-permute-done.3 = bf16[128,4096]{1,0:T(8,128)(2,1)S(1)} collective-permute-done((bf16[128,4096]{1,0:T(8,128)(2,1)}, bf16[128,4096]{1,0:T(8,128)(2,1)S(1)}, u32[]{:S(2)}, u32[]{:S(2)}) %collective-permute-start.3) | collective-permute-done | bytes 1048608 | tf_op jit(solution)/shard_map/ppermute | solution.py:16
  80.1 1.1 %constant_dynamic-update-slice_fusion = bf16[128,8192]{1,0:T(8,128)(2,1)} fusion(bf16[128,8192]{1,0:T(8,128)(2,1)} %shard_map.37, bf16[128,4096]{1,0:T(8,128)(2,1)S(1)} %collective-permute-done.3, s32[]{:T(128)S(6)} %select_n.30), kind=kLoop, calls=%fused_computation.4 | loop fusion | bytes 2097156 | tf_op jit(solution)/shard_map/dynamic_update_slice | solution.py:172
Async XLA Ops:
  0.0 37.3 %copy-start = (bf16[256,32,128]{2,1,0:T(8,128)(2,1)S(1)}, bf16[256,32,128]{2,1,0:T(8,128)(2,1)}, u32[]{:S(2)}) copy-start(bf16[256,32,128]{2,1,0:T(8,128)(2,1)} %param.3) | copy-start | bytes 6291460
  1.4 38.1 %copy-start.1 = (bf16[2,256,512]{2,1,0:T(8,128)(2,1)}, bf16[2,256,512]{2,1,0:T(8,128)(2,1)S(1)}, u32[]{:S(2)}) copy-start(bf16[2,256,512]{2,1,0:T(8,128)(2,1)S(1)} %reshape.3.refs_0_) | copy-start | bytes 1572868
  1.4 20.2 %collective-permute-start.1 = (bf16[2,256,512]{2,1,0:T(8,128)(2,1)S(1)}, bf16[2,256,512]{2,1,0:T(8,128)(2,1)S(1)}, u32[]{:S(2)}, u32[]{:S(2)}) collective-permute-start(bf16[2,256,512]{2,1,0:T(8,128)(2,1)S(1)} %reshape.3.refs_0_), channel_id=1, source_target_pairs={{0,6},{2,8},{4,10},{6,12},{8,14},{10,16},{12,18},{14,20},{16,22},{... | collective-permute-start | bytes 1572872 | tf_op jit(solution)/shard_map/ppermute | solution.py:16
  4.0 29.6 %collective-permute-start = (bf16[2,256,512]{2,1,0:T(8,128)(2,1)S(1)}, bf16[2,256,512]{2,1,0:T(8,128)(2,1)}, u32[]{:S(2)}, u32[]{:S(2)}) collective-permute-start(bf16[2,256,512]{2,1,0:T(8,128)(2,1)S(1)} %reshape.3.refs_0_), channel_id=1, source_target_pairs={{0,2},{2,4},{4,6},{6,8},{8,10},{10,12},{12,14},{14,16},{16,18},{18... | collective-permute-start | bytes 1572872 | tf_op jit(solution)/shard_map/ppermute | solution.py:16
  21.6 18.0 %copy-start.2 = (bf16[2,256,512]{2,1,0:T(8,128)(2,1)}, bf16[2,256,512]{2,1,0:T(8,128)(2,1)S(1)}, u32[]{:S(2)}) copy-start(bf16[2,256,512]{2,1,0:T(8,128)(2,1)S(1)} %collective-permute-done.1.refs_3_) | copy-start | bytes 1572868
  35.4 4.7 %collective-permute-start.2 = (bf16[2,256,512]{2,1,0:T(8,128)(2,1)}, bf16[2,256,512]{2,1,0:T(8,128)(2,1)}, u32[]{:S(2)}, u32[]{:S(2)}) collective-permute-start(bf16[2,256,512]{2,1,0:T(8,128)(2,1)} %broadcast_select_fusion), channel_id=1, source_target_pairs={{0,2},{2,0},{4,6},{6,4},{8,10},{10,8},{12,14},{14,12},{16,18},{18,... | collective-permute-start | bytes 1572872 | tf_op jit(solution)/shard_map/ppermute | solution.py:150
  48.6 31.5 %collective-permute-start.3 = (bf16[128,4096]{1,0:T(8,128)(2,1)}, bf16[128,4096]{1,0:T(8,128)(2,1)S(1)}, u32[]{:S(2)}, u32[]{:S(2)}) collective-permute-start(bf16[128,4096]{1,0:T(8,128)(2,1)} %shard_map.38), channel_id=1, source_target_pairs={{0,1},{1,0},{2,3},{3,2},{4,5},{5,4},{6,7},{7,6},{8,9},{9,8},{10,11... | collective-permute-start | bytes 3145736 | tf_op jit(solution)/shard_map/ppermute | solution.py:16

commit v12 on v10

--- a/solution.py
+++ b/solution.py
@@ -142,10 +142,12 @@
     half = lax.axis_index("kvh")
     table = span_table.reshape(cycle, 2)
 
-    q2 = jnp.transpose(queries, (1, 0, 2))
     own = key_value.reshape(2, rows, kv_here * head_size)
     first = shifted(own, "ctx", 1)
     third = shifted(own, "ctx", 3)
+    queries, third = lax.optimization_barrier((queries, third))
+    q2 = jnp.transpose(queries, (1, 0, 2))
+    first, q2 = lax.optimization_barrier((first, q2))
     pairs = [(d, d ^ 1) for d in range(cycle)]
     second = lax.ppermute(jnp.where(myself % 2 == 0, first, third), "ctx", pairs)
     blocks = [own, first, second, third]

time: 78.9 us -> 76.6 us (0.971)
  the two profiles are of different devices: /device:TPU:4 before, /device:TPU:1 now
where the time goes in v12:
time: 76.6 us; the launch traced here: 76.1 us
  waiting for transfers between devices  26.1 us (34%)
  Pallas kernels  25.2 us (33%)
  starting transfers between devices  15.8 us (21%)
  local copies, waits for them, and re-layouts  7.65 us (10%)
  other arithmetic  1.17 us (2%)
    pallas_call x3, Pallas kernels, attend_half(): pl.pallas_call(kernel, out_shape=jax.ShapeDtypeStruct((span, out_cols), j...  25.2 us
    ppermute x4, waiting for transfers between devices, shifted(): return lax.ppermute(value, axis, pairs)  25.1 us
    ppermute x4, starting transfers between devices, shifted(): return lax.ppermute(value, axis, pairs)  12.7 us
    optimization_barrier x1, local copies, waits for them, and re-layouts, body(): queries, third = lax.optimization_barrier((queries, third))  3.94 us
    ppermute x1, starting transfers between devices, body(): lax.ppermute(jnp.where(myself % 2 == 0, first, third), 'ctx', pairs)  3.13 us
    dynamic_update_slice x2, local copies, waits for them, and re-layouts, body(): lax.dynamic_update_slice(out, arrived[j], (0, (1 - half) * width + j * pe...  1.65 us
  transfers between devices with their start and end apart: 5, of which 3 were waited for; matrix products, arithmetic and copies ran while one was open for 8% of the time, Pallas kernels for 23%

profile of v12, /device:TPU:1, one launch (start us, length us, event | category | flops | bytes accessed | tf_op | source)
XLA Modules:
  0.0 76.1 jit_solution(2433114621364231802)
XLA Ops:
  0.0 1.2 %reshape.3.refs_0_ = bf16[2,256,512]{2,1,0:T(8,128)(2,1)S(1)} reshape(bf16[2,256,4,128]{3,2,1,0:T(4,128)(2,1)} %param.4) | data formatting | bytes 1048576 | tf_op jit(solution)/shard_map/reshape | solution.py:145
  1.2 0.0 copy-start
  1.3 4.6 %collective-permute-start.1 = (bf16[2,256,512]{2,1,0:T(8,128)(2,1)S(1)}, bf16[2,256,512]{2,1,0:T(8,128)(2,1)S(1)}, u32[]{:S(2)}, u32[]{:S(2)}) collective-permute-start(bf16[2,256,512]{2,1,0:T(8,128)(2,1)S(1)} %reshape.3.refs_0_), channel_id=1, source_target_pairs={{0,6},{2,8},{4,10},{6,12},{8,14},{10,16},{12,18},{14,20},{16,22},{... | collective-permute-start | bytes 1572872 | tf_op jit(solution)/shard_map/ppermute | solution.py:16
  5.9 2.8 %collective-permute-start = (bf16[2,256,512]{2,1,0:T(8,128)(2,1)S(1)}, bf16[2,256,512]{2,1,0:T(8,128)(2,1)S(1)}, u32[]{:S(2)}, u32[]{:S(2)}) collective-permute-start(bf16[2,256,512]{2,1,0:T(8,128)(2,1)S(1)} %reshape.3.refs_0_), channel_id=1, source_target_pairs={{0,2},{2,4},{4,6},{6,8},{8,10},{10,12},{12,14},{14,16},{16,18},{18... | collective-permute-start | bytes 1572872 | tf_op jit(solution)/shard_map/ppermute | solution.py:16
  8.7 21.2 %collective-permute-done.1.refs_3_ = bf16[2,256,512]{2,1,0:T(8,128)(2,1)S(1)} collective-permute-done((bf16[2,256,512]{2,1,0:T(8,128)(2,1)S(1)}, bf16[2,256,512]{2,1,0:T(8,128)(2,1)S(1)}, u32[]{:S(2)}, u32[]{:S(2)}) %collective-permute-start.1) | collective-permute-done | bytes 524320 | tf_op jit(solution)/shard_map/ppermute | solution.py:16
  29.9 3.9 %copy.6 = bf16[256,32,128]{2,0,1:T(8,128)(2,1)} copy(bf16[256,32,128]{2,1,0:T(8,128)(2,1)} %param.3) | data formatting | bytes 4194304 | tf_op jit(solution)/shard_map/optimization_barrier | solution.py:148
  33.8 0.0 copy-done
  33.8 0.0 collective-permute-done.refs_1_
  33.8 0.0 copy-done.1
  33.8 0.1 broadcast_select_fusion
  33.9 3.1 %collective-permute-start.2 = (bf16[2,256,512]{2,1,0:T(8,128)(2,1)S(1)}, bf16[2,256,512]{2,1,0:T(8,128)(2,1)S(1)}, u32[]{:S(2)}, u32[]{:S(2)}) collective-permute-start(bf16[2,256,512]{2,1,0:T(8,128)(2,1)S(1)} %broadcast_select_fusion), channel_id=1, source_target_pairs={{0,2},{2,0},{4,6},{6,4},{8,10},{10,8},{12,14},{14,12},{16,18},{18,... | collective-permute-start | bytes 1572872 | tf_op jit(solution)/shard_map/ppermute | solution.py:152
  37.1 0.5 compare_select_fusion.where_ref
  37.6 1.0 %collective-permute-done.2.refs_2_ = bf16[2,256,512]{2,1,0:T(8,128)(2,1)S(1)} collective-permute-done((bf16[2,256,512]{2,1,0:T(8,128)(2,1)S(1)}, bf16[2,256,512]{2,1,0:T(8,128)(2,1)S(1)}, u32[]{:S(2)}, u32[]{:S(2)}) %collective-permute-start.2) | collective-permute-done | bytes 524320 | tf_op jit(solution)/shard_map/ppermute | solution.py:152
  38.6 0.8 %copy-done.3 = bf16[2,256,512]{2,1,0:T(8,128)(2,1)} copy-done((bf16[2,256,512]{2,1,0:T(8,128)(2,1)}, bf16[2,256,512]{2,1,0:T(8,128)(2,1)S(1)}, u32[]{:S(2)}) %copy-start.3) | copy-done | bytes 524312
  39.4 7.8 %shard_map.38 = bf16[128,2048]{1,0:T(8,128)(2,1)} custom-call(s32[512]{0:T(512)} %table_ref.5, s32[2]{0:T(128)} %compare_select_fusion.where_ref, bf16[32,256,128]{2,1,0:T(8,128)(2,1)} %bitcast.3, bf16[2,256,512]{2,1,0:T(8,128)(2,1)} %copy-done, bf16[2,256,512]{2,1,0:T(8,128)(2,1)} %copy-done.2, bf16[2,256,512]{2,1,0:T(8,128)(2,1)} %copy-done.3, ...), custom_call_target="tpu_custom_call" | custom-call | flops 1073741824 | bytes 2097152 | tf_op jit(solution)/shard_map/pallas_call | solution.py:108
  47.2 2.7 %collective-permute-start.3 = (bf16[128,2048]{1,0:T(8,128)(2,1)}, bf16[128,2048]{1,0:T(8,128)(2,1)S(1)}, u32[]{:S(2)}, u32[]{:S(2)}) collective-permute-start(bf16[128,2048]{1,0:T(8,128)(2,1)} %shard_map.38), channel_id=1, source_target_pairs={{0,1},{1,0},{2,3},{3,2},{4,5},{5,4},{6,7},{7,6},{8,9},{9,8},{10,11... | collective-permute-start | bytes 1572872 | tf_op jit(solution)/shard_map/ppermute | solution.py:16
  49.9 7.8 %shard_map.39 = bf16[128,2048]{1,0:T(8,128)(2,1)} custom-call(s32[512]{0:T(512)} %table_ref.5, s32[2]{0:T(128)} %compare_select_fusion.where_ref, bf16[32,256,128]{2,1,0:T(8,128)(2,1)} %bitcast.4, bf16[2,256,512]{2,1,0:T(8,128)(2,1)} %copy-done, bf16[2,256,512]{2,1,0:T(8,128)(2,1)} %copy-done.2, bf16[2,256,512]{2,1,0:T(8,128)(2,1)} %copy-done.3, ...), custom_call_target="tpu_custom_call" | custom-call | flops 1073741824 | bytes 2097152 | tf_op jit(solution)/shard_map/pallas_call | solution.py:108
  57.6 2.6 %collective-permute-start.4 = (bf16[128,2048]{1,0:T(8,128)(2,1)}, bf16[128,2048]{1,0:T(8,128)(2,1)S(1)}, u32[]{:S(2)}, u32[]{:S(2)}) collective-permute-start(bf16[128,2048]{1,0:T(8,128)(2,1)} %shard_map.39), channel_id=1, source_target_pairs={{0,1},{1,0},{2,3},{3,2},{4,5},{5,4},{6,7},{7,6},{8,9},{9,8},{10,11... | collective-permute-start | bytes 1572872 | tf_op jit(solution)/shard_map/ppermute | solution.py:16
  60.2 0.6 compare_select_fusion.1.where_ref
  60.8 9.6 %shard_map.37 = bf16[128,8192]{1,0:T(8,128)(2,1)} custom-call(s32[512]{0:T(512)} %table_ref.5, s32[2]{0:T(128)} %compare_select_fusion.1.where_ref, bf16[32,256,128]{2,1,0:T(8,128)(2,1)} %bitcast.5, bf16[2,256,512]{2,1,0:T(8,128)(2,1)} %copy-done, bf16[2,256,512]{2,1,0:T(8,128)(2,1)} %copy-done.2, bf16[2,256,512]{2,1,0:T(8,128)(2,1)} %copy-done.3, ...), custom_call_target="tpu_custom_call" | custom-call | flops 2147483648 | bytes 4194304 | tf_op jit(solution)/shard_map/pallas_call | solution.py:108
  70.5 0.0 collective-permute-done.3
  70.5 0.8 %constant_dynamic-update-slice_fusion.1 = bf16[128,8192]{1,0:T(8,128)(2,1)} fusion(bf16[128,8192]{1,0:T(8,128)(2,1)} %shard_map.37, bf16[128,2048]{1,0:T(8,128)(2,1)S(1)} %collective-permute-done.3, s32[]{:T(128)S(6)} %select_n.33), kind=kLoop, calls=%fused_computation.5 | loop fusion | bytes 1048580 | tf_op jit(solution)/shard_map/dynamic_update_slice | solution.py:174
  71.3 3.9 %collective-permute-done.4 = bf16[128,2048]{1,0:T(8,128)(2,1)S(1)} collective-permute-done((bf16[128,2048]{1,0:T(8,128)(2,1)}, bf16[128,2048]{1,0:T(8,128)(2,1)S(1)}, u32[]{:S(2)}, u32[]{:S(2)}) %collective-permute-start.4) | collective-permute-done | bytes 524320 | tf_op jit(solution)/shard_map/ppermute | solution.py:16
  75.3 0.8 %constant_dynamic-update-slice_fusion = bf16[128,8192]{1,0:T(8,128)(2,1)} fusion(bf16[128,8192]{1,0:T(8,128)(2,1)} %constant_dynamic-update-slice_fusion.1, bf16[128,2048]{1,0:T(8,128)(2,1)S(1)} %collective-permute-done.4, s32[]{:T(128)S(6)} %select_n.34), kind=kLoop, calls=%fused_computation.4 | loop fusion | bytes 1048580 | tf_op jit(solution)/shard_map/dynamic_update_slice | solution.py:174
  (4 shorter events, 0.0 us)
Async XLA Ops:
  1.2 32.6 %copy-start = (bf16[2,256,512]{2,1,0:T(8,128)(2,1)}, bf16[2,256,512]{2,1,0:T(8,128)(2,1)S(1)}, u32[]{:S(2)}) copy-start(bf16[2,256,512]{2,1,0:T(8,128)(2,1)S(1)} %reshape.3.refs_0_) | copy-start | bytes 1572868
  1.3 28.6 %collective-permute-start.1 = (bf16[2,256,512]{2,1,0:T(8,128)(2,1)S(1)}, bf16[2,256,512]{2,1,0:T(8,128)(2,1)S(1)}, u32[]{:S(2)}, u32[]{:S(2)}) collective-permute-start(bf16[2,256,512]{2,1,0:T(8,128)(2,1)S(1)} %reshape.3.refs_0_), channel_id=1, source_target_pairs={{0,6},{2,8},{4,10},{6,12},{8,14},{10,16},{12,18},{14,20},{16,22},{... | collective-permute-start | bytes 1572872 | tf_op jit(solution)/shard_map/ppermute | solution.py:16
  5.9 28.0 %collective-permute-start = (bf16[2,256,512]{2,1,0:T(8,128)(2,1)S(1)}, bf16[2,256,512]{2,1,0:T(8,128)(2,1)S(1)}, u32[]{:S(2)}, u32[]{:S(2)}) collective-permute-start(bf16[2,256,512]{2,1,0:T(8,128)(2,1)S(1)} %reshape.3.refs_0_), channel_id=1, source_target_pairs={{0,2},{2,4},{4,6},{6,8},{8,10},{10,12},{12,14},{14,16},{16,18},{18... | collective-permute-start | bytes 1572872 | tf_op jit(solution)/shard_map/ppermute | solution.py:16
  29.9 4.0 %copy-start.1 = (bf16[2,256,512]{2,1,0:T(8,128)(2,1)}, bf16[2,256,512]{2,1,0:T(8,128)(2,1)S(1)}, u32[]{:S(2)}) copy-start(bf16[2,256,512]{2,1,0:T(8,128)(2,1)S(1)} %collective-permute-done.1.refs_3_) | copy-start | bytes 1572868
  33.8 4.7 %copy-start.2 = (bf16[2,256,512]{2,1,0:T(8,128)(2,1)}, bf16[2,256,512]{2,1,0:T(8,128)(2,1)S(1)}, u32[]{:S(2)}) copy-start(bf16[2,256,512]{2,1,0:T(8,128)(2,1)S(1)} %collective-permute-done.refs_1_) | copy-start | bytes 1572868
  33.9 4.7 %collective-permute-start.2 = (bf16[2,256,512]{2,1,0:T(8,128)(2,1)S(1)}, bf16[2,256,512]{2,1,0:T(8,128)(2,1)S(1)}, u32[]{:S(2)}, u32[]{:S(2)}) collective-permute-start(bf16[2,256,512]{2,1,0:T(8,128)(2,1)S(1)} %broadcast_select_fusion), channel_id=1, source_target_pairs={{0,2},{2,0},{4,6},{6,4},{8,10},{10,8},{12,14},{14,12},{16,18},{18,... | collective-permute-start | bytes 1572872 | tf_op jit(solution)/shard_map/ppermute | solution.py:152
  38.6 0.8 %copy-start.3 = (bf16[2,256,512]{2,1,0:T(8,128)(2,1)}, bf16[2,256,512]{2,1,0:T(8,128)(2,1)S(1)}, u32[]{:S(2)}) copy-start(bf16[2,256,512]{2,1,0:T(8,128)(2,1)S(1)} %collective-permute-done.2.refs_2_) | copy-start | bytes 1572868
  47.2 23.3 %collective-permute-start.3 = (bf16[128,2048]{1,0:T(8,128)(2,1)}, bf16[128,2048]{1,0:T(8,128)(2,1)S(1)}, u32[]{:S(2)}, u32[]{:S(2)}) collective-permute-start(bf16[128,2048]{1,0:T(8,128)(2,1)} %shard_map.38), channel_id=1, source_target_pairs={{0,1},{1,0},{2,3},{3,2},{4,5},{5,4},{6,7},{7,6},{8,9},{9,8},{10,11... | collective-permute-start | bytes 1572872 | tf_op jit(solution)/shard_map/ppermute | solution.py:16
  57.6 17.6 %collective-permute-start.4 = (bf16[128,2048]{1,0:T(8,128)(2,1)}, bf16[128,2048]{1,0:T(8,128)(2,1)S(1)}, u32[]{:S(2)}, u32[]{:S(2)}) collective-permute-start(bf16[128,2048]{1,0:T(8,128)(2,1)} %shard_map.39), channel_id=1, source_target_pairs={{0,1},{1,0},{2,3},{3,2},{4,5},{5,4},{6,7},{7,6},{8,9},{9,8},{10,11... | collective-permute-start | bytes 1572872 | tf_op jit(solution)/shard_map/ppermute | solution.py:16

commit v13 on v12

--- a/solution.py
+++ b/solution.py
@@ -147,15 +147,15 @@
     third = shifted(own, "ctx", 3)
     queries, third = lax.optimization_barrier((queries, third))
     q2 = jnp.transpose(queries, (1, 0, 2))
-    first, q2 = lax.optimization_barrier((first, q2))
+    lanes = jnp.arange(2, dtype=jnp.int32)
+    sent_where = jnp.where(lanes == 0, 1 - half, myself).astype(jnp.int32)
+    kept_where = jnp.where(lanes == 0, half, myself).astype(jnp.int32)
+    first, q2, sent_where, kept_where = lax.optimization_barrier((first, q2, sent_where, kept_where))
     pairs = [(d, d ^ 1) for d in range(cycle)]
     second = lax.ppermute(jnp.where(myself % 2 == 0, first, third), "ctx", pairs)
     blocks = [own, first, second, third]
 
     width = heads_here * head_size
-    lanes = jnp.arange(2, dtype=jnp.int32)
-    sent_where = jnp.where(lanes == 0, 1 - half, myself).astype(jnp.int32)
-    kept_where = jnp.where(lanes == 0, half, myself).astype(jnp.int32)
     common = dict(span=span, group=group, head_size=head_size)
     chunks = 2
     per = kv_here // chunks

time: 76.6 us -> 76.4 us (level)
  waiting for transfers between devices: 26.1 us -> 28.8 us
  Pallas kernels: 25.2 us -> 22.8 us
    pallas_call x3, Pallas kernels: 25.2 us -> 22.8 us  [attend_half(): pl.pallas_call(kernel, out_shape=jax.ShapeDtypeStruct((span, out_cols), j...]
    ppermute x4, waiting for transfers between devices: 25.1 us -> 27.3 us  [shifted(): return lax.ppermute(value, axis, pairs)]
  transfers between devices with their start and end apart: 5 -> 5, of which waited for: 3 -> 3; matrix products, arithmetic and copies ran while one was open for 8% -> 7% of each run, Pallas kernels for 23% -> 21%
where the time goes in v13:
time: 76.4 us; the launch traced here: 75.8 us
  waiting for transfers between devices  28.8 us (38%)
  Pallas kernels  22.8 us (30%)
  starting transfers between devices  15.8 us (21%)
  local copies, waits for them, and re-layouts  7.63 us (10%)
    ppermute x4, waiting for transfers between devices, shifted(): return lax.ppermute(value, axis, pairs)  27.3 us
    pallas_call x3, Pallas kernels, attend_half(): pl.pallas_call(kernel, out_shape=jax.ShapeDtypeStruct((span, out_cols), j...  22.8 us
    ppermute x4, starting transfers between devices, shifted(): return lax.ppermute(value, axis, pairs)  12.7 us
    optimization_barrier x1, local copies, waits for them, and re-layouts, body(): queries, third = lax.optimization_barrier((queries, third))  3.93 us
    ppermute x1, starting transfers between devices, body(): lax.ppermute(jnp.where(myself % 2 == 0, first, third), 'ctx', pairs)  3.14 us
    dynamic_update_slice x2, local copies, waits for them, and re-layouts, body(): lax.dynamic_update_slice(out, arrived[j], (0, (1 - half) * width + j * pe...  1.65 us
  transfers between devices with their start and end apart: 5, of which 3 were waited for; matrix products, arithmetic and copies ran while one was open for 7% of the time, Pallas kernels for 21%

profile of v13, /device:TPU:1, one launch (start us, length us, event | category | flops | bytes accessed | tf_op | source)
XLA Modules:
  0.0 75.8 jit_solution(14093370896788249326)
XLA Ops:
  0.0 1.2 %reshape.3.refs_0_ = bf16[2,256,512]{2,1,0:T(8,128)(2,1)S(1)} reshape(bf16[2,256,4,128]{3,2,1,0:T(4,128)(2,1)} %param.4) | data formatting | bytes 1048576 | tf_op jit(solution)/shard_map/reshape | solution.py:145
  1.2 0.0 copy-start
  1.3 4.6 %collective-permute-start.1 = (bf16[2,256,512]{2,1,0:T(8,128)(2,1)S(1)}, bf16[2,256,512]{2,1,0:T(8,128)(2,1)S(1)}, u32[]{:S(2)}, u32[]{:S(2)}) collective-permute-start(bf16[2,256,512]{2,1,0:T(8,128)(2,1)S(1)} %reshape.3.refs_0_), channel_id=1, source_target_pairs={{0,6},{2,8},{4,10},{6,12},{8,14},{10,16},{12,18},{14,20},{16,22},{... | collective-permute-start | bytes 1572872 | tf_op jit(solution)/shard_map/ppermute | solution.py:16
  5.9 2.8 %collective-permute-start = (bf16[2,256,512]{2,1,0:T(8,128)(2,1)S(1)}, bf16[2,256,512]{2,1,0:T(8,128)(2,1)S(1)}, u32[]{:S(2)}, u32[]{:S(2)}) collective-permute-start(bf16[2,256,512]{2,1,0:T(8,128)(2,1)S(1)} %reshape.3.refs_0_), channel_id=1, source_target_pairs={{0,2},{2,4},{4,6},{6,8},{8,10},{10,12},{12,14},{14,16},{16,18},{18... | collective-permute-start | bytes 1572872 | tf_op jit(solution)/shard_map/ppermute | solution.py:16
  8.7 0.5 compare_select_fusion
  9.2 20.7 %collective-permute-done.1.refs_3_ = bf16[2,256,512]{2,1,0:T(8,128)(2,1)S(1)} collective-permute-done((bf16[2,256,512]{2,1,0:T(8,128)(2,1)S(1)}, bf16[2,256,512]{2,1,0:T(8,128)(2,1)S(1)}, u32[]{:S(2)}, u32[]{:S(2)}) %collective-permute-start.1) | collective-permute-done | bytes 524320 | tf_op jit(solution)/shard_map/ppermute | solution.py:16
  29.9 3.9 %copy.6 = bf16[256,32,128]{2,0,1:T(8,128)(2,1)} copy(bf16[256,32,128]{2,1,0:T(8,128)(2,1)} %param.3) | data formatting | bytes 4194304 | tf_op jit(solution)/shard_map/optimization_barrier | solution.py:148
  33.8 0.0 copy-done
  33.8 0.0 collective-permute-done.refs_1_
  33.8 0.0 copy-done.1
  33.8 0.1 broadcast_select_fusion
  33.9 3.1 %collective-permute-start.2 = (bf16[2,256,512]{2,1,0:T(8,128)(2,1)S(1)}, bf16[2,256,512]{2,1,0:T(8,128)(2,1)S(1)}, u32[]{:S(2)}, u32[]{:S(2)}) collective-permute-start(bf16[2,256,512]{2,1,0:T(8,128)(2,1)S(1)} %broadcast_select_fusion), channel_id=1, source_target_pairs={{0,2},{2,0},{4,6},{6,4},{8,10},{10,8},{12,14},{14,12},{16,18},{18,... | collective-permute-start | bytes 1572872 | tf_op jit(solution)/shard_map/ppermute | solution.py:155
  37.1 1.5 %collective-permute-done.2.refs_2_ = bf16[2,256,512]{2,1,0:T(8,128)(2,1)S(1)} collective-permute-done((bf16[2,256,512]{2,1,0:T(8,128)(2,1)S(1)}, bf16[2,256,512]{2,1,0:T(8,128)(2,1)S(1)}, u32[]{:S(2)}, u32[]{:S(2)}) %collective-permute-start.2) | collective-permute-done | bytes 524320 | tf_op jit(solution)/shard_map/ppermute | solution.py:155
  38.6 0.0 copy-done.2
  38.6 0.8 %copy-done.3 = bf16[2,256,512]{2,1,0:T(8,128)(2,1)} copy-done((bf16[2,256,512]{2,1,0:T(8,128)(2,1)}, bf16[2,256,512]{2,1,0:T(8,128)(2,1)S(1)}, u32[]{:S(2)}) %copy-start.3) | copy-done | bytes 524312
  39.4 7.2 %shard_map.38 = bf16[128,2048]{1,0:T(8,128)(2,1)} custom-call(s32[512]{0:T(512)} %table_ref.5, s32[2]{0:T(128)} %get-tuple-element.16.where_ref, bf16[32,256,128]{2,1,0:T(8,128)(2,1)} %bitcast.3, bf16[2,256,512]{2,1,0:T(8,128)(2,1)} %copy-done, bf16[2,256,512]{2,1,0:T(8,128)(2,1)} %copy-done.2, bf16[2,256,512]{2,1,0:T(8,128)(2,1)} %copy-done.3, ...), custom_call_target="tpu_custom_call" | custom-call | flops 1073741824 | bytes 2097152 | tf_op jit(solution)/shard_map/pallas_call | solution.py:108
  46.6 2.7 %collective-permute-start.3 = (bf16[128,2048]{1,0:T(8,128)(2,1)}, bf16[128,2048]{1,0:T(8,128)(2,1)S(1)}, u32[]{:S(2)}, u32[]{:S(2)}) collective-permute-start(bf16[128,2048]{1,0:T(8,128)(2,1)} %shard_map.38), channel_id=1, source_target_pairs={{0,1},{1,0},{2,3},{3,2},{4,5},{5,4},{6,7},{7,6},{8,9},{9,8},{10,11... | collective-permute-start | bytes 1572872 | tf_op jit(solution)/shard_map/ppermute | solution.py:16
  49.2 7.2 %shard_map.39 = bf16[128,2048]{1,0:T(8,128)(2,1)} custom-call(s32[512]{0:T(512)} %table_ref.5, s32[2]{0:T(128)} %get-tuple-element.16.where_ref, bf16[32,256,128]{2,1,0:T(8,128)(2,1)} %bitcast.4, bf16[2,256,512]{2,1,0:T(8,128)(2,1)} %copy-done, bf16[2,256,512]{2,1,0:T(8,128)(2,1)} %copy-done.2, bf16[2,256,512]{2,1,0:T(8,128)(2,1)} %copy-done.3, ...), custom_call_target="tpu_custom_call" | custom-call | flops 1073741824 | bytes 2097152 | tf_op jit(solution)/shard_map/pallas_call | solution.py:108
  56.4 2.6 %collective-permute-start.4 = (bf16[128,2048]{1,0:T(8,128)(2,1)}, bf16[128,2048]{1,0:T(8,128)(2,1)S(1)}, u32[]{:S(2)}, u32[]{:S(2)}) collective-permute-start(bf16[128,2048]{1,0:T(8,128)(2,1)} %shard_map.39), channel_id=1, source_target_pairs={{0,1},{1,0},{2,3},{3,2},{4,5},{5,4},{6,7},{7,6},{8,9},{9,8},{10,11... | collective-permute-start | bytes 1572872 | tf_op jit(solution)/shard_map/ppermute | solution.py:16
  59.0 8.5 %shard_map.37 = bf16[128,8192]{1,0:T(8,128)(2,1)} custom-call(s32[512]{0:T(512)} %table_ref.5, s32[2]{0:T(128)} %get-tuple-element.12.where_ref, bf16[32,256,128]{2,1,0:T(8,128)(2,1)} %bitcast.5, bf16[2,256,512]{2,1,0:T(8,128)(2,1)} %copy-done, bf16[2,256,512]{2,1,0:T(8,128)(2,1)} %copy-done.2, bf16[2,256,512]{2,1,0:T(8,128)(2,1)} %copy-done.3, ...), custom_call_target="tpu_custom_call" | custom-call | flops 2147483648 | bytes 4194304 | tf_op jit(solution)/shard_map/pallas_call | solution.py:108
  67.5 0.0 collective-permute-done.3
  67.5 0.8 %constant_dynamic-update-slice_fusion.1 = bf16[128,8192]{1,0:T(8,128)(2,1)} fusion(bf16[128,8192]{1,0:T(8,128)(2,1)} %shard_map.37, bf16[128,2048]{1,0:T(8,128)(2,1)S(1)} %collective-permute-done.3, s32[]{:T(128)S(6)} %select_n.33), kind=kLoop, calls=%fused_computation.5 | loop fusion | bytes 1048580 | tf_op jit(solution)/shard_map/dynamic_update_slice | solution.py:174
  68.3 6.6 %collective-permute-done.4 = bf16[128,2048]{1,0:T(8,128)(2,1)S(1)} collective-permute-done((bf16[128,2048]{1,0:T(8,128)(2,1)}, bf16[128,2048]{1,0:T(8,128)(2,1)S(1)}, u32[]{:S(2)}, u32[]{:S(2)}) %collective-permute-start.4) | collective-permute-done | bytes 524320 | tf_op jit(solution)/shard_map/ppermute | solution.py:16
  75.0 0.8 %constant_dynamic-update-slice_fusion = bf16[128,8192]{1,0:T(8,128)(2,1)} fusion(bf16[128,8192]{1,0:T(8,128)(2,1)} %constant_dynamic-update-slice_fusion.1, bf16[128,2048]{1,0:T(8,128)(2,1)S(1)} %collective-permute-done.4, s32[]{:T(128)S(6)} %select_n.34), kind=kLoop, calls=%fused_computation.4 | loop fusion | bytes 1048580 | tf_op jit(solution)/shard_map/dynamic_update_slice | solution.py:174
  (3 shorter events, 0.0 us)
Async XLA Ops:
  1.2 32.6 %copy-start = (bf16[2,256,512]{2,1,0:T(8,128)(2,1)}, bf16[2,256,512]{2,1,0:T(8,128)(2,1)S(1)}, u32[]{:S(2)}) copy-start(bf16[2,256,512]{2,1,0:T(8,128)(2,1)S(1)} %reshape.3.refs_0_) | copy-start | bytes 1572868
  1.3 28.6 %collective-permute-start.1 = (bf16[2,256,512]{2,1,0:T(8,128)(2,1)S(1)}, bf16[2,256,512]{2,1,0:T(8,128)(2,1)S(1)}, u32[]{:S(2)}, u32[]{:S(2)}) collective-permute-start(bf16[2,256,512]{2,1,0:T(8,128)(2,1)S(1)} %reshape.3.refs_0_), channel_id=1, source_target_pairs={{0,6},{2,8},{4,10},{6,12},{8,14},{10,16},{12,18},{14,20},{16,22},{... | collective-permute-start | bytes 1572872 | tf_op jit(solution)/shard_map/ppermute | solution.py:16
  5.9 28.0 %collective-permute-start = (bf16[2,256,512]{2,1,0:T(8,128)(2,1)S(1)}, bf16[2,256,512]{2,1,0:T(8,128)(2,1)S(1)}, u32[]{:S(2)}, u32[]{:S(2)}) collective-permute-start(bf16[2,256,512]{2,1,0:T(8,128)(2,1)S(1)} %reshape.3.refs_0_), channel_id=1, source_target_pairs={{0,2},{2,4},{4,6},{6,8},{8,10},{10,12},{12,14},{14,16},{16,18},{18... | collective-permute-start | bytes 1572872 | tf_op jit(solution)/shard_map/ppermute | solution.py:16
  29.9 3.9 %copy-start.1 = (bf16[2,256,512]{2,1,0:T(8,128)(2,1)}, bf16[2,256,512]{2,1,0:T(8,128)(2,1)S(1)}, u32[]{:S(2)}) copy-start(bf16[2,256,512]{2,1,0:T(8,128)(2,1)S(1)} %collective-permute-done.1.refs_3_) | copy-start | bytes 1572868
  33.8 4.7 %copy-start.2 = (bf16[2,256,512]{2,1,0:T(8,128)(2,1)}, bf16[2,256,512]{2,1,0:T(8,128)(2,1)S(1)}, u32[]{:S(2)}) copy-start(bf16[2,256,512]{2,1,0:T(8,128)(2,1)S(1)} %collective-permute-done.refs_1_) | copy-start | bytes 1572868
  33.9 4.7 %collective-permute-start.2 = (bf16[2,256,512]{2,1,0:T(8,128)(2,1)S(1)}, bf16[2,256,512]{2,1,0:T(8,128)(2,1)S(1)}, u32[]{:S(2)}, u32[]{:S(2)}) collective-permute-start(bf16[2,256,512]{2,1,0:T(8,128)(2,1)S(1)} %broadcast_select_fusion), channel_id=1, source_target_pairs={{0,2},{2,0},{4,6},{6,4},{8,10},{10,8},{12,14},{14,12},{16,18},{18,... | collective-permute-start | bytes 1572872 | tf_op jit(solution)/shard_map/ppermute | solution.py:155
  38.6 0.8 %copy-start.3 = (bf16[2,256,512]{2,1,0:T(8,128)(2,1)}, bf16[2,256,512]{2,1,0:T(8,128)(2,1)S(1)}, u32[]{:S(2)}) copy-start(bf16[2,256,512]{2,1,0:T(8,128)(2,1)S(1)} %collective-permute-done.2.refs_2_) | copy-start | bytes 1572868
  46.6 20.9 %collective-permute-start.3 = (bf16[128,2048]{1,0:T(8,128)(2,1)}, bf16[128,2048]{1,0:T(8,128)(2,1)S(1)}, u32[]{:S(2)}, u32[]{:S(2)}) collective-permute-start(bf16[128,2048]{1,0:T(8,128)(2,1)} %shard_map.38), channel_id=1, source_target_pairs={{0,1},{1,0},{2,3},{3,2},{4,5},{5,4},{6,7},{7,6},{8,9},{9,8},{10,11... | collective-permute-start | bytes 1572872 | tf_op jit(solution)/shard_map/ppermute | solution.py:16
  56.4 18.5 %collective-permute-start.4 = (bf16[128,2048]{1,0:T(8,128)(2,1)}, bf16[128,2048]{1,0:T(8,128)(2,1)S(1)}, u32[]{:S(2)}, u32[]{:S(2)}) collective-permute-start(bf16[128,2048]{1,0:T(8,128)(2,1)} %shard_map.39), channel_id=1, source_target_pairs={{0,1},{1,0},{2,3},{3,2},{4,5},{5,4},{6,7},{7,6},{8,9},{9,8},{10,11... | collective-permute-start | bytes 1572872 | tf_op jit(solution)/shard_map/ppermute | solution.py:16

commit v14 on v13

--- a/solution.py
+++ b/solution.py
@@ -19,7 +19,7 @@
 def attend_kernel(table_ref, where_ref, q_ref, *refs, span, group, head_size, steps, scale):
     kv_refs = refs[:steps]
     o_ref = refs[steps]
-    s_ref, mx_ref, sm_ref, p_ref, v_ref = refs[steps + 1 :]
+    s_ref, mx_ref, sm_ref, p_ref, v_ref, qf_ref = refs[steps + 1 :]
     cycle = table_ref.shape[0] // 2
     half = where_ref[0]
     myself = where_ref[1]
@@ -29,10 +29,13 @@
     def key_span(b, t):
         return table_ref[2 * ((myself + cycle - b) % cycle) + t]
 
+    for h in range(group):
+        qf_ref[h * span : (h + 1) * span, :] = q_ref[:, h, :]
+
     def run(tiles, always, diag):
         def score(idx, b, t, first):
             k = kv_refs[b][0, t * span : (t + 1) * span, :]
-            q = q_ref[...].reshape(n, head_size)
+            q = qf_ref[...]
             s = jnp.dot(q, k.T, preferred_element_type=jnp.float32) * scale
             if idx == diag:
                 row = lax.broadcasted_iota(jnp.int32, (n, span), 0) % span
@@ -101,7 +104,7 @@
         steps=steps,
         scale=1.0 / head_size**0.5,
     )
-    q_spec = pl.BlockSpec((group, span, head_size), lambda g, tb, w: (g + first, w[0], 0))
+    q_spec = pl.BlockSpec((span, group, head_size), lambda g, tb, w: (w[0], g + first, 0))
     kv_spec = pl.BlockSpec((2, 2 * span, head_size), lambda g, tb, w: (0, 0, g + first))
     o_spec = pl.BlockSpec((span, width), lambda g, tb, w: (0, out_block0(w) + g))
     flops = 4 * span * 2 * span * steps * head_size * group * count
@@ -119,6 +122,7 @@
                 pltpu.VMEM((group * span, span), jnp.float32),
                 pltpu.VMEM((group * span, 2 * steps * span), jnp.bfloat16),
                 pltpu.VMEM((2 * steps * span, head_size), jnp.bfloat16),
+                pltpu.VMEM((group * span, head_size), jnp.bfloat16),
             ],
         ),
         compiler_params=pltpu.CompilerParams(dimension_semantics=("arbitrary",)),
@@ -145,8 +149,7 @@
     own = key_value.reshape(2, rows, kv_here * head_size)
     first = shifted(own, "ctx", 1)
     third = shifted(own, "ctx", 3)
-    queries, third = lax.optimization_barrier((queries, third))
-    q2 = jnp.transpose(queries, (1, 0, 2))
+    q2 = queries
     lanes = jnp.arange(2, dtype=jnp.int32)
     sent_where = jnp.where(lanes == 0, 1 - half, myself).astype(jnp.int32)
     kept_where = jnp.where(lanes == 0, half, myself).astype(jnp.int32)

time: 76.4 us -> 79.2 us (1.037)
  the two profiles are of different devices: /device:TPU:1 before, /device:TPU:7 now
where the time goes in v14:
time: 79.2 us; the launch traced here: 78.7 us
  Pallas kernels  29.7 us (38%)
  starting transfers between devices  28.2 us (36%)
  waiting for transfers between devices  16.3 us (21%)
  local copies, waits for them, and re-layouts  3.74 us (5%)
    pallas_call x3, Pallas kernels, attend_half(): pl.pallas_call(kernel, out_shape=jax.ShapeDtypeStruct((span, out_cols), j...  29.7 us
    ppermute x4, starting transfers between devices, shifted(): return lax.ppermute(value, axis, pairs)  15.6 us
    ppermute x4, waiting for transfers between devices, shifted(): return lax.ppermute(value, axis, pairs)  14.8 us
    ppermute x1, starting transfers between devices, body(): lax.ppermute(jnp.where(myself % 2 == 0, first, third), 'ctx', pairs)  12.6 us
    dynamic_update_slice x2, local copies, waits for them, and re-layouts, body(): lax.dynamic_update_slice(out, arrived[j], (0, (1 - half) * width + j * pe...  1.67 us
  transfers between devices with their start and end apart: 5, of which 3 were waited for; matrix products, arithmetic and copies ran while one was open for 2% of the time, Pallas kernels for 29%

profile of v14, /device:TPU:7, one launch (start us, length us, event | category | flops | bytes accessed | tf_op | source)
XLA Modules:
  0.0 78.7 jit_solution(4013440460326824203)
XLA Ops:
  0.0 1.2 %reshape.3.refs_0_ = bf16[2,256,512]{2,1,0:T(8,128)(2,1)S(1)} reshape(bf16[2,256,4,128]{3,2,1,0:T(4,128)(2,1)} %param.4) | data formatting | bytes 1048576 | tf_op jit(solution)/shard_map/reshape | solution.py:149
  1.2 0.0 copy-start
  1.3 4.0 %collective-permute-start = (bf16[2,256,512]{2,1,0:T(8,128)(2,1)S(1)}, bf16[2,256,512]{2,1,0:T(8,128)(2,1)S(1)}, u32[]{:S(2)}, u32[]{:S(2)}) collective-permute-start(bf16[2,256,512]{2,1,0:T(8,128)(2,1)S(1)} %reshape.3.refs_0_), channel_id=1, source_target_pairs={{0,2},{2,4},{4,6},{6,8},{8,10},{10,12},{12,14},{14,16},{16,18},{18... | collective-permute-start | bytes 1572872 | tf_op jit(solution)/shard_map/ppermute | solution.py:16
  5.3 1.9 %collective-permute-start.1 = (bf16[2,256,512]{2,1,0:T(8,128)(2,1)S(1)}, bf16[2,256,512]{2,1,0:T(8,128)(2,1)S(1)}, u32[]{:S(2)}, u32[]{:S(2)}) collective-permute-start(bf16[2,256,512]{2,1,0:T(8,128)(2,1)S(1)} %reshape.3.refs_0_), channel_id=1, source_target_pairs={{0,6},{2,8},{4,10},{6,12},{8,14},{10,16},{12,18},{14,20},{16,22},{... | collective-permute-start | bytes 1572872 | tf_op jit(solution)/shard_map/ppermute | solution.py:16
  7.2 0.6 compare_select_fusion
  7.8 5.7 %collective-permute-done.refs_1_ = bf16[2,256,512]{2,1,0:T(8,128)(2,1)S(1)} collective-permute-done((bf16[2,256,512]{2,1,0:T(8,128)(2,1)S(1)}, bf16[2,256,512]{2,1,0:T(8,128)(2,1)S(1)}, u32[]{:S(2)}, u32[]{:S(2)}) %collective-permute-start) | collective-permute-done | bytes 524320 | tf_op jit(solution)/shard_map/ppermute | solution.py:16
  13.5 0.0 copy-start.1
  13.5 9.1 %collective-permute-done.1.refs_3_ = bf16[2,256,512]{2,1,0:T(8,128)(2,1)S(1)} collective-permute-done((bf16[2,256,512]{2,1,0:T(8,128)(2,1)S(1)}, bf16[2,256,512]{2,1,0:T(8,128)(2,1)S(1)}, u32[]{:S(2)}, u32[]{:S(2)}) %collective-permute-start.1) | collective-permute-done | bytes 524320 | tf_op jit(solution)/shard_map/ppermute | solution.py:16
  22.6 0.1 broadcast_select_fusion
  22.7 12.6 %collective-permute-start.2 = (bf16[2,256,512]{2,1,0:T(8,128)(2,1)S(1)}, bf16[2,256,512]{2,1,0:T(8,128)(2,1)S(1)}, u32[]{:S(2)}, u32[]{:S(2)}) collective-permute-start(bf16[2,256,512]{2,1,0:T(8,128)(2,1)S(1)} %broadcast_select_fusion), channel_id=1, source_target_pairs={{0,2},{2,0},{4,6},{6,4},{8,10},{10,8},{12,14},{14,12},{16,18},{18,... | collective-permute-start | bytes 1572872 | tf_op jit(solution)/shard_map/ppermute | solution.py:158
  35.3 1.5 %collective-permute-done.2.refs_2_ = bf16[2,256,512]{2,1,0:T(8,128)(2,1)S(1)} collective-permute-done((bf16[2,256,512]{2,1,0:T(8,128)(2,1)S(1)}, bf16[2,256,512]{2,1,0:T(8,128)(2,1)S(1)}, u32[]{:S(2)}, u32[]{:S(2)}) %collective-permute-start.2) | collective-permute-done | bytes 524320 | tf_op jit(solution)/shard_map/ppermute | solution.py:158
  36.8 0.0 copy-done
  36.8 0.0 copy-done.1
  36.8 0.0 copy-done.2
  36.8 0.8 %copy-done.3 = bf16[2,256,512]{2,1,0:T(8,128)(2,1)} copy-done((bf16[2,256,512]{2,1,0:T(8,128)(2,1)}, bf16[2,256,512]{2,1,0:T(8,128)(2,1)S(1)}, u32[]{:S(2)}) %copy-start.3) | copy-done | bytes 524312
  37.6 6.9 %shard_map.38 = bf16[128,2048]{1,0:T(8,128)(2,1)} custom-call(s32[512]{0:T(512)} %table_ref.5, s32[2]{0:T(128)} %get-tuple-element.12.where_ref, bf16[256,32,128]{2,1,0:T(8,128)(2,1)} %q_ref.2, bf16[2,256,512]{2,1,0:T(8,128)(2,1)} %copy-done, bf16[2,256,512]{2,1,0:T(8,128)(2,1)} %copy-done.1, bf16[2,256,512]{2,1,0:T(8,128)(2,1)} %copy-done.3, ...), custom_call_target="tpu_custom_call" | custom-call | flops 1073741824 | bytes 2097152 | tf_op jit(solution)/shard_map/pallas_call | solution.py:111
  44.5 5.3 %collective-permute-start.3 = (bf16[128,2048]{1,0:T(8,128)(2,1)}, bf16[128,2048]{1,0:T(8,128)(2,1)S(1)}, u32[]{:S(2)}, u32[]{:S(2)}) collective-permute-start(bf16[128,2048]{1,0:T(8,128)(2,1)} %shard_map.38), channel_id=1, source_target_pairs={{0,1},{1,0},{2,3},{3,2},{4,5},{5,4},{6,7},{7,6},{8,9},{9,8},{10,11... | collective-permute-start | bytes 1572872 | tf_op jit(solution)/shard_map/ppermute | solution.py:16
  49.9 7.0 %shard_map.39 = bf16[128,2048]{1,0:T(8,128)(2,1)} custom-call(s32[512]{0:T(512)} %table_ref.5, s32[2]{0:T(128)} %get-tuple-element.12.where_ref, bf16[256,32,128]{2,1,0:T(8,128)(2,1)} %q_ref.2, bf16[2,256,512]{2,1,0:T(8,128)(2,1)} %copy-done, bf16[2,256,512]{2,1,0:T(8,128)(2,1)} %copy-done.1, bf16[2,256,512]{2,1,0:T(8,128)(2,1)} %copy-done.3, ...), custom_call_target="tpu_custom_call" | custom-call | flops 1073741824 | bytes 2097152 | tf_op jit(solution)/shard_map/pallas_call | solution.py:111
  56.8 4.4 %collective-permute-start.4 = (bf16[128,2048]{1,0:T(8,128)(2,1)}, bf16[128,2048]{1,0:T(8,128)(2,1)S(1)}, u32[]{:S(2)}, u32[]{:S(2)}) collective-permute-start(bf16[128,2048]{1,0:T(8,128)(2,1)} %shard_map.39), channel_id=1, source_target_pairs={{0,1},{1,0},{2,3},{3,2},{4,5},{5,4},{6,7},{7,6},{8,9},{9,8},{10,11... | collective-permute-start | bytes 1572872 | tf_op jit(solution)/shard_map/ppermute | solution.py:16
  61.2 15.8 %shard_map.37 = bf16[128,8192]{1,0:T(8,128)(2,1)} custom-call(s32[512]{0:T(512)} %table_ref.5, s32[2]{0:T(128)} %get-tuple-element.9.where_ref, bf16[256,32,128]{2,1,0:T(8,128)(2,1)} %q_ref.2, bf16[2,256,512]{2,1,0:T(8,128)(2,1)} %copy-done, bf16[2,256,512]{2,1,0:T(8,128)(2,1)} %copy-done.1, bf16[2,256,512]{2,1,0:T(8,128)(2,1)} %copy-done.3, ...), custom_call_target="tpu_custom_call" | custom-call | flops 2147483648 | bytes 4194304 | tf_op jit(solution)/shard_map/pallas_call | solution.py:111
  77.1 0.0 collective-permute-done.3
  77.1 0.8 %constant_dynamic-update-slice_fusion.1 = bf16[128,8192]{1,0:T(8,128)(2,1)} fusion(bf16[128,8192]{1,0:T(8,128)(2,1)} %shard_map.37, bf16[128,2048]{1,0:T(8,128)(2,1)S(1)} %collective-permute-done.3, s32[]{:T(128)S(6)} %select_n.33), kind=kLoop, calls=%fused_computation.4 | loop fusion | bytes 1048580 | tf_op jit(solution)/shard_map/dynamic_update_slice | solution.py:177
  77.9 0.0 collective-permute-done.4
  77.9 0.8 %constant_dynamic-update-slice_fusion = bf16[128,8192]{1,0:T(8,128)(2,1)} fusion(bf16[128,8192]{1,0:T(8,128)(2,1)} %constant_dynamic-update-slice_fusion.1, bf16[128,2048]{1,0:T(8,128)(2,1)S(1)} %collective-permute-done.4, s32[]{:T(128)S(6)} %select_n.34), kind=kLoop, calls=%fused_computation.3 | loop fusion | bytes 1048580 | tf_op jit(solution)/shard_map/dynamic_update_slice | solution.py:177
  (2 shorter events, 0.0 us)
Async XLA Ops:
  1.2 35.6 %copy-start = (bf16[2,256,512]{2,1,0:T(8,128)(2,1)}, bf16[2,256,512]{2,1,0:T(8,128)(2,1)S(1)}, u32[]{:S(2)}) copy-start(bf16[2,256,512]{2,1,0:T(8,128)(2,1)S(1)} %reshape.3.refs_0_) | copy-start | bytes 1572868
  1.3 12.3 %collective-permute-start = (bf16[2,256,512]{2,1,0:T(8,128)(2,1)S(1)}, bf16[2,256,512]{2,1,0:T(8,128)(2,1)S(1)}, u32[]{:S(2)}, u32[]{:S(2)}) collective-permute-start(bf16[2,256,512]{2,1,0:T(8,128)(2,1)S(1)} %reshape.3.refs_0_), channel_id=1, source_target_pairs={{0,2},{2,4},{4,6},{6,8},{8,10},{10,12},{12,14},{14,16},{16,18},{18... | collective-permute-start | bytes 1572872 | tf_op jit(solution)/shard_map/ppermute | solution.py:16
  5.3 17.3 %collective-permute-start.1 = (bf16[2,256,512]{2,1,0:T(8,128)(2,1)S(1)}, bf16[2,256,512]{2,1,0:T(8,128)(2,1)S(1)}, u32[]{:S(2)}, u32[]{:S(2)}) collective-permute-start(bf16[2,256,512]{2,1,0:T(8,128)(2,1)S(1)} %reshape.3.refs_0_), channel_id=1, source_target_pairs={{0,6},{2,8},{4,10},{6,12},{8,14},{10,16},{12,18},{14,20},{16,22},{... | collective-permute-start | bytes 1572872 | tf_op jit(solution)/shard_map/ppermute | solution.py:16
  13.5 23.3 %copy-start.1 = (bf16[2,256,512]{2,1,0:T(8,128)(2,1)}, bf16[2,256,512]{2,1,0:T(8,128)(2,1)S(1)}, u32[]{:S(2)}) copy-start(bf16[2,256,512]{2,1,0:T(8,128)(2,1)S(1)} %collective-permute-done.refs_1_) | copy-start | bytes 1572868
  22.6 14.2 %copy-start.2 = (bf16[2,256,512]{2,1,0:T(8,128)(2,1)}, bf16[2,256,512]{2,1,0:T(8,128)(2,1)S(1)}, u32[]{:S(2)}) copy-start(bf16[2,256,512]{2,1,0:T(8,128)(2,1)S(1)} %collective-permute-done.1.refs_3_) | copy-start | bytes 1572868
  22.7 14.1 %collective-permute-start.2 = (bf16[2,256,512]{2,1,0:T(8,128)(2,1)S(1)}, bf16[2,256,512]{2,1,0:T(8,128)(2,1)S(1)}, u32[]{:S(2)}, u32[]{:S(2)}) collective-permute-start(bf16[2,256,512]{2,1,0:T(8,128)(2,1)S(1)} %broadcast_select_fusion), channel_id=1, source_target_pairs={{0,2},{2,0},{4,6},{6,4},{8,10},{10,8},{12,14},{14,12},{16,18},{18,... | collective-permute-start | bytes 1572872 | tf_op jit(solution)/shard_map/ppermute | solution.py:158
  36.8 0.8 %copy-start.3 = (bf16[2,256,512]{2,1,0:T(8,128)(2,1)}, bf16[2,256,512]{2,1,0:T(8,128)(2,1)S(1)}, u32[]{:S(2)}) copy-start(bf16[2,256,512]{2,1,0:T(8,128)(2,1)S(1)} %collective-permute-done.2.refs_2_) | copy-start | bytes 1572868
  44.5 32.5 %collective-permute-start.3 = (bf16[128,2048]{1,0:T(8,128)(2,1)}, bf16[128,2048]{1,0:T(8,128)(2,1)S(1)}, u32[]{:S(2)}, u32[]{:S(2)}) collective-permute-start(bf16[128,2048]{1,0:T(8,128)(2,1)} %shard_map.38), channel_id=1, source_target_pairs={{0,1},{1,0},{2,3},{3,2},{4,5},{5,4},{6,7},{7,6},{8,9},{9,8},{10,11... | collective-permute-start | bytes 1572872 | tf_op jit(solution)/shard_map/ppermute | solution.py:16
  56.8 21.1 %collective-permute-start.4 = (bf16[128,2048]{1,0:T(8,128)(2,1)}, bf16[128,2048]{1,0:T(8,128)(2,1)S(1)}, u32[]{:S(2)}, u32[]{:S(2)}) collective-permute-start(bf16[128,2048]{1,0:T(8,128)(2,1)} %shard_map.39), channel_id=1, source_target_pairs={{0,1},{1,0},{2,3},{3,2},{4,5},{5,4},{6,7},{7,6},{8,9},{9,8},{10,11... | collective-permute-start | bytes 1572872 | tf_op jit(solution)/shard_map/ppermute | solution.py:16

commit v15 on v13

--- a/solution.py
+++ b/solution.py
@@ -44,8 +44,8 @@
             else:
                 mx_ref[...] = jnp.maximum(mx_ref[...], s)
 
-        def weigh(idx, first):
-            p = jnp.exp(s_ref[idx] - mx_ref[...])
+        def weigh(idx, first, m):
+            p = jnp.exp(s_ref[idx] - m)
             p_ref[:, idx * span : (idx + 1) * span] = p.astype(jnp.bfloat16)
             if first:
                 sm_ref[...] = p
@@ -63,15 +63,14 @@
                 pl.when(key_span(b, t) < query_span)(functools.partial(score, idx, b, t, False))
 
         m = jnp.max(mx_ref[...], axis=1, keepdims=True)
-        mx_ref[...] = jnp.broadcast_to(m, (n, span))
 
-        weigh(0, True)
+        weigh(0, True, m)
         for idx, (b, t) in enumerate(tiles[1:], start=1):
             if always[idx]:
-                weigh(idx, False)
+                weigh(idx, False, m)
             else:
                 visible = key_span(b, t) < query_span
-                pl.when(visible)(functools.partial(weigh, idx, False))
+                pl.when(visible)(functools.partial(weigh, idx, False, m))
                 pl.when(jnp.logical_not(visible))(functools.partial(hide, idx))
         for idx, (b, t) in enumerate(tiles):
             v_ref[idx * span : (idx + 1) * span, :] = kv_refs[b][1, t * span : (t + 1) * span, :]

time: 76.4 us -> 76.9 us (level)
  Pallas kernels: 22.8 us -> 26.3 us
  waiting for transfers between devices: 28.8 us -> 26.5 us
    pallas_call x3, Pallas kernels: 22.8 us -> 26.3 us  [attend_half(): pl.pallas_call(kernel, out_shape=jax.ShapeDtypeStruct((span, out_cols), j...]
    ppermute x4, waiting for transfers between devices: 27.3 us -> 24.9 us  [shifted(): return lax.ppermute(value, axis, pairs)]
  transfers between devices with their start and end apart: 5 -> 5, of which waited for: 3 -> 3; matrix products, arithmetic and copies ran while one was open for 7% -> 7% of each run, Pallas kernels for 21% -> 24%
where the time goes in v15:
time: 76.9 us; the launch traced here: 76.4 us
  waiting for transfers between devices  26.5 us (34%)
  Pallas kernels  26.3 us (34%)
  starting transfers between devices  15.3 us (20%)
  local copies, waits for them, and re-layouts  7.63 us (10%)
    pallas_call x3, Pallas kernels, attend_half(): pl.pallas_call(kernel, out_shape=jax.ShapeDtypeStruct((span, out_cols), j...  26.3 us
    ppermute x4, waiting for transfers between devices, shifted(): return lax.ppermute(value, axis, pairs)  24.9 us
    ppermute x4, starting transfers between devices, shifted(): return lax.ppermute(value, axis, pairs)  12.1 us
    optimization_barrier x1, local copies, waits for them, and re-layouts, body(): queries, third = lax.optimization_barrier((queries, third))  3.93 us
    ppermute x1, starting transfers between devices, body(): lax.ppermute(jnp.where(myself % 2 == 0, first, third), 'ctx', pairs)  3.14 us
    dynamic_update_slice x2, local copies, waits for them, and re-layouts, body(): lax.dynamic_update_slice(out, arrived[j], (0, (1 - half) * width + j * pe...  1.65 us
  transfers between devices with their start and end apart: 5, of which 3 were waited for; matrix products, arithmetic and copies ran while one was open for 7% of the time, Pallas kernels for 24%

profile of v15, /device:TPU:1, one launch (start us, length us, event | category | flops | bytes accessed | tf_op | source)
XLA Modules:
  0.0 76.4 jit_solution(2435471713800885838)
XLA Ops:
  0.0 1.2 %reshape.3.refs_0_ = bf16[2,256,512]{2,1,0:T(8,128)(2,1)S(1)} reshape(bf16[2,256,4,128]{3,2,1,0:T(4,128)(2,1)} %param.4) | data formatting | bytes 1048576 | tf_op jit(solution)/shard_map/reshape | solution.py:144
  1.2 0.0 copy-start
  1.3 4.6 %collective-permute-start.1 = (bf16[2,256,512]{2,1,0:T(8,128)(2,1)S(1)}, bf16[2,256,512]{2,1,0:T(8,128)(2,1)S(1)}, u32[]{:S(2)}, u32[]{:S(2)}) collective-permute-start(bf16[2,256,512]{2,1,0:T(8,128)(2,1)S(1)} %reshape.3.refs_0_), channel_id=1, source_target_pairs={{0,6},{2,8},{4,10},{6,12},{8,14},{10,16},{12,18},{14,20},{16,22},{... | collective-permute-start | bytes 1572872 | tf_op jit(solution)/shard_map/ppermute | solution.py:16
  5.9 2.8 %collective-permute-start = (bf16[2,256,512]{2,1,0:T(8,128)(2,1)S(1)}, bf16[2,256,512]{2,1,0:T(8,128)(2,1)S(1)}, u32[]{:S(2)}, u32[]{:S(2)}) collective-permute-start(bf16[2,256,512]{2,1,0:T(8,128)(2,1)S(1)} %reshape.3.refs_0_), channel_id=1, source_target_pairs={{0,2},{2,4},{4,6},{6,8},{8,10},{10,12},{12,14},{14,16},{16,18},{18... | collective-permute-start | bytes 1572872 | tf_op jit(solution)/shard_map/ppermute | solution.py:16
  8.7 0.5 compare_select_fusion
  9.2 20.7 %collective-permute-done.1.refs_3_ = bf16[2,256,512]{2,1,0:T(8,128)(2,1)S(1)} collective-permute-done((bf16[2,256,512]{2,1,0:T(8,128)(2,1)S(1)}, bf16[2,256,512]{2,1,0:T(8,128)(2,1)S(1)}, u32[]{:S(2)}, u32[]{:S(2)}) %collective-permute-start.1) | collective-permute-done | bytes 524320 | tf_op jit(solution)/shard_map/ppermute | solution.py:16
  29.9 3.9 %copy.6 = bf16[256,32,128]{2,0,1:T(8,128)(2,1)} copy(bf16[256,32,128]{2,1,0:T(8,128)(2,1)} %param.3) | data formatting | bytes 4194304 | tf_op jit(solution)/shard_map/optimization_barrier | solution.py:147
  33.8 0.0 copy-done
  33.8 0.0 collective-permute-done.refs_1_
  33.8 0.0 copy-done.1
  33.8 0.1 broadcast_select_fusion
  33.9 3.1 %collective-permute-start.2 = (bf16[2,256,512]{2,1,0:T(8,128)(2,1)S(1)}, bf16[2,256,512]{2,1,0:T(8,128)(2,1)S(1)}, u32[]{:S(2)}, u32[]{:S(2)}) collective-permute-start(bf16[2,256,512]{2,1,0:T(8,128)(2,1)S(1)} %broadcast_select_fusion), channel_id=1, source_target_pairs={{0,2},{2,0},{4,6},{6,4},{8,10},{10,8},{12,14},{14,12},{16,18},{18,... | collective-permute-start | bytes 1572872 | tf_op jit(solution)/shard_map/ppermute | solution.py:154
  37.1 1.5 %collective-permute-done.2.refs_2_ = bf16[2,256,512]{2,1,0:T(8,128)(2,1)S(1)} collective-permute-done((bf16[2,256,512]{2,1,0:T(8,128)(2,1)S(1)}, bf16[2,256,512]{2,1,0:T(8,128)(2,1)S(1)}, u32[]{:S(2)}, u32[]{:S(2)}) %collective-permute-start.2) | collective-permute-done | bytes 524320 | tf_op jit(solution)/shard_map/ppermute | solution.py:154
  38.6 0.0 copy-done.2
  38.6 0.8 %copy-done.3 = bf16[2,256,512]{2,1,0:T(8,128)(2,1)} copy-done((bf16[2,256,512]{2,1,0:T(8,128)(2,1)}, bf16[2,256,512]{2,1,0:T(8,128)(2,1)S(1)}, u32[]{:S(2)}) %copy-start.3) | copy-done | bytes 524312
  39.4 8.4 %shard_map.38 = bf16[128,2048]{1,0:T(8,128)(2,1)} custom-call(s32[512]{0:T(512)} %table_ref.5, s32[2]{0:T(128)} %get-tuple-element.16.where_ref, bf16[32,256,128]{2,1,0:T(8,128)(2,1)} %bitcast.3, bf16[2,256,512]{2,1,0:T(8,128)(2,1)} %copy-done, bf16[2,256,512]{2,1,0:T(8,128)(2,1)} %copy-done.2, bf16[2,256,512]{2,1,0:T(8,128)(2,1)} %copy-done.3, ...), custom_call_target="tpu_custom_call" | custom-call | flops 1073741824 | bytes 2097152 | tf_op jit(solution)/shard_map/pallas_call | solution.py:107
  47.7 2.1 %collective-permute-start.3 = (bf16[128,2048]{1,0:T(8,128)(2,1)}, bf16[128,2048]{1,0:T(8,128)(2,1)S(1)}, u32[]{:S(2)}, u32[]{:S(2)}) collective-permute-start(bf16[128,2048]{1,0:T(8,128)(2,1)} %shard_map.38), channel_id=1, source_target_pairs={{0,1},{1,0},{2,3},{3,2},{4,5},{5,4},{6,7},{7,6},{8,9},{9,8},{10,11... | collective-permute-start | bytes 1572872 | tf_op jit(solution)/shard_map/ppermute | solution.py:16
  49.8 8.3 %shard_map.39 = bf16[128,2048]{1,0:T(8,128)(2,1)} custom-call(s32[512]{0:T(512)} %table_ref.5, s32[2]{0:T(128)} %get-tuple-element.16.where_ref, bf16[32,256,128]{2,1,0:T(8,128)(2,1)} %bitcast.4, bf16[2,256,512]{2,1,0:T(8,128)(2,1)} %copy-done, bf16[2,256,512]{2,1,0:T(8,128)(2,1)} %copy-done.2, bf16[2,256,512]{2,1,0:T(8,128)(2,1)} %copy-done.3, ...), custom_call_target="tpu_custom_call" | custom-call | flops 1073741824 | bytes 2097152 | tf_op jit(solution)/shard_map/pallas_call | solution.py:107
  58.2 2.6 %collective-permute-start.4 = (bf16[128,2048]{1,0:T(8,128)(2,1)}, bf16[128,2048]{1,0:T(8,128)(2,1)S(1)}, u32[]{:S(2)}, u32[]{:S(2)}) collective-permute-start(bf16[128,2048]{1,0:T(8,128)(2,1)} %shard_map.39), channel_id=1, source_target_pairs={{0,1},{1,0},{2,3},{3,2},{4,5},{5,4},{6,7},{7,6},{8,9},{9,8},{10,11... | collective-permute-start | bytes 1572872 | tf_op jit(solution)/shard_map/ppermute | solution.py:16
  60.8 9.6 %shard_map.37 = bf16[128,8192]{1,0:T(8,128)(2,1)} custom-call(s32[512]{0:T(512)} %table_ref.5, s32[2]{0:T(128)} %get-tuple-element.12.where_ref, bf16[32,256,128]{2,1,0:T(8,128)(2,1)} %bitcast.5, bf16[2,256,512]{2,1,0:T(8,128)(2,1)} %copy-done, bf16[2,256,512]{2,1,0:T(8,128)(2,1)} %copy-done.2, bf16[2,256,512]{2,1,0:T(8,128)(2,1)} %copy-done.3, ...), custom_call_target="tpu_custom_call" | custom-call | flops 2147483648 | bytes 4194304 | tf_op jit(solution)/shard_map/pallas_call | solution.py:107
  70.4 0.0 collective-permute-done.3
  70.4 0.8 %constant_dynamic-update-slice_fusion.1 = bf16[128,8192]{1,0:T(8,128)(2,1)} fusion(bf16[128,8192]{1,0:T(8,128)(2,1)} %shard_map.37, bf16[128,2048]{1,0:T(8,128)(2,1)S(1)} %collective-permute-done.3, s32[]{:T(128)S(6)} %select_n.33), kind=kLoop, calls=%fused_computation.5 | loop fusion | bytes 1048580 | tf_op jit(solution)/shard_map/dynamic_update_slice | solution.py:173
  71.3 4.3 %collective-permute-done.4 = bf16[128,2048]{1,0:T(8,128)(2,1)S(1)} collective-permute-done((bf16[128,2048]{1,0:T(8,128)(2,1)}, bf16[128,2048]{1,0:T(8,128)(2,1)S(1)}, u32[]{:S(2)}, u32[]{:S(2)}) %collective-permute-start.4) | collective-permute-done | bytes 524320 | tf_op jit(solution)/shard_map/ppermute | solution.py:16
  75.5 0.8 %constant_dynamic-update-slice_fusion = bf16[128,8192]{1,0:T(8,128)(2,1)} fusion(bf16[128,8192]{1,0:T(8,128)(2,1)} %constant_dynamic-update-slice_fusion.1, bf16[128,2048]{1,0:T(8,128)(2,1)S(1)} %collective-permute-done.4, s32[]{:T(128)S(6)} %select_n.34), kind=kLoop, calls=%fused_computation.4 | loop fusion | bytes 1048580 | tf_op jit(solution)/shard_map/dynamic_update_slice | solution.py:173
  (3 shorter events, 0.0 us)
Async XLA Ops:
  1.2 32.6 %copy-start = (bf16[2,256,512]{2,1,0:T(8,128)(2,1)}, bf16[2,256,512]{2,1,0:T(8,128)(2,1)S(1)}, u32[]{:S(2)}) copy-start(bf16[2,256,512]{2,1,0:T(8,128)(2,1)S(1)} %reshape.3.refs_0_) | copy-start | bytes 1572868
  1.3 28.6 %collective-permute-start.1 = (bf16[2,256,512]{2,1,0:T(8,128)(2,1)S(1)}, bf16[2,256,512]{2,1,0:T(8,128)(2,1)S(1)}, u32[]{:S(2)}, u32[]{:S(2)}) collective-permute-start(bf16[2,256,512]{2,1,0:T(8,128)(2,1)S(1)} %reshape.3.refs_0_), channel_id=1, source_target_pairs={{0,6},{2,8},{4,10},{6,12},{8,14},{10,16},{12,18},{14,20},{16,22},{... | collective-permute-start | bytes 1572872 | tf_op jit(solution)/shard_map/ppermute | solution.py:16
  5.9 28.0 %collective-permute-start = (bf16[2,256,512]{2,1,0:T(8,128)(2,1)S(1)}, bf16[2,256,512]{2,1,0:T(8,128)(2,1)S(1)}, u32[]{:S(2)}, u32[]{:S(2)}) collective-permute-start(bf16[2,256,512]{2,1,0:T(8,128)(2,1)S(1)} %reshape.3.refs_0_), channel_id=1, source_target_pairs={{0,2},{2,4},{4,6},{6,8},{8,10},{10,12},{12,14},{14,16},{16,18},{18... | collective-permute-start | bytes 1572872 | tf_op jit(solution)/shard_map/ppermute | solution.py:16
  29.9 3.9 %copy-start.1 = (bf16[2,256,512]{2,1,0:T(8,128)(2,1)}, bf16[2,256,512]{2,1,0:T(8,128)(2,1)S(1)}, u32[]{:S(2)}) copy-start(bf16[2,256,512]{2,1,0:T(8,128)(2,1)S(1)} %collective-permute-done.1.refs_3_) | copy-start | bytes 1572868
  33.8 4.7 %copy-start.2 = (bf16[2,256,512]{2,1,0:T(8,128)(2,1)}, bf16[2,256,512]{2,1,0:T(8,128)(2,1)S(1)}, u32[]{:S(2)}) copy-start(bf16[2,256,512]{2,1,0:T(8,128)(2,1)S(1)} %collective-permute-done.refs_1_) | copy-start | bytes 1572868
  33.9 4.7 %collective-permute-start.2 = (bf16[2,256,512]{2,1,0:T(8,128)(2,1)S(1)}, bf16[2,256,512]{2,1,0:T(8,128)(2,1)S(1)}, u32[]{:S(2)}, u32[]{:S(2)}) collective-permute-start(bf16[2,256,512]{2,1,0:T(8,128)(2,1)S(1)} %broadcast_select_fusion), channel_id=1, source_target_pairs={{0,2},{2,0},{4,6},{6,4},{8,10},{10,8},{12,14},{14,12},{16,18},{18,... | collective-permute-start | bytes 1572872 | tf_op jit(solution)/shard_map/ppermute | solution.py:154
  38.6 0.8 %copy-start.3 = (bf16[2,256,512]{2,1,0:T(8,128)(2,1)}, bf16[2,256,512]{2,1,0:T(8,128)(2,1)S(1)}, u32[]{:S(2)}) copy-start(bf16[2,256,512]{2,1,0:T(8,128)(2,1)S(1)} %collective-permute-done.2.refs_2_) | copy-start | bytes 1572868
  47.7 22.7 %collective-permute-start.3 = (bf16[128,2048]{1,0:T(8,128)(2,1)}, bf16[128,2048]{1,0:T(8,128)(2,1)S(1)}, u32[]{:S(2)}, u32[]{:S(2)}) collective-permute-start(bf16[128,2048]{1,0:T(8,128)(2,1)} %shard_map.38), channel_id=1, source_target_pairs={{0,1},{1,0},{2,3},{3,2},{4,5},{5,4},{6,7},{7,6},{8,9},{9,8},{10,11... | collective-permute-start | bytes 1572872 | tf_op jit(solution)/shard_map/ppermute | solution.py:16
  58.2 17.4 %collective-permute-start.4 = (bf16[128,2048]{1,0:T(8,128)(2,1)}, bf16[128,2048]{1,0:T(8,128)(2,1)S(1)}, u32[]{:S(2)}, u32[]{:S(2)}) collective-permute-start(bf16[128,2048]{1,0:T(8,128)(2,1)} %shard_map.39), channel_id=1, source_target_pairs={{0,1},{1,0},{2,3},{3,2},{4,5},{5,4},{6,7},{7,6},{8,9},{9,8},{10,11... | collective-permute-start | bytes 1572872 | tf_op jit(solution)/shard_map/ppermute | solution.py:16
